TPU v7x, 512 devices: a whole 4x4x16 slice. The times are simulated.
512 devices in a mesh: req: 128 (over z, y, core), wt: 4 (over x).
Axes of the slice: x: 4, y: 4, z: 16, core: 2. Of those that a mesh axis runs over, the one named last changes fastest.
Arguments:
- hidden_in: bfloat16 [32768, 5120], P('req', 'wt'), may hold values from -6 to 6
- queries: bfloat16 [32768, 5120], P('req', 'wt'), as said below
- key_proj: bfloat16 [32768, 5120], P('req', 'wt'), as said below
- values: bfloat16 [32768, 5120], P('req', 'wt'), may hold values from -6 to 6
- query_gain: float32 [5120], P('wt'), may hold values from 0.1 to 1.9
- key_gain: float32 [5120], P('wt'), may hold values from 0.1 to 1.9
- attn_gain: float32 [5120], P('wt'), may hold values from 0.1 to 1.9
- gate_w: bfloat16 [5120, 13824], P('wt', 'req'), may hold values from -0.078125 to 0.078125
- up_w: bfloat16 [5120, 13824], P('wt', 'req'), may hold values from -0.078125 to 0.078125
- lengths: int32 [128], replicated, may hold values from 1 to 256, 4608 in all
- assign: int32 [128], replicated, may hold values from 0 to 127, each once
- page_table: int32 [128, 2], P('req'), may hold values from 0 to 1, each once within a row
Outputs:
- gated: bfloat16 [128, 36, 13824], P(None, 'wt', 'req')
- key_cache: bfloat16 [256, 128, 5120], P('req', None, 'wt')
- value_cache: bfloat16 [256, 128, 5120], P('req', None, 'wt')
Inputs may be any that keep to these rules, and one draw needn't show every extreme that they name: lengths sum to 4608 and at least one request has exactly 256 tokens. `assign`: each device of req serves exactly one request. `page_table`: each row names each of the 2 pages of one device once. `queries`: real-valued entries within -24 to 24. `key_proj`: real-valued entries within -24 to 24.
All inputs are finite; a program needn't handle non-finite values.
Results may differ from a plain program's by a relative error of at most 0.013.
Values may be sent and summed in bfloat16 or wider, within the bound.
No kernel may reach another device: no remote copies, remote signals or barrier semaphores. Data moves between devices by JAX's collectives and lax.ppermute only.
A program may use at most 128 MiB of HBM per device.

v0:
```python
import jax
import jax.numpy as jnp
from jax import lax
from jax.sharding import PartitionSpec as P

D = 5120
HD = 128
PAGE = 128
LIVE = 36


EPS = 1e-06
THETA = 500000.0


def rope_tables(row_count, head_width):
    half_width = head_width // 2
    frequency = THETA ** (-(jnp.arange(half_width, dtype=jnp.float32) * 2.0 / head_width))
    angles = jnp.arange(row_count, dtype=jnp.float32)[:, None] * frequency[None, :]
    return (jnp.cos(angles), jnp.sin(angles))


def rotate(heads_in, cosine, sine_table):
    half_width = heads_in.shape[-1] // 2
    leading = heads_in[..., :half_width]
    trailing = heads_in[..., half_width:]
    cos_b = cosine[:, None, :]
    sin_b = sine_table[:, None, :]
    return jnp.concatenate(
        [leading * cos_b - trailing * sin_b, trailing * cos_b + leading * sin_b], axis=-1
    )


def deal_rows(source, owner_start, owner_len, device, owners, live_rows):
    slot_count = source.shape[0]
    feature_count = source.shape[1]
    per_peer = slot_count // owners
    column = jnp.arange(per_peer, dtype=jnp.int32)[None, :]
    target_dev = jnp.arange(owners, dtype=jnp.int32)[:, None]
    my_start = owner_start[device]
    my_length = owner_len[device]
    local_index = (target_dev - my_start) % owners + owners * column
    usable = local_index < my_length
    picked = jnp.where(
        usable[:, :, None],
        source[jnp.minimum(local_index, slot_count - 1)],
        jnp.zeros((), source.dtype),
    )
    arrived = lax.all_to_all(picked, "req", split_axis=0, concat_axis=0, tiled=True)
    src_start = owner_start[:, None]
    src_length = owner_len[:, None]
    sent_index = (device - src_start) % owners + owners * column
    landing = jnp.where(
        sent_index < src_length, (src_start + sent_index - device) // owners, live_rows
    )
    packed = jnp.zeros((live_rows, feature_count), source.dtype)
    return packed.at[landing.reshape(-1)].set(arrived.reshape(-1, feature_count), mode="drop")


def per_device(
    hidden_in,
    queries,
    key_proj,
    values,
    query_gain,
    key_gain,
    attn_gain,
    gate_w,
    up_w,
    lengths,
    assign,
    page_table,
):
    slot_count = hidden_in.shape[0]
    feature_count = hidden_in.shape[1]
    owners = lax.axis_size("req")
    device = lax.axis_index("req")
    head_count = feature_count // HD
    unit_count = gate_w.shape[1]
    owner_req = jnp.zeros((owners,), jnp.int32).at[assign].set(jnp.arange(owners, dtype=jnp.int32))
    starts = jnp.cumsum(lengths) - lengths
    owner_start = starts[owner_req]
    owner_len = lengths[owner_req]
    my_length = owner_len[device]
    query_f = queries.astype(jnp.float32)
    key_f = key_proj.astype(jnp.float32)
    query_sq, key_sq = lax.psum(
        (jnp.sum(query_f * query_f, axis=1), jnp.sum(key_f * key_f, axis=1)), "wt"
    )
    query_n = query_f * lax.rsqrt(query_sq / D + EPS)[:, None] * query_gain
    key_n = key_f * lax.rsqrt(key_sq / D + EPS)[:, None] * key_gain
    cosine, sine_table = rope_tables(slot_count, HD)
    query_r = rotate(query_n.reshape(slot_count, head_count, HD), cosine, sine_table).astype(
        jnp.bfloat16
    )
    key_r = rotate(key_n.reshape(slot_count, head_count, HD), cosine, sine_table).astype(
        jnp.bfloat16
    )
    scores = jnp.einsum(
        "qhd,khd->hqk", query_r, key_r, preferred_element_type=jnp.float32
    ) * HD ** (-0.5)
    position = jnp.arange(slot_count, dtype=jnp.int32)
    allowed = (position[None, :] <= position[:, None]) & (position[None, :] < my_length)
    scores = jnp.where(allowed[None], scores, -jnp.inf)
    row_peak = jnp.max(scores, axis=2, keepdims=True)
    expd = jnp.exp(scores - row_peak)
    probabilities = (expd / jnp.sum(expd, axis=2, keepdims=True)).astype(jnp.bfloat16)
    value_heads = values.reshape(slot_count, head_count, HD)
    attended = jnp.einsum(
        "hqk,khd->qhd", probabilities, value_heads, preferred_element_type=jnp.float32
    )
    attended = attended.astype(jnp.bfloat16).reshape(slot_count, feature_count)
    attended_f = attended.astype(jnp.float32)
    attn_sq = lax.psum(jnp.sum(attended_f * attended_f, axis=1), "wt")
    layer_rows = (
        hidden_in.astype(jnp.float32)
        + attended_f * lax.rsqrt(attn_sq / D + EPS)[:, None] * attn_gain
    ).astype(jnp.bfloat16)
    live_mask = (position < my_length)[:, None]
    page_count = slot_count // PAGE
    zero_value = jnp.zeros((), jnp.bfloat16)
    key_pages = jnp.where(live_mask, key_r.reshape(slot_count, feature_count), zero_value).reshape(
        page_count, PAGE, feature_count
    )
    value_pages = jnp.where(live_mask, values, zero_value).reshape(page_count, PAGE, feature_count)
    placement = page_table[0]
    key_cache = jnp.zeros_like(key_pages).at[placement].set(key_pages)
    value_cache = jnp.zeros_like(value_pages).at[placement].set(value_pages)
    regrouped = deal_rows(layer_rows, owner_start, owner_len, device, owners, LIVE)
    piece = lax.all_gather(regrouped, "req", axis=0, tiled=True)
    stacked = jnp.stack(
        [
            jnp.dot(piece, gate_w, preferred_element_type=jnp.float32),
            jnp.dot(piece, up_w, preferred_element_type=jnp.float32),
        ]
    )
    stacked = stacked.reshape(2, owners, LIVE, unit_count)
    gate_part, up_part = (
        lax.psum_scatter(stacked[0], "wt", scatter_dimension=1, tiled=True),
        lax.psum_scatter(stacked[1], "wt", scatter_dimension=1, tiled=True),
    )
    gated = (jax.nn.silu(gate_part) * up_part).astype(jnp.bfloat16)
    return (gated, key_cache, value_cache)


def solution(mesh):
    placed = (
        P("req", "wt"),
        P("req", "wt"),
        P("req", "wt"),
        P("req", "wt"),
        P("wt"),
        P("wt"),
        P("wt"),
        P("wt", "req"),
        P("wt", "req"),
        P(),
        P(),
        P("req", None),
    )
    return jax.shard_map(
        per_device,
        mesh=mesh,
        in_specs=placed,
        out_specs=(P(None, "wt", "req"), P("req", None, "wt"), P("req", None, "wt")),
        check_vma=False,
    )
```

profile of v0, /device:TPU:1, one launch (start us, length us, event | category | flops | bytes accessed | tf_op | source)
XLA Modules:
  0.0 378.9 jit_solution(4246838663136592697)
XLA Ops:
  7.2 1.4 copy.56
  9.3 9.3 %all-reduce = (f32[256]{0:T(256)S(1)}, f32[256]{0:T(256)S(1)}) all-reduce(f32[256]{0:T(256)S(1)} %fusion.5, f32[256]{0:T(256)S(1)} %fusion.3), channel_id=1, replica_groups=mesh['req'=128,'wt'=4] {'wt'}, use_global_device_ids=true, to_apply=%region_5.6 | all-reduce | flops 512 | bytes 4096 | tf_op jit(solution)/shard_map/psum | solution.py:87
  19.8 1.5 copy.78
  21.3 1.5 copy.79
  24.5 1.5 copy.76
  26.0 2.6 copy.77
  29.7 1.2 gather_fusion.1
  33.2 1.9 multiply_subtract_fusion
  36.5 1.5 subtract_convert_fusion
  38.0 4.1 %fusion.38 = (f32[10,256]{1,0:T(8,128)S(1)}, f32[10,256,256]{1,2,0:T(8,128)}) fusion(pred[256,256]{0,1:T(8,128)(4,1)S(1)} %fusion.14, bf16[256,10,128]{2,0,1:T(8,128)(2,1)S(1)} %maximum_convert_fusion, bf16[256,10,64]{2,0,1:T(8,128)(2,1)} %get-tuple-element.9, bf16[256,10,64]{2,0,1:T(8,128)(2,1)} %get-tuple-element.8), kind=kOutput, calls=%fused_computation.86 | convolution fusion | flops 171704576 | bytes 4007936 | tf_op jit(solution)/shard_map/sub | solution.py:106
  42.0 3.2 multiply_reduce_fusion
  45.2 1.7 copy.64
  47.0 6.0 %psum.23 = f32[256]{0:T(256)S(1)} all-reduce(f32[256]{0:T(256)S(1)} %get-tuple-element.22), channel_id=1, replica_groups=mesh['req'=128,'wt'=4] {'wt'}, use_global_device_ids=true, to_apply=%region_9.10 | all-reduce | flops 256 | bytes 2048 | tf_op jit(solution)/shard_map/psum | solution.py:114
  53.4 1.2 gather_fusion
  56.1 1.4 add_convert_fusion
  57.5 1.3 gather_fusion.2
  59.8 1.5 broadcast_select_fusion
  61.3 23.5 %all-to-all-start = ((bf16[128,2,1280]{2,1,0:T(2,128)(2,1)}), bf16[128,2,1280]{2,1,0:T(2,128)(2,1)S(1)}, u32[]{:S(2)}, u32[]{:S(2)}) async-start(bf16[128,2,1280]{2,1,0:T(2,128)(2,1)} %broadcast_select_fusion), calls=%async_computation | async-start | bytes 1310720 | tf_op jit(solution)/shard_map/all_to_all | solution.py:49
  85.5 35.7 %all-to-all-done = bf16[128,2,1280]{2,1,0:T(2,128)(2,1)S(1)} async-done(((bf16[128,2,1280]{2,1,0:T(2,128)(2,1)}), bf16[128,2,1280]{2,1,0:T(2,128)(2,1)S(1)}, u32[]{:S(2)}, u32[]{:S(2)}) %all-to-all-start) | async-done | bytes 655392 | tf_op jit(solution)/shard_map/all_to_all | solution.py:49
  121.5 2.2 scatter_custom_fusion.1
  123.8 146.6 %all-gather.3.cloned.1.call-done = bf16[128,36,1280]{2,1,0:T(8,128)(2,1)} async-done(((bf16[1,36,1280]{2,1,0:T(8,128)(2,1)}), bf16[128,36,1280]{2,1,0:T(8,128)(2,1)}) %all-gather.3.cloned.1.call-update) | async-done | bytes 11796496 | tf_op jit(solution)/shard_map/all_gather | solution.py:130
  270.4 16.9 %reshape.488 = bf16[4608,1280]{1,0:T(8,128)(2,1)} reshape(bf16[128,36,1280]{2,1,0:T(8,128)(2,1)} %all-gather.3.cloned.1.call-done) | data formatting | bytes 23592960
  287.3 6.1 %fusion.41 = f32[4608,108]{1,0:T(8,128)S(1)} fusion(bf16[4608,1280]{1,0:T(8,128)(2,1)} %reshape.488, bf16[1280,108]{0,1:T(8,128)(2,1)S(1)} %copy-done), kind=kOutput, calls=%fused_computation.87 | convolution fusion | flops 1274019840 | bytes 14063616 | tf_op jit(solution)/shard_map/dot_general | solution.py:133
  293.4 1.6 squeeze.18
  295.0 3.3 copy.66
  299.3 6.1 %fusion.42 = f32[4608,108]{1,0:T(8,128)S(1)} fusion(bf16[4608,1280]{1,0:T(8,128)(2,1)} %reshape.488, bf16[1280,108]{0,1:T(8,128)(2,1)S(1)} %copy-done.11), kind=kOutput, calls=%fused_computation.88 | convolution fusion | flops 1274019840 | bytes 14063616 | tf_op jit(solution)/shard_map/dot_general | solution.py:134
  305.4 1.6 squeeze.19
  307.0 3.3 copy.68
  313.9 2.5 scatter_fusion
  317.3 13.0 %reduce-scatter.3.cloned.1.call-done = f32[128,9,108]{0,2,1:T(8,128)} async-done(((f32[128,36,108]{0,2,1:T(8,128)}), f32[128,9,108]{0,2,1:T(8,128)}) %reduce-scatter.3.cloned.1.call-update) | async-done | bytes 497680 | tf_op jit(solution)/shard_map/reduce_scatter | solution.py:139
  330.3 40.0 %reduce-scatter.5.cloned.1.call-done = f32[128,9,108]{0,2,1:T(8,128)} async-done(((f32[128,36,108]{0,2,1:T(8,128)}), f32[128,9,108]{0,2,1:T(8,128)}) %reduce-scatter.5.cloned.1.call-update) | async-done | bytes 497680 | tf_op jit(solution)/shard_map/reduce_scatter | solution.py:140
  370.3 2.0 multiply_convert_fusion
  (90 shorter events, 17.5 us)
Async XLA Ops:
  7.2 280.1 %copy-start = (bf16[1280,108]{0,1:T(8,128)(2,1)S(1)}, bf16[1280,108]{0,1:T(8,128)(2,1)}, u32[]{:S(2)}) copy-start(bf16[1280,108]{0,1:T(8,128)(2,1)} %param.19) | copy-start | bytes 829444
  7.2 1.7 copy-start.9
  8.6 10.0 %copy-start.12 = (f32[1280]{0:T(1024)S(1)}, f32[1280]{0:T(1024)}, u32[]{:S(2)}) copy-start(f32[1280]{0:T(1024)} %param.17) | copy-start | bytes 15364
  21.3 2.0 copy-start.13
  26.0 2.7 copy-start.15
  26.0 3.7 copy-start.2
  26.0 6.2 %copy-start.5 = (bf16[256,1280]{1,0:T(8,128)(2,1)S(1)}, bf16[256,1280]{1,0:T(8,128)(2,1)}, u32[]{:S(2)}) copy-start(bf16[256,1280]{1,0:T(8,128)(2,1)} %param.15) | copy-start | bytes 1966084
  33.2 2.3 copy-start.4
  35.2 1.3 copy-start.3
  36.5 1.5 copy-start.7
  38.0 4.1 %copy-start.10 = (bf16[256,1280]{0,1:T(8,128)(2,1)S(1)}, bf16[256,1280]{0,1:T(8,128)(2,1)}, u32[]{:S(2)}) copy-start(bf16[256,1280]{0,1:T(8,128)(2,1)} %copy.62) | copy-start | bytes 1966084
  45.2 10.9 %copy-start.14 = (f32[1280]{0:T(1024)S(1)}, f32[1280]{0:T(1024)}, u32[]{:S(2)}) copy-start(f32[1280]{0:T(1024)} %param.18) | copy-start | bytes 15364
  61.3 59.9 %all-to-all-start = ((bf16[128,2,1280]{2,1,0:T(2,128)(2,1)}), bf16[128,2,1280]{2,1,0:T(2,128)(2,1)S(1)}, u32[]{:S(2)}, u32[]{:S(2)}) async-start(bf16[128,2,1280]{2,1,0:T(2,128)(2,1)} %broadcast_select_fusion), calls=%async_computation | async-start | bytes 1310720 | tf_op jit(solution)/shard_map/all_to_all | solution.py:49
  84.8 185.6 %all-gather.3.cloned.1.call-start = ((), (), s32[]{:S(2)}) async-start(), calls=%async_computation.5 | async-start | bytes 13209600 | tf_op jit(solution)/shard_map/all_gather | solution.py:130
  123.7 206.6 %reduce-scatter.3.cloned.1.call-start = ((), (), s32[]{:S(2)}) async-start(), calls=%async_computation.3 | async-start | bytes 2580480 | tf_op jit(solution)/shard_map/reduce_scatter | solution.py:139
  298.3 1.0 copy-start.11
  298.3 72.0 %reduce-scatter.5.cloned.1.call-start = ((), (), s32[]{:S(2)}) async-start(), calls=%async_computation.4 | async-start | bytes 2580480 | tf_op jit(solution)/shard_map/reduce_scatter | solution.py:140
  310.3 1.1 copy-start.8
  311.4 1.4 copy-start.16
  316.5 55.8 %copy-start.1 = (bf16[1280,108]{0,1:T(8,128)(2,1)S(1)}, bf16[1280,108]{0,1:T(8,128)(2,1)}, u32[]{:S(2)}) copy-start(bf16[1280,108]{0,1:T(8,128)(2,1)} %param.19) | copy-start | bytes 829444
  317.3 55.0 %copy-start.6 = (bf16[2,128,1280]{2,1,0:T(8,128)(2,1)}, bf16[2,128,1280]{2,1,0:T(8,128)(2,1)S(1)}, u32[]{:S(2)}) copy-start(bf16[2,128,1280]{2,1,0:T(8,128)(2,1)S(1)} %scatter_fusion.1) | copy-start | bytes 1966084
Sparse Core Ops, SparseCore 0:
  123.9 146.5 all-gather.2
  298.5 31.7 reduce-scatter.2
  333.4 36.8 reduce-scatter.4
where the time goes:
time: 380 us; the launch traced here: 379 us
  waiting for transfers between devices  235 us (62%)
  local copies, waits for them, and re-layouts  57.6 us (15%)
  starting transfers between devices  23.6 us (6%)
  matrix products  19.5 us (5%)
  blocking collectives  15.3 us (4%)
  between operations  14.1 us (4%)
  other arithmetic  13.3 us (4%)
    all_gather x1, waiting for transfers between devices, per_device(): piece = lax.all_gather(regrouped, 'req', axis=0, tiled=True)  147 us
    reduce_scatter x1, waiting for transfers between devices, per_device(): lax.psum_scatter(stacked[1], 'wt', scatter_dimension=1, tiled=True)  40 us
    all_to_all x1, waiting for transfers between devices, deal_rows(): lax.all_to_all(picked, 'req', split_axis=0, concat_axis=0, tiled=True)  35.7 us
    unnamed x42, local copies, waits for them, and re-layouts  29.6 us
    all_to_all x1, starting transfers between devices, deal_rows(): lax.all_to_all(picked, 'req', split_axis=0, concat_axis=0, tiled=True)  23.5 us
    reduce_scatter x1, waiting for transfers between devices, per_device(): lax.psum_scatter(stacked[0], 'wt', scatter_dimension=1, tiled=True)  13 us
    psum x1, blocking collectives, per_device(): lax.psum((jnp.sum(query_f * query_f, axis=1), jnp.sum(key_f * key_f, axis...  9.29 us
  transfers between devices with their start and end apart: 4, of which 4 were waited for; matrix products, arithmetic and copies ran while one was open for 5% of the time, Pallas kernels for 0%

commit v1 on v0

--- a/solution.py
+++ b/solution.py
@@ -1,7 +1,7 @@
 import jax
 import jax.numpy as jnp
 from jax import lax
-from jax.sharding import PartitionSpec as P
+from jax.sharding import Mesh, PartitionSpec as P
 
 D = 5120
 HD = 128
@@ -46,7 +46,7 @@
         source[jnp.minimum(local_index, slot_count - 1)],
         jnp.zeros((), source.dtype),
     )
-    arrived = lax.all_to_all(picked, "req", split_axis=0, concat_axis=0, tiled=True)
+    arrived = lax.all_to_all(picked, ("ra", "rb"), split_axis=0, concat_axis=0, tiled=True)
     src_start = owner_start[:, None]
     src_length = owner_len[:, None]
     sent_index = (device - src_start) % owners + owners * column
@@ -73,8 +73,8 @@
 ):
     slot_count = hidden_in.shape[0]
     feature_count = hidden_in.shape[1]
-    owners = lax.axis_size("req")
-    device = lax.axis_index("req")
+    owners = lax.axis_size(("ra", "rb"))
+    device = lax.axis_index("ra") * lax.axis_size("rb") + lax.axis_index("rb")
     head_count = feature_count // HD
     unit_count = gate_w.shape[1]
     owner_req = jnp.zeros((owners,), jnp.int32).at[assign].set(jnp.arange(owners, dtype=jnp.int32))
@@ -127,41 +127,44 @@
     key_cache = jnp.zeros_like(key_pages).at[placement].set(key_pages)
     value_cache = jnp.zeros_like(value_pages).at[placement].set(value_pages)
     regrouped = deal_rows(layer_rows, owner_start, owner_len, device, owners, LIVE)
-    piece = lax.all_gather(regrouped, "req", axis=0, tiled=True)
-    stacked = jnp.stack(
-        [
-            jnp.dot(piece, gate_w, preferred_element_type=jnp.float32),
-            jnp.dot(piece, up_w, preferred_element_type=jnp.float32),
-        ]
-    )
-    stacked = stacked.reshape(2, owners, LIVE, unit_count)
-    gate_part, up_part = (
-        lax.psum_scatter(stacked[0], "wt", scatter_dimension=1, tiled=True),
-        lax.psum_scatter(stacked[1], "wt", scatter_dimension=1, tiled=True),
-    )
-    gated = (jax.nn.silu(gate_part) * up_part).astype(jnp.bfloat16)
+    outer = lax.axis_size("ra")
+    inner = lax.axis_size("rb")
+    piece = lax.all_gather(regrouped, "ra", axis=0, tiled=True)
+    weights = lax.all_gather(jnp.stack([gate_w, up_w]), "rb", axis=2, tiled=True)
+    stacked = jnp.einsum("tk,skn->tsn", piece, weights, preferred_element_type=jnp.float32)
+    stacked = stacked.reshape(outer, LIVE, 2, inner * unit_count)
+    summed = lax.psum_scatter(stacked, "wt", scatter_dimension=1, tiled=True)
+    gated = (jax.nn.silu(summed[:, :, 0]) * summed[:, :, 1]).astype(jnp.bfloat16)
+    rows_here = gated.shape[1]
+    gated = gated.reshape(outer, rows_here, inner, unit_count)
+    gated = lax.all_to_all(gated, "rb", split_axis=2, concat_axis=2, tiled=True)
+    gated = jnp.transpose(gated, (0, 2, 1, 3)).reshape(outer * inner, rows_here, unit_count)
     return (gated, key_cache, value_cache)
 
 
 def solution(mesh):
+    inner = 4
+    outer = mesh.shape["req"] // inner
+    split = Mesh(mesh.devices.reshape(outer, inner, mesh.shape["wt"]), ("ra", "rb", "wt"))
+    req = ("ra", "rb")
     placed = (
-        P("req", "wt"),
-        P("req", "wt"),
-        P("req", "wt"),
-        P("req", "wt"),
+        P(req, "wt"),
+        P(req, "wt"),
+        P(req, "wt"),
+        P(req, "wt"),
         P("wt"),
         P("wt"),
         P("wt"),
-        P("wt", "req"),
-        P("wt", "req"),
+        P("wt", req),
+        P("wt", req),
         P(),
         P(),
-        P("req", None),
+        P(req, None),
     )
     return jax.shard_map(
         per_device,
-        mesh=mesh,
+        mesh=split,
         in_specs=placed,
-        out_specs=(P(None, "wt", "req"), P("req", None, "wt"), P("req", None, "wt")),
+        out_specs=(P(None, "wt", req), P(req, None, "wt"), P(req, None, "wt")),
         check_vma=False,
     )

time: 380 us -> 411 us (1.082)
  waiting for transfers between devices: 235 us -> 278 us
  matrix products: 19.5 us -> 11.4 us
  local copies, waits for them, and re-layouts: 57.6 us -> 50.9 us
  starting transfers between devices: 23.6 us -> 27.8 us
    all_gather x1 -> x2, waiting for transfers between devices: 147 us -> 182 us  [the longest x1 141 us: per_device(): piece = lax.all_gather(regrouped, 'ra', axis=0, tiled=True)]
    unnamed x42 -> x55, local copies, waits for them, and re-layouts: 29.6 us -> 16.3 us
    squeeze x4 -> x2, local copies, waits for them, and re-layouts: 9.86 us -> 0.78 us  [the longest x1 0.39 us: per_device(): summed[:, :, 0]]
    dot_general x0 -> x1, local copies, waits for them, and re-layouts: none -> 7.91 us  [per_device(): jnp.einsum('tk,skn->tsn', piece, weights, preferred_element_type=jnp.floa...]
    reshape x0 -> x1, local copies, waits for them, and re-layouts: none -> 7.21 us  [per_device(): stacked = stacked.reshape(outer, LIVE, 2, inner * unit_count)]
    dot_general x2 -> x1, matrix products: 12.2 us -> 6.56 us  [per_device(): jnp.einsum('tk,skn->tsn', piece, weights, preferred_element_type=jnp.floa...]
    all_to_all x1 -> x2, starting transfers between devices: 23.5 us -> 27.7 us  [the longest x1 23.6 us: deal_rows(): lax.all_to_all(picked, ('ra', 'rb'), split_axis=0, concat_axis=0, tiled=T...]
    all_to_all x1 -> x2, waiting for transfers between devices: 35.7 us -> 39.6 us  [the longest x1 35.7 us: deal_rows(): lax.all_to_all(picked, ('ra', 'rb'), split_axis=0, concat_axis=0, tiled=T...]
  transfers between devices with their start and end apart: 4 -> 5, of which waited for: 4 -> 5; matrix products, arithmetic and copies ran while one was open for 5% -> 2% of each run, Pallas kernels for 0% -> 0%
where the time goes in v1:
time: 411 us; the launch traced here: 410 us
  waiting for transfers between devices  278 us (68%)
  local copies, waits for them, and re-layouts  50.9 us (12%)
  starting transfers between devices  27.8 us (7%)
  blocking collectives  15.3 us (4%)
  between operations  14.2 us (3%)
  other arithmetic  12.1 us (3%)
  matrix products  11.4 us (3%)
    all_gather x1, waiting for transfers between devices, per_device(): piece = lax.all_gather(regrouped, 'ra', axis=0, tiled=True)  141 us
    reduce_scatter x1, waiting for transfers between devices, per_device(): summed = lax.psum_scatter(stacked, 'wt', scatter_dimension=1, tiled=True)  56.7 us
    all_gather x1, waiting for transfers between devices, per_device(): lax.all_gather(jnp.stack([gate_w, up_w]), 'rb', axis=2, tiled=True)  41 us
    all_to_all x1, waiting for transfers between devices, deal_rows(): lax.all_to_all(picked, ('ra', 'rb'), split_axis=0, concat_axis=0, tiled=T...  35.7 us
    all_to_all x1, starting transfers between devices, deal_rows(): lax.all_to_all(picked, ('ra', 'rb'), split_axis=0, concat_axis=0, tiled=T...  23.6 us
    unnamed x55, local copies, waits for them, and re-layouts  16.3 us
    psum x1, blocking collectives, per_device(): lax.psum((jnp.sum(query_f * query_f, axis=1), jnp.sum(key_f * key_f, axis...  9.29 us
  transfers between devices with their start and end apart: 5, of which 5 were waited for; matrix products, arithmetic and copies ran while one was open for 2% of the time, Pallas kernels for 0%

profile of v1, /device:TPU:1, one launch (start us, length us, event | category | flops | bytes accessed | tf_op | source)
XLA Modules:
  0.0 409.6 jit_solution(2444078418245778688)
XLA Ops:
  7.7 1.3 copy.84
  9.7 9.3 %all-reduce = (f32[256]{0:T(256)S(1)}, f32[256]{0:T(256)S(1)}) all-reduce(f32[256]{0:T(256)S(1)} %fusion.7, f32[256]{0:T(256)S(1)} %fusion.5), channel_id=1, replica_groups=mesh['ra'=32,'rb'=4,'wt'=4] {'wt'}, use_global_device_ids=true, to_apply=%region_5.6 | all-reduce | flops 512 | bytes 4096 | tf_op jit(solution)/shard_map/psum | solution.py:87
  19.8 0.9 fusion.40
  21.2 1.5 copy.110
  23.2 1.2 compare_select_fusion.4
  24.9 1.1 scatter_custom_fusion
  26.1 1.7 gather_fusion.1
  27.8 1.2 dynamic_slice.8
  32.2 1.5 copy.107
  33.7 2.6 copy.108
  36.3 1.1 copy.90
  40.1 2.7 fusion.42
  42.8 2.1 multiply_reduce_fusion
  45.4 6.0 %psum.23 = f32[256]{0:T(256)S(1)} all-reduce(f32[256]{0:T(256)S(1)} %get-tuple-element.33), channel_id=1, replica_groups=mesh['ra'=32,'rb'=4,'wt'=4] {'wt'}, use_global_device_ids=true, to_apply=%region_9.10 | all-reduce | flops 256 | bytes 2048 | tf_op jit(solution)/shard_map/psum | solution.py:114
  51.8 1.2 gather_fusion
  54.8 1.3 gather_fusion.2
  57.5 1.5 broadcast_select_fusion
  59.0 23.6 %all-to-all-start = ((bf16[128,2,1280]{2,1,0:T(2,128)(2,1)}), bf16[128,2,1280]{2,1,0:T(2,128)(2,1)S(1)}, u32[]{:S(2)}, u32[]{:S(2)}) async-start(bf16[128,2,1280]{2,1,0:T(2,128)(2,1)} %broadcast_select_fusion), calls=%async_computation | async-start | bytes 1310720 | tf_op jit(solution)/shard_map/all_to_all | solution.py:49
  83.3 35.7 %all-to-all-done = bf16[128,2,1280]{2,1,0:T(2,128)(2,1)S(1)} async-done(((bf16[128,2,1280]{2,1,0:T(2,128)(2,1)}), bf16[128,2,1280]{2,1,0:T(2,128)(2,1)S(1)}, u32[]{:S(2)}, u32[]{:S(2)}) %all-to-all-start) | async-done | bytes 655392 | tf_op jit(solution)/shard_map/all_to_all | solution.py:49
  119.3 2.2 scatter_custom_fusion.1
  121.7 1.2 copy.93
  123.0 140.6 %all-gather.6.cloned.1.call-done = bf16[32,36,1280]{2,1,0:T(8,128)(2,1)} async-done(((bf16[1,36,1280]{2,1,0:T(8,128)(2,1)}), bf16[32,36,1280]{2,1,0:T(8,128)(2,1)}) %all-gather.6.cloned.1.call-update) | async-done | bytes 2949136 | tf_op jit(solution)/shard_map/all_gather | solution.py:132
  263.5 3.7 reshape.493
  267.2 41.0 %all-gather.4.cloned.1.call-done = bf16[2,1280,432]{1,0,2:T(2,128)(2,1)} async-done(((bf16[2,1280,108]{1,0,2:T(2,128)(2,1)}), bf16[2,1280,432]{1,0,2:T(2,128)(2,1)}) %all-gather.4.cloned.1.call-update) | async-done | bytes 2211856 | tf_op jit(solution)/shard_map/all_gather | solution.py:133
  308.2 6.6 %fusion.1 = f32[1152,2,432]{0,2,1:T(8,128)} fusion(bf16[1152,1280,1]{1,0,2:T(8,128)(2,1)S(1)} %reshape.493, bf16[2,1280,432]{1,0,2:T(2,128)(2,1)} %all-gather.4.cloned.1.call-done), kind=kOutput, calls=%fused_computation.11 | convolution fusion | flops 2548039680 | bytes 9142272 | tf_op jit(solution)/shard_map/tk,skn->tsn/dot_general | solution.py:134
  314.8 7.9 %copy.95 = f32[1152,2,432]{2,1,0:T(2,128)} copy(f32[1152,2,432]{0,2,1:T(8,128)} %fusion.1) | data formatting | bytes 7962624 | tf_op jit(solution)/shard_map/tk,skn->tsn/dot_general | solution.py:134
  322.7 7.2 %copy.96 = f32[32,36,2,432]{3,0,2,1:T(8,128)} copy(f32[32,36,2,432]{3,2,1,0:T(2,128)} %bitcast.35) | data formatting | bytes 7962624 | tf_op jit(solution)/shard_map/reshape | solution.py:135
  329.9 1.1 copy-done.8
  332.7 56.7 %reduce-scatter.2.cloned.1.call-done = f32[32,9,2,432]{3,0,2,1:T(8,128)} async-done(((f32[32,36,2,432]{3,0,2,1:T(8,128)}), f32[32,9,2,432]{3,0,2,1:T(8,128)}) %reduce-scatter.2.cloned.1.call-update) | async-done | bytes 995344 | tf_op jit(solution)/shard_map/reduce_scatter | solution.py:136
  389.4 1.4 fusion.41
  392.4 4.1 all-to-all-start.1
  398.1 3.9 all-to-all-done.1
  (108 shorter events, 20.3 us)
Async XLA Ops:
  7.2 2.1 copy-start.9
  9.1 10.5 %copy-start.15 = (f32[1280]{0:T(1024)S(1)}, f32[1280]{0:T(1024)}, u32[]{:S(2)}) copy-start(f32[1280]{0:T(1024)} %param.17) | copy-start | bytes 15364
  21.2 4.9 %copy-start = (s32[128]{0:T(128)S(1)}, s32[128]{0:T(128)}, u32[]{:S(2)}) copy-start(s32[128]{0:T(128)} %param.21) | copy-start | bytes 1540
  21.2 9.1 %copy-start.16 = (f32[1280]{0:T(1024)S(1)}, f32[1280]{0:T(1024)}, u32[]{:S(2)}) copy-start(f32[1280]{0:T(1024)} %param.16) | copy-start | bytes 15364
  29.5 0.7 copy-start.19
  33.7 2.6 copy-start.3
  37.4 1.3 copy-start.2
  37.7 1.4 copy-start.1
  39.2 0.8 copy-start.7
  39.2 0.9 copy-start.14
  40.1 2.7 copy-start.10
  44.9 9.4 %copy-start.18 = (s32[2]{0:T(128)S(1)}, s32[2]{0:T(128)}, u32[]{:S(2)}) copy-start(s32[2]{0:T(128)} %iota_multiply_fusion.1) | copy-start | bytes 28
  44.9 9.6 %copy-start.11 = (bf16[256,1280]{1,0:T(8,128)(2,1)S(1)}, bf16[256,1280]{1,0:T(8,128)(2,1)}, u32[]{:S(2)}) copy-start(bf16[256,1280]{1,0:T(8,128)(2,1)} %param.12) | copy-start | bytes 1966084
  45.0 9.6 %copy-start.17 = (f32[1280]{0:T(1024)S(1)}, f32[1280]{0:T(1024)}, u32[]{:S(2)}) copy-start(f32[1280]{0:T(1024)} %param.18) | copy-start | bytes 15364
  56.1 0.6 copy-start.21
  59.0 62.6 %copy-start.12 = (bf16[1280,108]{0,1:T(8,128)(2,1)S(1)}, bf16[1280,108]{0,1:T(8,128)(2,1)}, u32[]{:S(2)}) copy-start(bf16[1280,108]{0,1:T(8,128)(2,1)} %param.20) | copy-start | bytes 829444
  59.0 62.6 %copy-start.13 = (bf16[1280,108]{0,1:T(8,128)(2,1)S(1)}, bf16[1280,108]{0,1:T(8,128)(2,1)}, u32[]{:S(2)}) copy-start(bf16[1280,108]{0,1:T(8,128)(2,1)} %param.19) | copy-start | bytes 829444
  59.0 60.1 %all-to-all-start = ((bf16[128,2,1280]{2,1,0:T(2,128)(2,1)}), bf16[128,2,1280]{2,1,0:T(2,128)(2,1)S(1)}, u32[]{:S(2)}, u32[]{:S(2)}) async-start(bf16[128,2,1280]{2,1,0:T(2,128)(2,1)} %broadcast_select_fusion), calls=%async_computation | async-start | bytes 1310720 | tf_op jit(solution)/shard_map/all_to_all | solution.py:49
  82.6 180.9 %all-gather.6.cloned.1.call-start = ((), (), s32[]{:S(2)}) async-start(), calls=%async_computation.5 | async-start | bytes 3379200 | tf_op jit(solution)/shard_map/all_gather | solution.py:132
  121.5 186.7 %all-gather.4.cloned.1.call-start = ((), (), s32[]{:S(2)}) async-start(), calls=%async_computation.3 | async-start | bytes 2764800 | tf_op jit(solution)/shard_map/all_gather | solution.py:133
  122.9 266.5 %reduce-scatter.2.cloned.1.call-start = ((), (), s32[]{:S(2)}) async-start(), calls=%async_computation.4 | async-start | bytes 5898240 | tf_op jit(solution)/shard_map/reduce_scatter | solution.py:136
  329.9 1.1 copy-start.8
  331.0 1.4 copy-start.4
  331.0 1.5 copy-start.20
  391.5 5.0 %copy-start.22 = (s32[1,2]{1,0:T(1,128)S(1)}, s32[1,2]{1,0:T(1,128)}, u32[]{:S(2)}) copy-start(s32[1,2]{1,0:T(1,128)} %param.23) | copy-start | bytes 28
  392.4 9.6 %all-to-all-start.1 = ((bf16[32,9,4,108]{3,0,1,2:T(8,128)(2,1)}), bf16[32,9,4,108]{3,0,1,2:T(8,128)(2,1)S(1)}, u32[]{:S(2)}, u32[]{:S(2)}) async-start(bf16[32,9,4,108]{3,0,1,2:T(8,128)(2,1)} %fusion.16), calls=%async_computation.2 | async-start | bytes 589824 | tf_op jit(solution)/shard_map/all_to_all | solution.py:140
  397.3 0.8 copy-start.6
  398.1 5.0 %copy-start.5 = (bf16[2,128,1280]{2,1,0:T(8,128)(2,1)}, bf16[2,128,1280]{2,1,0:T(8,128)(2,1)S(1)}, u32[]{:S(2)}) copy-start(bf16[2,128,1280]{2,1,0:T(8,128)(2,1)S(1)} %scatter_fusion.1) | copy-start | bytes 1966084
Sparse Core Ops, SparseCore 0:
  121.7 141.8 all-gather.5
  266.2 41.9 all-gather.3
  330.0 59.3 reduce-scatter.1

commit v2 on v1

--- a/solution.py
+++ b/solution.py
@@ -82,6 +82,7 @@
     owner_start = starts[owner_req]
     owner_len = lengths[owner_req]
     my_length = owner_len[device]
+    weights = lax.all_gather(jnp.stack([gate_w, up_w]), "ra", axis=2, tiled=True)
     query_f = queries.astype(jnp.float32)
     key_f = key_proj.astype(jnp.float32)
     query_sq, key_sq = lax.psum(
@@ -110,6 +111,7 @@
         "hqk,khd->qhd", probabilities, value_heads, preferred_element_type=jnp.float32
     )
     attended = attended.astype(jnp.bfloat16).reshape(slot_count, feature_count)
+    attended, weights = lax.optimization_barrier((attended, weights))
     attended_f = attended.astype(jnp.float32)
     attn_sq = lax.psum(jnp.sum(attended_f * attended_f, axis=1), "wt")
     layer_rows = (
@@ -129,22 +131,21 @@
     regrouped = deal_rows(layer_rows, owner_start, owner_len, device, owners, LIVE)
     outer = lax.axis_size("ra")
     inner = lax.axis_size("rb")
-    piece = lax.all_gather(regrouped, "ra", axis=0, tiled=True)
-    weights = lax.all_gather(jnp.stack([gate_w, up_w]), "rb", axis=2, tiled=True)
+    piece = lax.all_gather(regrouped, "rb", axis=0, tiled=True)
     stacked = jnp.einsum("tk,skn->tsn", piece, weights, preferred_element_type=jnp.float32)
-    stacked = stacked.reshape(outer, LIVE, 2, inner * unit_count)
+    stacked = stacked.reshape(inner, LIVE, 2, outer * unit_count)
     summed = lax.psum_scatter(stacked, "wt", scatter_dimension=1, tiled=True)
     gated = (jax.nn.silu(summed[:, :, 0]) * summed[:, :, 1]).astype(jnp.bfloat16)
     rows_here = gated.shape[1]
-    gated = gated.reshape(outer, rows_here, inner, unit_count)
-    gated = lax.all_to_all(gated, "rb", split_axis=2, concat_axis=2, tiled=True)
-    gated = jnp.transpose(gated, (0, 2, 1, 3)).reshape(outer * inner, rows_here, unit_count)
+    gated = gated.reshape(inner, rows_here, outer, unit_count)
+    gated = lax.all_to_all(gated, "ra", split_axis=2, concat_axis=2, tiled=True)
+    gated = jnp.transpose(gated, (2, 0, 1, 3)).reshape(outer * inner, rows_here, unit_count)
     return (gated, key_cache, value_cache)
 
 
 def solution(mesh):
-    inner = 4
-    outer = mesh.shape["req"] // inner
+    outer = 4
+    inner = mesh.shape["req"] // outer
     split = Mesh(mesh.devices.reshape(outer, inner, mesh.shape["wt"]), ("ra", "rb", "wt"))
     req = ("ra", "rb")
     placed = (

time: 411 us -> 363 us (0.88)
  waiting for transfers between devices: 278 us -> 234 us
    all_gather x2, waiting for transfers between devices: 182 us -> 128 us  [the longest x1 68.6 us: per_device(): lax.all_gather(jnp.stack([gate_w, up_w]), 'ra', axis=2, tiled=True)]
    all_to_all x1, waiting for transfers between devices: 3.89 us -> 15.1 us  [per_device(): gated = lax.all_to_all(gated, 'ra', split_axis=2, concat_axis=2, tiled=True)]
    all_to_all x1, starting transfers between devices: 23.6 us -> 14.4 us  [deal_rows(): lax.all_to_all(picked, ('ra', 'rb'), split_axis=0, concat_axis=0, tiled=T...]
    all_to_all x1, starting transfers between devices: 4.06 us -> 12 us  [per_device(): gated = lax.all_to_all(gated, 'ra', split_axis=2, concat_axis=2, tiled=True)]
    unnamed x55 -> x45, local copies, waits for them, and re-layouts: 16.3 us -> 15.1 us
  transfers between devices with their start and end apart: 5 -> 5, of which waited for: 5 -> 5; matrix products, arithmetic and copies ran while one was open for 2% -> 8% of each run, Pallas kernels for 0% -> 0%
where the time goes in v2:
time: 363 us; the launch traced here: 361 us
  waiting for transfers between devices  234 us (64%)
  local copies, waits for them, and re-layouts  47.6 us (13%)
  starting transfers between devices  26.6 us (7%)
  blocking collectives  17.3 us (5%)
  between operations  14.2 us (4%)
  matrix products  11.4 us (3%)
  other arithmetic  10 us (3%)
    all_gather x1, waiting for transfers between devices, per_device(): lax.all_gather(jnp.stack([gate_w, up_w]), 'ra', axis=2, tiled=True)  68.6 us
    all_gather x1, waiting for transfers between devices, per_device(): piece = lax.all_gather(regrouped, 'rb', axis=0, tiled=True)  59 us
    reduce_scatter x1, waiting for transfers between devices, per_device(): summed = lax.psum_scatter(stacked, 'wt', scatter_dimension=1, tiled=True)  55.1 us
    all_to_all x1, waiting for transfers between devices, deal_rows(): lax.all_to_all(picked, ('ra', 'rb'), split_axis=0, concat_axis=0, tiled=T...  35.7 us
    all_to_all x1, waiting for transfers between devices, per_device(): gated = lax.all_to_all(gated, 'ra', split_axis=2, concat_axis=2, tiled=True)  15.1 us
    unnamed x45, local copies, waits for them, and re-layouts  15.1 us
    all_to_all x1, starting transfers between devices, deal_rows(): lax.all_to_all(picked, ('ra', 'rb'), split_axis=0, concat_axis=0, tiled=T...  14.4 us
    all_to_all x1, starting transfers between devices, per_device(): gated = lax.all_to_all(gated, 'ra', split_axis=2, concat_axis=2, tiled=True)  12 us
  transfers between devices with their start and end apart: 5, of which 5 were waited for; matrix products, arithmetic and copies ran while one was open for 8% of the time, Pallas kernels for 0%

profile of v2, /device:TPU:1, one launch (start us, length us, event | category | flops | bytes accessed | tf_op | source)
XLA Modules:
  0.0 360.7 jit_solution(15634709577130811022)
XLA Ops:
  7.2 1.2 pad_maximum_fusion
  8.4 1.2 copy.92
  11.2 9.3 %all-reduce = (f32[256]{0:T(256)S(1)}, f32[256]{0:T(256)S(1)}) all-reduce(f32[256]{0:T(256)S(1)} %fusion.6, f32[256]{0:T(256)S(1)} %fusion.4), channel_id=1, replica_groups=mesh['ra'=4,'rb'=32,'wt'=4] {'wt'}, use_global_device_ids=true, to_apply=%region_5.6 | all-reduce | flops 512 | bytes 4096 | tf_op jit(solution)/shard_map/psum | solution.py:88
  20.7 1.0 fusion.43
  22.0 1.0 fusion.42
  22.9 1.0 scatter_custom_fusion
  24.3 1.5 copy.110
  25.8 1.5 copy.107
  27.3 2.6 copy.108
  29.9 1.1 copy.90
  31.0 1.2 gather_fusion.1
  32.7 1.2 gather_fusion
  40.2 2.7 fusion.45
  42.9 2.1 convolution_convert_fusion
  45.0 68.6 %all-gather.4.cloned.1.call-done = bf16[2,1280,432]{1,0,2:T(2,128)(2,1)} async-done(((bf16[2,1280,108]{1,0,2:T(2,128)(2,1)}), bf16[2,1280,432]{1,0,2:T(2,128)(2,1)}) %all-gather.4.cloned.1.call-update) | async-done | bytes 2211856 | tf_op jit(solution)/shard_map/all_gather | solution.py:85
  114.1 8.0 %psum.23 = f32[256]{0:T(256)S(1)} all-reduce(f32[256]{0:T(256)S(1)} %fusion.8), channel_id=1, replica_groups=mesh['ra'=4,'rb'=32,'wt'=4] {'wt'}, use_global_device_ids=true, to_apply=%region_9.10 | all-reduce | flops 256 | bytes 2048 | tf_op jit(solution)/shard_map/psum | solution.py:116
  122.5 1.3 gather_fusion.2
  124.0 1.5 broadcast_select_fusion
  125.5 14.4 %all-to-all-start = ((bf16[128,2,1280]{2,1,0:T(2,128)(2,1)}), bf16[128,2,1280]{2,1,0:T(2,128)(2,1)S(1)}, u32[]{:S(2)}, u32[]{:S(2)}) async-start(bf16[128,2,1280]{2,1,0:T(2,128)(2,1)} %broadcast_select_fusion), calls=%async_computation | async-start | bytes 1310720 | tf_op jit(solution)/shard_map/all_to_all | solution.py:49
  140.6 35.7 %all-to-all-done = bf16[128,2,1280]{2,1,0:T(2,128)(2,1)S(1)} async-done(((bf16[128,2,1280]{2,1,0:T(2,128)(2,1)}), bf16[128,2,1280]{2,1,0:T(2,128)(2,1)S(1)}, u32[]{:S(2)}, u32[]{:S(2)}) %all-to-all-start) | async-done | bytes 655392 | tf_op jit(solution)/shard_map/all_to_all | solution.py:49
  176.6 2.2 scatter_custom_fusion.1
  178.9 59.0 %all-gather.6.cloned.1.call-done = bf16[32,36,1280]{2,1,0:T(8,128)(2,1)} async-done(((bf16[1,36,1280]{2,1,0:T(8,128)(2,1)}), bf16[32,36,1280]{2,1,0:T(8,128)(2,1)}) %all-gather.6.cloned.1.call-update) | async-done | bytes 2949136 | tf_op jit(solution)/shard_map/all_gather | solution.py:134
  237.9 3.7 %reshape.493 = bf16[1152,1280,1]{1,0,2:T(8,128)(2,1)S(1)} reshape(bf16[32,36,1280]{2,1,0:T(8,128)(2,1)} %all-gather.6.cloned.1.call-done) | data formatting | bytes 5898240
  241.6 6.6 %fusion.1 = f32[1152,2,432]{0,2,1:T(8,128)} fusion(bf16[1152,1280,1]{1,0,2:T(8,128)(2,1)S(1)} %reshape.493, bf16[2,1280,432]{1,0,2:T(2,128)(2,1)} %all-gather.4.cloned.1.call-done), kind=kOutput, calls=%fused_computation.11 | convolution fusion | flops 2548039680 | bytes 9142272 | tf_op jit(solution)/shard_map/tk,skn->tsn/dot_general | solution.py:135
  248.1 7.9 %copy.95 = f32[1152,2,432]{2,1,0:T(2,128)} copy(f32[1152,2,432]{0,2,1:T(8,128)} %fusion.1) | data formatting | bytes 7962624 | tf_op jit(solution)/shard_map/tk,skn->tsn/dot_general | solution.py:135
  256.0 7.2 %copy.96 = f32[32,36,2,432]{3,0,2,1:T(8,128)} copy(f32[32,36,2,432]{3,2,1,0:T(2,128)} %bitcast.35) | data formatting | bytes 7962624 | tf_op jit(solution)/shard_map/reshape | solution.py:136
  263.3 1.1 copy-done.8
  265.8 55.1 %reduce-scatter.2.cloned.1.call-done = f32[32,9,2,432]{3,0,2,1:T(8,128)} async-done(((f32[32,36,2,432]{3,0,2,1:T(8,128)}), f32[32,9,2,432]{3,0,2,1:T(8,128)}) %reduce-scatter.2.cloned.1.call-update) | async-done | bytes 995344 | tf_op jit(solution)/shard_map/reduce_scatter | solution.py:137
  320.9 1.4 fusion.44
  323.9 12.0 %all-to-all-start.1 = ((bf16[32,9,4,108]{3,0,1,2:T(8,128)(2,1)}), bf16[32,9,4,108]{3,0,1,2:T(8,128)(2,1)S(1)}, u32[]{:S(2)}, u32[]{:S(2)}) async-start(bf16[32,9,4,108]{3,0,1,2:T(8,128)(2,1)} %fusion.19), calls=%async_computation.2 | async-start | bytes 589824 | tf_op jit(solution)/shard_map/all_to_all | solution.py:141
  338.1 15.1 %all-to-all-done.1 = bf16[32,9,4,108]{3,0,1,2:T(8,128)(2,1)S(1)} async-done(((bf16[32,9,4,108]{3,0,1,2:T(8,128)(2,1)}), bf16[32,9,4,108]{3,0,1,2:T(8,128)(2,1)S(1)}, u32[]{:S(2)}, u32[]{:S(2)}) %all-to-all-start.1) | async-done | bytes 248864 | tf_op jit(solution)/shard_map/all_to_all | solution.py:141
  353.2 0.9 copy.103
  (99 shorter events, 16.3 us)
Async XLA Ops:
  7.2 106.5 %all-gather.4.cloned.1.call-start = ((), (), s32[]{:S(2)}) async-start(), calls=%async_computation.3 | async-start | bytes 2764800 | tf_op jit(solution)/shard_map/all_gather | solution.py:85
  7.2 2.5 copy-start.10
  9.6 1.1 copy-start.11
  9.9 10.6 %copy-start.13 = (f32[1280]{0:T(1024)S(1)}, f32[1280]{0:T(1024)}, u32[]{:S(2)}) copy-start(f32[1280]{0:T(1024)} %param.17) | copy-start | bytes 15364
  20.7 1.0 copy-start.16
  20.7 1.0 copy-start.14
  27.3 2.6 copy-start.3
  27.3 3.7 %copy-start = (s32[128]{0:T(128)S(1)}, s32[128]{0:T(128)}, u32[]{:S(2)}) copy-start(s32[128]{0:T(128)} %param.21) | copy-start | bytes 1540
  38.0 1.3 copy-start.2
  38.4 1.4 copy-start.1
  38.8 1.4 copy-start.7
  40.2 2.7 copy-start.12
  45.0 77.2 %copy-start.9 = (bf16[256,1280]{1,0:T(8,128)(2,1)S(1)}, bf16[256,1280]{1,0:T(8,128)(2,1)}, u32[]{:S(2)}) copy-start(bf16[256,1280]{1,0:T(8,128)(2,1)} %param.12) | copy-start | bytes 1966084
  45.0 77.1 %copy-start.15 = (f32[1280]{0:T(1024)S(1)}, f32[1280]{0:T(1024)}, u32[]{:S(2)}) copy-start(f32[1280]{0:T(1024)} %param.18) | copy-start | bytes 15364
  125.5 50.9 %all-to-all-start = ((bf16[128,2,1280]{2,1,0:T(2,128)(2,1)}), bf16[128,2,1280]{2,1,0:T(2,128)(2,1)S(1)}, u32[]{:S(2)}, u32[]{:S(2)}) async-start(bf16[128,2,1280]{2,1,0:T(2,128)(2,1)} %broadcast_select_fusion), calls=%async_computation | async-start | bytes 1310720 | tf_op jit(solution)/shard_map/all_to_all | solution.py:49
  139.9 97.9 %all-gather.6.cloned.1.call-start = ((), (), s32[]{:S(2)}) async-start(), calls=%async_computation.5 | async-start | bytes 3379200 | tf_op jit(solution)/shard_map/all_gather | solution.py:134
  178.9 142.0 %reduce-scatter.2.cloned.1.call-start = ((), (), s32[]{:S(2)}) async-start(), calls=%async_computation.4 | async-start | bytes 5898240 | tf_op jit(solution)/shard_map/reduce_scatter | solution.py:137
  263.2 1.1 copy-start.8
  323.9 12.1 %copy-start.17 = (s32[1,2]{1,0:T(1,128)S(1)}, s32[1,2]{1,0:T(1,128)}, u32[]{:S(2)}) copy-start(s32[1,2]{1,0:T(1,128)} %param.23) | copy-start | bytes 28
  323.9 29.3 %all-to-all-start.1 = ((bf16[32,9,4,108]{3,0,1,2:T(8,128)(2,1)}), bf16[32,9,4,108]{3,0,1,2:T(8,128)(2,1)S(1)}, u32[]{:S(2)}, u32[]{:S(2)}) async-start(bf16[32,9,4,108]{3,0,1,2:T(8,128)(2,1)} %fusion.19), calls=%async_computation.2 | async-start | bytes 589824 | tf_op jit(solution)/shard_map/all_to_all | solution.py:141
  336.1 1.1 copy-start.4
  337.2 0.9 copy-start.6
  338.1 16.0 %copy-start.5 = (bf16[2,128,1280]{2,1,0:T(8,128)(2,1)}, bf16[2,128,1280]{2,1,0:T(8,128)(2,1)S(1)}, u32[]{:S(2)}) copy-start(bf16[2,128,1280]{2,1,0:T(8,128)(2,1)S(1)} %scatter_fusion.1) | copy-start | bytes 1966084
Sparse Core Ops, SparseCore 0:
  10.1 103.4 all-gather.3
  179.0 58.8 all-gather.5
  263.4 57.4 reduce-scatter.1

commit v3 on v2

--- a/solution.py
+++ b/solution.py
@@ -111,7 +111,6 @@
         "hqk,khd->qhd", probabilities, value_heads, preferred_element_type=jnp.float32
     )
     attended = attended.astype(jnp.bfloat16).reshape(slot_count, feature_count)
-    attended, weights = lax.optimization_barrier((attended, weights))
     attended_f = attended.astype(jnp.float32)
     attn_sq = lax.psum(jnp.sum(attended_f * attended_f, axis=1), "wt")
     layer_rows = (
@@ -129,12 +128,15 @@
     key_cache = jnp.zeros_like(key_pages).at[placement].set(key_pages)
     value_cache = jnp.zeros_like(value_pages).at[placement].set(value_pages)
     regrouped = deal_rows(layer_rows, owner_start, owner_len, device, owners, LIVE)
+    regrouped, weights = lax.optimization_barrier((regrouped, weights))
     outer = lax.axis_size("ra")
     inner = lax.axis_size("rb")
     piece = lax.all_gather(regrouped, "rb", axis=0, tiled=True)
     stacked = jnp.einsum("tk,skn->tsn", piece, weights, preferred_element_type=jnp.float32)
-    stacked = stacked.reshape(inner, LIVE, 2, outer * unit_count)
-    summed = lax.psum_scatter(stacked, "wt", scatter_dimension=1, tiled=True)
+    parts = lax.axis_size("wt")
+    stacked = stacked.astype(jnp.bfloat16).reshape(inner, parts, LIVE // parts, 2, outer * unit_count)
+    stacked = lax.all_to_all(stacked, "wt", split_axis=1, concat_axis=1, tiled=True)
+    summed = jnp.sum(stacked.astype(jnp.float32), axis=1)
     gated = (jax.nn.silu(summed[:, :, 0]) * summed[:, :, 1]).astype(jnp.bfloat16)
     rows_here = gated.shape[1]
     gated = gated.reshape(inner, rows_here, outer, unit_count)

time: 363 us -> 300 us (0.83)
  waiting for transfers between devices: 234 us -> 160 us
  starting transfers between devices: 26.6 us -> 37.3 us
  local copies, waits for them, and re-layouts: 47.6 us -> 43.9 us
    all_gather x1, waiting for transfers between devices: 68.6 us -> 0.01 us  [per_device(): lax.all_gather(jnp.stack([gate_w, up_w]), 'ra', axis=2, tiled=True)]
    reduce_scatter x1 -> x0, waiting for transfers between devices: 55.1 us -> none  [per_device(): summed = lax.psum_scatter(stacked, 'wt', scatter_dimension=1, tiled=True)]
    all_to_all x0 -> x1, waiting for transfers between devices: none -> 25.3 us  [per_device(): lax.all_to_all(stacked, 'wt', split_axis=1, concat_axis=1, tiled=True)]
    all_to_all x1, waiting for transfers between devices: 35.7 us -> 56.8 us  [deal_rows(): lax.all_to_all(picked, ('ra', 'rb'), split_axis=0, concat_axis=0, tiled=T...]
    all_to_all x1, starting transfers between devices: 14.4 us -> 22.7 us  [deal_rows(): lax.all_to_all(picked, ('ra', 'rb'), split_axis=0, concat_axis=0, tiled=T...]
    dot_general x1 -> x0, local copies, waits for them, and re-layouts: 7.89 us -> none  [per_device(): jnp.einsum('tk,skn->tsn', piece, weights, preferred_element_type=jnp.floa...]
    convert_element_type x0 -> x3, local copies, waits for them, and re-layouts: none -> 6.84 us  [the longest x1 5.67 us: per_device(): stacked.astype(jnp.bfloat16)]
    reshape x1, local copies, waits for them, and re-layouts: 7.19 us -> 3.04 us  [per_device(): stacked.astype(jnp.bfloat16)]
  transfers between devices with their start and end apart: 5 -> 5, of which waited for: 5 -> 4; matrix products, arithmetic and copies ran while one was open for 8% -> 14% of each run, Pallas kernels for 0% -> 0%
where the time goes in v3:
time: 300 us; the launch traced here: 295 us
  waiting for transfers between devices  160 us (53%)
  local copies, waits for them, and re-layouts  43.9 us (15%)
  starting transfers between devices  37.3 us (12%)
  blocking collectives  16.1 us (5%)
  between operations  14.6 us (5%)
  other arithmetic  13 us (4%)
  matrix products  10.9 us (4%)
    all_gather x1, waiting for transfers between devices, per_device(): piece = lax.all_gather(regrouped, 'rb', axis=0, tiled=True)  62.8 us
    all_to_all x1, waiting for transfers between devices, deal_rows(): lax.all_to_all(picked, ('ra', 'rb'), split_axis=0, concat_axis=0, tiled=T...  56.8 us
    all_to_all x1, waiting for transfers between devices, per_device(): lax.all_to_all(stacked, 'wt', split_axis=1, concat_axis=1, tiled=True)  25.3 us
    all_to_all x1, starting transfers between devices, deal_rows(): lax.all_to_all(picked, ('ra', 'rb'), split_axis=0, concat_axis=0, tiled=T...  22.7 us
    all_to_all x1, waiting for transfers between devices, per_device(): gated = lax.all_to_all(gated, 'ra', split_axis=2, concat_axis=2, tiled=True)  14.9 us
    unnamed x53, local copies, waits for them, and re-layouts  14.4 us
    all_to_all x1, starting transfers between devices, per_device(): gated = lax.all_to_all(gated, 'ra', split_axis=2, concat_axis=2, tiled=True)  10.5 us
    psum x1, blocking collectives, per_device(): lax.psum((jnp.sum(query_f * query_f, axis=1), jnp.sum(key_f * key_f, axis...  9.29 us
  transfers between devices with their start and end apart: 5, of which 4 were waited for; matrix products, arithmetic and copies ran while one was open for 14% of the time, Pallas kernels for 0%

profile of v3, /device:TPU:1, one launch (start us, length us, event | category | flops | bytes accessed | tf_op | source)
XLA Modules:
  0.0 295.5 jit_solution(14080311544671479011)
XLA Ops:
  7.2 1.2 pad_maximum_fusion
  8.4 1.2 copy.90
  11.2 9.3 %all-reduce = (f32[256]{0:T(256)S(1)}, f32[256]{0:T(256)S(1)}) all-reduce(f32[256]{0:T(256)S(1)} %fusion.6, f32[256]{0:T(256)S(1)} %fusion.4), channel_id=1, replica_groups=mesh['ra'=4,'rb'=32,'wt'=4] {'wt'}, use_global_device_ids=true, to_apply=%region_5.6 | all-reduce | flops 512 | bytes 4096 | tf_op jit(solution)/shard_map/psum | solution.py:88
  21.3 1.0 fusion.40
  22.7 1.5 copy.112
  24.7 1.2 compare_select_fusion.4
  26.4 1.1 scatter_custom_fusion
  27.5 1.7 gather_fusion.1
  29.2 1.2 dynamic_slice.8
  33.6 1.5 copy.109
  35.1 2.6 copy.110
  37.7 1.1 copy.87
  41.5 2.7 fusion.41
  44.2 2.1 multiply_reduce_fusion
  46.8 6.8 %psum.23 = f32[256]{0:T(256)S(1)} all-reduce(f32[256]{0:T(256)S(1)} %get-tuple-element.37), channel_id=1, replica_groups=mesh['ra'=4,'rb'=32,'wt'=4] {'wt'}, use_global_device_ids=true, to_apply=%region_9.10 | all-reduce | flops 256 | bytes 2048 | tf_op jit(solution)/shard_map/psum | solution.py:115
  54.0 1.2 gather_fusion
  57.0 1.3 gather_fusion.2
  59.7 1.5 broadcast_select_fusion
  61.2 22.7 %all-to-all-start = ((bf16[128,2,1280]{2,1,0:T(2,128)(2,1)}), bf16[128,2,1280]{2,1,0:T(2,128)(2,1)S(1)}, u32[]{:S(2)}, u32[]{:S(2)}) async-start(bf16[128,2,1280]{2,1,0:T(2,128)(2,1)} %broadcast_select_fusion), calls=%async_computation | async-start | bytes 1310720 | tf_op jit(solution)/shard_map/all_to_all | solution.py:49
  84.6 56.8 %all-to-all-done = bf16[128,2,1280]{2,1,0:T(2,128)(2,1)S(1)} async-done(((bf16[128,2,1280]{2,1,0:T(2,128)(2,1)}), bf16[128,2,1280]{2,1,0:T(2,128)(2,1)S(1)}, u32[]{:S(2)}, u32[]{:S(2)}) %all-to-all-start) | async-done | bytes 655392 | tf_op jit(solution)/shard_map/all_to_all | solution.py:49
  141.6 2.2 scatter_custom_fusion.1
  143.8 62.8 %all-gather.6.cloned.1.call-done = bf16[32,36,1280]{2,1,0:T(8,128)(2,1)} async-done(((bf16[1,36,1280]{2,1,0:T(8,128)(2,1)}), bf16[32,36,1280]{2,1,0:T(8,128)(2,1)}) %all-gather.6.cloned.1.call-update) | async-done | bytes 2949136 | tf_op jit(solution)/shard_map/all_gather | solution.py:134
  206.6 3.7 %reshape.493 = bf16[1152,1280,1]{1,0,2:T(8,128)(2,1)S(1)} reshape(bf16[32,36,1280]{2,1,0:T(8,128)(2,1)} %all-gather.6.cloned.1.call-done) | data formatting | bytes 5898240
  210.3 6.0 %convolution_convert_fusion = bf16[1152,2,432]{0,2,1:T(8,128)(2,1)} fusion(bf16[1152,1280,1]{1,0,2:T(8,128)(2,1)S(1)} %reshape.493, bf16[2,1280,432]{1,0,2:T(2,128)(2,1)} %all-gather.4.cloned.1.call-done), kind=kOutput, calls=%fused_computation.9 | convolution fusion | flops 2549035008 | bytes 7151616 | tf_op jit(solution)/shard_map/tk,skn->tsn/dot_general | solution.py:135
  216.3 5.7 %copy.92 = bf16[1152,2,432]{2,1,0:T(2,128)(2,1)S(1)} copy(bf16[1152,2,432]{0,2,1:T(8,128)(2,1)} %convolution_convert_fusion) | data formatting | bytes 3981312 | tf_op jit(solution)/shard_map/convert_element_type | solution.py:137
  222.0 3.0 %copy.93 = bf16[32,4,9,2,432]{4,3,2,0,1:T(2,128)(2,1)} copy(bf16[32,4,9,2,432]{4,3,2,1,0:T(2,128)(2,1)S(1)} %bitcast.35) | data formatting | bytes 3981312 | tf_op jit(solution)/shard_map/reshape | solution.py:137
  225.0 4.0 %all-to-all-start.1 = ((bf16[32,4,9,2,432]{4,3,2,0,1:T(2,128)(2,1)}), bf16[32,4,9,2,432]{4,3,2,0,1:T(2,128)(2,1)S(1)}, u32[]{:S(2)}, u32[]{:S(2)}) async-start(bf16[32,4,9,2,432]{4,3,2,0,1:T(2,128)(2,1)} %copy.93), calls=%async_computation.1 | async-start | bytes 4718592 | tf_op jit(solution)/shard_map/all_to_all | solution.py:138
  229.1 1.6 copy.106
  230.6 1.2 reshape.497
  232.4 25.3 %all-to-all-done.1 = bf16[32,4,9,2,432]{4,3,2,0,1:T(2,128)(2,1)S(1)} async-done(((bf16[32,4,9,2,432]{4,3,2,0,1:T(2,128)(2,1)}), bf16[32,4,9,2,432]{4,3,2,0,1:T(2,128)(2,1)S(1)}, u32[]{:S(2)}, u32[]{:S(2)}) %all-to-all-start.1) | async-done | bytes 1990688 | tf_op jit(solution)/shard_map/all_to_all | solution.py:138
  260.1 10.5 %all-to-all-start.2 = ((bf16[32,9,4,108]{3,0,1,2:T(8,128)(2,1)}), bf16[32,9,4,108]{3,0,1,2:T(8,128)(2,1)S(1)}, u32[]{:S(2)}, u32[]{:S(2)}) async-start(bf16[32,9,4,108]{3,0,1,2:T(8,128)(2,1)} %copy.98), calls=%async_computation.2 | async-start | bytes 589824 | tf_op jit(solution)/shard_map/all_to_all | solution.py:143
  272.8 14.9 %all-to-all-done.2 = bf16[32,9,4,108]{3,0,1,2:T(8,128)(2,1)S(1)} async-done(((bf16[32,9,4,108]{3,0,1,2:T(8,128)(2,1)}), bf16[32,9,4,108]{3,0,1,2:T(8,128)(2,1)S(1)}, u32[]{:S(2)}, u32[]{:S(2)}) %all-to-all-start.2) | async-done | bytes 248864 | tf_op jit(solution)/shard_map/all_to_all | solution.py:143
  (107 shorter events, 20.4 us)
Async XLA Ops:
  7.2 136.6 %all-gather.4.cloned.1.call-start = ((), (), s32[]{:S(2)}) async-start(), calls=%async_computation.3 | async-start | bytes 2764800 | tf_op jit(solution)/shard_map/all_gather | solution.py:85
  7.2 3.0 %copy-start.9 = (bf16[256,1280]{1,0:T(8,128)(2,1)S(1)}, bf16[256,1280]{1,0:T(8,128)(2,1)}, u32[]{:S(2)}) copy-start(bf16[256,1280]{1,0:T(8,128)(2,1)} %param.13) | copy-start | bytes 1966084
  9.6 1.1 copy-start.10
  10.5 10.5 %copy-start.14 = (f32[1280]{0:T(1024)S(1)}, f32[1280]{0:T(1024)}, u32[]{:S(2)}) copy-start(f32[1280]{0:T(1024)} %param.17) | copy-start | bytes 15364
  22.6 4.9 %copy-start = (s32[128]{0:T(128)S(1)}, s32[128]{0:T(128)}, u32[]{:S(2)}) copy-start(s32[128]{0:T(128)} %param.21) | copy-start | bytes 1540
  22.6 9.1 %copy-start.15 = (f32[1280]{0:T(1024)S(1)}, f32[1280]{0:T(1024)}, u32[]{:S(2)}) copy-start(f32[1280]{0:T(1024)} %param.16) | copy-start | bytes 15364
  31.0 0.7 copy-start.18
  35.1 2.6 copy-start.3
  38.8 1.3 copy-start.2
  39.2 1.4 copy-start.1
  40.6 0.8 copy-start.8
  40.6 0.9 copy-start.13
  41.5 2.7 copy-start.11
  46.3 10.2 %copy-start.17 = (s32[2]{0:T(128)S(1)}, s32[2]{0:T(128)}, u32[]{:S(2)}) copy-start(s32[2]{0:T(128)} %iota_multiply_fusion.1) | copy-start | bytes 28
  46.3 10.4 %copy-start.12 = (bf16[256,1280]{1,0:T(8,128)(2,1)S(1)}, bf16[256,1280]{1,0:T(8,128)(2,1)}, u32[]{:S(2)}) copy-start(bf16[256,1280]{1,0:T(8,128)(2,1)} %param.12) | copy-start | bytes 1966084
  46.4 10.4 %copy-start.16 = (f32[1280]{0:T(1024)S(1)}, f32[1280]{0:T(1024)}, u32[]{:S(2)}) copy-start(f32[1280]{0:T(1024)} %param.18) | copy-start | bytes 15364
  58.3 0.6 copy-start.20
  61.2 80.2 %all-to-all-start = ((bf16[128,2,1280]{2,1,0:T(2,128)(2,1)}), bf16[128,2,1280]{2,1,0:T(2,128)(2,1)S(1)}, u32[]{:S(2)}, u32[]{:S(2)}) async-start(bf16[128,2,1280]{2,1,0:T(2,128)(2,1)} %broadcast_select_fusion), calls=%async_computation | async-start | bytes 1310720 | tf_op jit(solution)/shard_map/all_to_all | solution.py:49
  83.9 122.7 %all-gather.6.cloned.1.call-start = ((), (), s32[]{:S(2)}) async-start(), calls=%async_computation.4 | async-start | bytes 3379200 | tf_op jit(solution)/shard_map/all_gather | solution.py:134
  225.0 32.7 %all-to-all-start.1 = ((bf16[32,4,9,2,432]{4,3,2,0,1:T(2,128)(2,1)}), bf16[32,4,9,2,432]{4,3,2,0,1:T(2,128)(2,1)S(1)}, u32[]{:S(2)}, u32[]{:S(2)}) async-start(bf16[32,4,9,2,432]{4,3,2,0,1:T(2,128)(2,1)} %copy.93), calls=%async_computation.1 | async-start | bytes 4718592 | tf_op jit(solution)/shard_map/all_to_all | solution.py:138
  259.0 11.6 %copy-start.5 = (bf16[2,128,1280]{2,1,0:T(8,128)(2,1)S(1)}, bf16[2,128,1280]{2,1,0:T(8,128)(2,1)}, u32[]{:S(2)}) copy-start(bf16[2,128,1280]{2,1,0:T(8,128)(2,1)} %reshape.497) | copy-start | bytes 1966084
  259.3 11.4 %copy-start.21 = (s32[1,2]{1,0:T(1,128)S(1)}, s32[1,2]{1,0:T(1,128)}, u32[]{:S(2)}) copy-start(s32[1,2]{1,0:T(1,128)} %param.23) | copy-start | bytes 28
  260.1 27.6 %all-to-all-start.2 = ((bf16[32,9,4,108]{3,0,1,2:T(8,128)(2,1)}), bf16[32,9,4,108]{3,0,1,2:T(8,128)(2,1)S(1)}, u32[]{:S(2)}, u32[]{:S(2)}) async-start(bf16[32,9,4,108]{3,0,1,2:T(8,128)(2,1)} %copy.98), calls=%async_computation.2 | async-start | bytes 589824 | tf_op jit(solution)/shard_map/all_to_all | solution.py:143
  270.7 1.1 copy-start.4
  270.7 1.1 copy-start.19
  271.8 0.9 copy-start.7
  272.7 15.9 %copy-start.6 = (bf16[2,128,1280]{2,1,0:T(8,128)(2,1)}, bf16[2,128,1280]{2,1,0:T(8,128)(2,1)S(1)}, u32[]{:S(2)}) copy-start(bf16[2,128,1280]{2,1,0:T(8,128)(2,1)S(1)} %scatter_fusion.1) | copy-start | bytes 1966084
Sparse Core Ops, SparseCore 0:
  10.1 129.2 all-gather.3
  144.0 62.6 all-gather.5

commit v4 on v1

--- a/solution.py
+++ b/solution.py
@@ -82,6 +82,7 @@
     owner_start = starts[owner_req]
     owner_len = lengths[owner_req]
     my_length = owner_len[device]
+    weights = lax.all_gather(jnp.stack([gate_w, up_w]), "rb", axis=2, tiled=True)
     query_f = queries.astype(jnp.float32)
     key_f = key_proj.astype(jnp.float32)
     query_sq, key_sq = lax.psum(
@@ -127,13 +128,15 @@
     key_cache = jnp.zeros_like(key_pages).at[placement].set(key_pages)
     value_cache = jnp.zeros_like(value_pages).at[placement].set(value_pages)
     regrouped = deal_rows(layer_rows, owner_start, owner_len, device, owners, LIVE)
+    regrouped, weights = lax.optimization_barrier((regrouped, weights))
     outer = lax.axis_size("ra")
     inner = lax.axis_size("rb")
     piece = lax.all_gather(regrouped, "ra", axis=0, tiled=True)
-    weights = lax.all_gather(jnp.stack([gate_w, up_w]), "rb", axis=2, tiled=True)
     stacked = jnp.einsum("tk,skn->tsn", piece, weights, preferred_element_type=jnp.float32)
-    stacked = stacked.reshape(outer, LIVE, 2, inner * unit_count)
-    summed = lax.psum_scatter(stacked, "wt", scatter_dimension=1, tiled=True)
+    parts = lax.axis_size("wt")
+    stacked = stacked.astype(jnp.bfloat16).reshape(outer, parts, LIVE // parts, 2, inner * unit_count)
+    stacked = lax.all_to_all(stacked, "wt", split_axis=1, concat_axis=1, tiled=True)
+    summed = jnp.sum(stacked.astype(jnp.float32), axis=1)
     gated = (jax.nn.silu(summed[:, :, 0]) * summed[:, :, 1]).astype(jnp.bfloat16)
     rows_here = gated.shape[1]
     gated = gated.reshape(outer, rows_here, inner, unit_count)
@@ -143,7 +146,7 @@
 
 
 def solution(mesh):
-    inner = 4
+    inner = 8
     outer = mesh.shape["req"] // inner
     split = Mesh(mesh.devices.reshape(outer, inner, mesh.shape["wt"]), ("ra", "rb", "wt"))
     req = ("ra", "rb")

time: 411 us -> 238 us (0.58)
  waiting for transfers between devices: 278 us -> 107 us
  starting transfers between devices: 27.8 us -> 43.1 us
  local copies, waits for them, and re-layouts: 50.9 us -> 36.4 us
    all_gather x1, waiting for transfers between devices: 141 us -> 55.6 us  [per_device(): piece = lax.all_gather(regrouped, 'ra', axis=0, tiled=True)]
    reduce_scatter x1 -> x0, waiting for transfers between devices: 56.7 us -> none  [per_device(): summed = lax.psum_scatter(stacked, 'wt', scatter_dimension=1, tiled=True)]
    all_gather x1, waiting for transfers between devices: 41 us -> 0.01 us  [per_device(): lax.all_gather(jnp.stack([gate_w, up_w]), 'rb', axis=2, tiled=True)]
    all_to_all x1, starting transfers between devices: 4.06 us -> 16.2 us  [per_device(): gated = lax.all_to_all(gated, 'rb', split_axis=2, concat_axis=2, tiled=True)]
    all_to_all x0 -> x1, waiting for transfers between devices: none -> 10.4 us  [per_device(): lax.all_to_all(stacked, 'wt', split_axis=1, concat_axis=1, tiled=True)]
    dot_general x1 -> x0, local copies, waits for them, and re-layouts: 7.91 us -> none  [per_device(): jnp.einsum('tk,skn->tsn', piece, weights, preferred_element_type=jnp.floa...]
    reshape x1, local copies, waits for them, and re-layouts: 7.21 us -> 2.75 us  [per_device(): stacked.astype(jnp.bfloat16)]
    unnamed x55 -> x43, local copies, waits for them, and re-layouts: 16.3 us -> 12.6 us
  transfers between devices with their start and end apart: 5 -> 5, of which waited for: 5 -> 4; matrix products, arithmetic and copies ran while one was open for 2% -> 16% of each run, Pallas kernels for 0% -> 0%
where the time goes in v4:
time: 238 us
  waiting for transfers between devices  107 us (45%)
  starting transfers between devices  43.1 us (18%)
  local copies, waits for them, and re-layouts  36.4 us (15%)
  blocking collectives  16.1 us (7%)
  between operations  14.5 us (6%)
  other arithmetic  10.4 us (4%)
  matrix products  10.2 us (4%)
    all_gather x1, waiting for transfers between devices, per_device(): piece = lax.all_gather(regrouped, 'ra', axis=0, tiled=True)  55.6 us
    all_to_all x1, waiting for transfers between devices, deal_rows(): lax.all_to_all(picked, ('ra', 'rb'), split_axis=0, concat_axis=0, tiled=T...  35.7 us
    all_to_all x1, starting transfers between devices, deal_rows(): lax.all_to_all(picked, ('ra', 'rb'), split_axis=0, concat_axis=0, tiled=T...  22.9 us
    all_to_all x1, starting transfers between devices, per_device(): gated = lax.all_to_all(gated, 'rb', split_axis=2, concat_axis=2, tiled=True)  16.2 us
    unnamed x43, local copies, waits for them, and re-layouts  12.6 us
    all_to_all x1, waiting for transfers between devices, per_device(): lax.all_to_all(stacked, 'wt', split_axis=1, concat_axis=1, tiled=True)  10.4 us
    psum x1, blocking collectives, per_device(): lax.psum((jnp.sum(query_f * query_f, axis=1), jnp.sum(key_f * key_f, axis...  9.29 us
    psum x1, blocking collectives, per_device(): attn_sq = lax.psum(jnp.sum(attended_f * attended_f, axis=1), 'wt')  6.81 us
  transfers between devices with their start and end apart: 5, of which 4 were waited for; matrix products, arithmetic and copies ran while one was open for 16% of the time, Pallas kernels for 0%

profile of v4, /device:TPU:1, one launch (start us, length us, event | category | flops | bytes accessed | tf_op | source)
XLA Modules:
  0.0 237.6 jit_solution(4864117195153276561)
XLA Ops:
  7.2 1.2 pad_maximum_fusion
  8.4 1.2 copy.89
  11.1 9.3 %all-reduce = (f32[256]{0:T(256)S(1)}, f32[256]{0:T(256)S(1)}) all-reduce(f32[256]{0:T(256)S(1)} %fusion.10, f32[256]{0:T(256)S(1)} %fusion.8), channel_id=1, replica_groups=mesh['ra'=16,'rb'=8,'wt'=4] {'wt'}, use_global_device_ids=true, to_apply=%region_5.6 | all-reduce | flops 512 | bytes 4096 | tf_op jit(solution)/shard_map/psum | solution.py:88
  20.7 1.0 fusion.42
  22.1 1.5 copy.111
  23.8 0.9 fusion.41
  24.8 1.5 copy.108
  26.3 2.6 %copy.109 = f32[256,10,64]{2,0,1:T(8,128)} copy(f32[256,10,64]{0,2,1:T(8,128)} %get-tuple-element.25) | data formatting | bytes 1310720
  28.9 1.1 copy.86
  30.0 1.0 scatter_custom_fusion
  31.0 1.2 gather_fusion.1
  36.4 2.7 %fusion.43 = (f32[10,256]{1,0:T(8,128)S(1)}, f32[10,256,256]{1,2,0:T(8,128)}) fusion(pred[256,256]{0,1:T(8,128)(4,1)S(1)} %fusion.19, bf16[256,10,128]{2,0,1:T(8,128)(2,1)S(1)} %maximum_convert_fusion, bf16[256,10,64]{2,0,1:T(8,128)(2,1)S(1)} %get-tuple-element.22, bf16[256,10,64]{2,0,1:T(8,128)(2,1)S(1)} %get-tuple-element.21), kind=kOutput, calls=%fused_computation.94 | convolution fusion | flops 171704576 | bytes 4007936 | tf_op jit(solution)/shard_map/sub | solution.py:107
  39.1 2.1 multiply_reduce_fusion
  42.1 1.2 gather_fusion
  44.8 6.8 %psum.23 = f32[256]{0:T(256)S(1)} all-reduce(f32[256]{0:T(256)S(1)} %get-tuple-element.37), channel_id=1, replica_groups=mesh['ra'=16,'rb'=8,'wt'=4] {'wt'}, use_global_device_ids=true, to_apply=%region_9.10 | all-reduce | flops 256 | bytes 2048 | tf_op jit(solution)/shard_map/psum | solution.py:115
  51.9 1.2 gather_fusion.2
  54.3 1.5 broadcast_select_fusion
  55.8 22.9 %all-to-all-start = ((bf16[128,2,1280]{2,1,0:T(2,128)(2,1)}), bf16[128,2,1280]{2,1,0:T(2,128)(2,1)S(1)}, u32[]{:S(2)}, u32[]{:S(2)}) async-start(bf16[128,2,1280]{2,1,0:T(2,128)(2,1)} %broadcast_select_fusion), calls=%async_computation | async-start | bytes 1310720 | tf_op jit(solution)/shard_map/all_to_all | solution.py:49
  79.4 35.7 %all-to-all-done = bf16[128,2,1280]{2,1,0:T(2,128)(2,1)S(1)} async-done(((bf16[128,2,1280]{2,1,0:T(2,128)(2,1)}), bf16[128,2,1280]{2,1,0:T(2,128)(2,1)S(1)}, u32[]{:S(2)}, u32[]{:S(2)}) %all-to-all-start) | async-done | bytes 655392 | tf_op jit(solution)/shard_map/all_to_all | solution.py:49
  115.4 2.2 scatter_custom_fusion.1
  117.6 55.6 %all-gather.6.cloned.1.call-done = bf16[16,36,1280]{2,1,0:T(8,128)(2,1)} async-done(((bf16[1,36,1280]{2,1,0:T(8,128)(2,1)}), bf16[16,36,1280]{2,1,0:T(8,128)(2,1)}) %all-gather.6.cloned.1.call-update) | async-done | bytes 1474576 | tf_op jit(solution)/shard_map/all_gather | solution.py:134
  173.2 2.3 reshape.493
  175.5 5.4 %fusion.4 = bf16[576,2,864]{2,0,1:T(8,128)(2,1)S(1)} fusion(bf16[576,1280,1]{1,0,2:T(8,128)(2,1)S(1)} %reshape.493, bf16[2,1280,864]{1,0,2:T(2,128)(2,1)} %all-gather.4.cloned.1.call-done), kind=kOutput, calls=%fused_computation.15 | convolution fusion | flops 2549035008 | bytes 7888896 | tf_op jit(solution)/shard_map/tk,skn->tsn/dot_general | solution.py:135
  180.9 2.1 copy.91
  183.0 2.7 %copy.92 = bf16[16,4,9,2,864]{4,3,2,0,1:T(2,128)(2,1)} copy(bf16[16,4,9,2,864]{4,3,2,1,0:T(2,128)(2,1)S(1)} %bitcast.37) | data formatting | bytes 3981312 | tf_op jit(solution)/shard_map/reshape | solution.py:137
  185.7 4.0 %all-to-all-start.1 = ((bf16[16,4,9,2,864]{4,3,2,0,1:T(2,128)(2,1)}), bf16[16,4,9,2,864]{4,3,2,0,1:T(2,128)(2,1)S(1)}, u32[]{:S(2)}, u32[]{:S(2)}) async-start(bf16[16,4,9,2,864]{4,3,2,0,1:T(2,128)(2,1)} %copy.92), calls=%async_computation.1 | async-start | bytes 4128768 | tf_op jit(solution)/shard_map/all_to_all | solution.py:138
  189.7 1.6 copy.105
  191.3 1.2 reshape.497
  193.2 1.2 broadcast_select_fusion.1
  194.5 10.4 %all-to-all-done.1 = bf16[16,4,9,2,864]{4,3,2,0,1:T(2,128)(2,1)S(1)} async-done(((bf16[16,4,9,2,864]{4,3,2,0,1:T(2,128)(2,1)}), bf16[16,4,9,2,864]{4,3,2,0,1:T(2,128)(2,1)S(1)}, u32[]{:S(2)}, u32[]{:S(2)}) %all-to-all-start.1) | async-done | bytes 1990688 | tf_op jit(solution)/shard_map/all_to_all | solution.py:138
  206.8 16.2 %all-to-all-start.2 = ((bf16[16,9,8,108]{3,0,1,2:T(8,128)(2,1)}), bf16[16,9,8,108]{3,0,1,2:T(8,128)(2,1)S(1)}, u32[]{:S(2)}, u32[]{:S(2)}) async-start(bf16[16,9,8,108]{3,0,1,2:T(8,128)(2,1)} %copy.97), calls=%async_computation.2 | async-start | bytes 589824 | tf_op jit(solution)/shard_map/all_to_all | solution.py:143
  224.6 5.2 %all-to-all-done.2 = bf16[16,9,8,108]{3,0,1,2:T(8,128)(2,1)S(1)} async-done(((bf16[16,9,8,108]{3,0,1,2:T(8,128)(2,1)}), bf16[16,9,8,108]{3,0,1,2:T(8,128)(2,1)S(1)}, u32[]{:S(2)}, u32[]{:S(2)}) %all-to-all-start.2) | async-done | bytes 248864 | tf_op jit(solution)/shard_map/all_to_all | solution.py:143
  (97 shorter events, 16.3 us)
Async XLA Ops:
  7.2 110.4 %all-gather.4.cloned.1.call-start = ((), (), s32[]{:S(2)}) async-start(), calls=%async_computation.3 | async-start | bytes 4976640 | tf_op jit(solution)/shard_map/all_gather | solution.py:85
  7.2 2.4 %copy-start.8 = (bf16[256,1280]{1,0:T(8,128)(2,1)S(1)}, bf16[256,1280]{1,0:T(8,128)(2,1)}, u32[]{:S(2)}) copy-start(bf16[256,1280]{1,0:T(8,128)(2,1)} %param.14) | copy-start | bytes 1966084
  9.6 1.1 copy-start.9
  9.9 10.6 %copy-start.12 = (f32[1280]{0:T(1024)S(1)}, f32[1280]{0:T(1024)}, u32[]{:S(2)}) copy-start(f32[1280]{0:T(1024)} %param.17) | copy-start | bytes 15364
  22.0 1.5 copy-start.13
  26.3 2.6 %copy-start.3 = (bf16[256,1280]{1,0:T(8,128)(2,1)S(1)}, bf16[256,1280]{1,0:T(8,128)(2,1)}, u32[]{:S(2)}) copy-start(bf16[256,1280]{1,0:T(8,128)(2,1)} %param.15) | copy-start | bytes 1966084
  26.3 3.7 %copy-start.15 = (s32[128]{0:T(128)S(1)}, s32[128]{0:T(128)}, u32[]{:S(2)}) copy-start(s32[128]{0:T(128)} %param.22) | copy-start | bytes 1540
  26.3 4.7 %copy-start = (s32[128]{0:T(128)S(1)}, s32[128]{0:T(128)}, u32[]{:S(2)}) copy-start(s32[128]{0:T(128)} %param.21) | copy-start | bytes 1540
  34.0 1.4 copy-start.2
  34.4 1.6 copy-start.1
  34.8 1.6 copy-start.7
  36.4 2.7 %copy-start.10 = (bf16[256,1280]{0,1:T(8,128)(2,1)S(1)}, bf16[256,1280]{0,1:T(8,128)(2,1)}, u32[]{:S(2)}) copy-start(bf16[256,1280]{0,1:T(8,128)(2,1)} %copy.86) | copy-start | bytes 1966084
  41.3 10.4 %copy-start.11 = (bf16[256,1280]{1,0:T(8,128)(2,1)S(1)}, bf16[256,1280]{1,0:T(8,128)(2,1)}, u32[]{:S(2)}) copy-start(bf16[256,1280]{1,0:T(8,128)(2,1)} %param.12) | copy-start | bytes 1966084
  41.3 10.4 %copy-start.14 = (f32[1280]{0:T(1024)S(1)}, f32[1280]{0:T(1024)}, u32[]{:S(2)}) copy-start(f32[1280]{0:T(1024)} %param.18) | copy-start | bytes 15364
  55.8 59.3 %all-to-all-start = ((bf16[128,2,1280]{2,1,0:T(2,128)(2,1)}), bf16[128,2,1280]{2,1,0:T(2,128)(2,1)S(1)}, u32[]{:S(2)}, u32[]{:S(2)}) async-start(bf16[128,2,1280]{2,1,0:T(2,128)(2,1)} %broadcast_select_fusion), calls=%async_computation | async-start | bytes 1310720 | tf_op jit(solution)/shard_map/all_to_all | solution.py:49
  78.7 94.5 %all-gather.6.cloned.1.call-start = ((), (), s32[]{:S(2)}) async-start(), calls=%async_computation.4 | async-start | bytes 1740800 | tf_op jit(solution)/shard_map/all_gather | solution.py:134
  185.7 19.2 %all-to-all-start.1 = ((bf16[16,4,9,2,864]{4,3,2,0,1:T(2,128)(2,1)}), bf16[16,4,9,2,864]{4,3,2,0,1:T(2,128)(2,1)S(1)}, u32[]{:S(2)}, u32[]{:S(2)}) async-start(bf16[16,4,9,2,864]{4,3,2,0,1:T(2,128)(2,1)} %copy.92), calls=%async_computation.1 | async-start | bytes 4128768 | tf_op jit(solution)/shard_map/all_to_all | solution.py:138
  192.5 1.9 copy-start.4
  205.9 17.1 %copy-start.16 = (s32[1,2]{1,0:T(1,128)S(1)}, s32[1,2]{1,0:T(1,128)}, u32[]{:S(2)}) copy-start(s32[1,2]{1,0:T(1,128)} %param.23) | copy-start | bytes 28
  206.8 23.0 %all-to-all-start.2 = ((bf16[16,9,8,108]{3,0,1,2:T(8,128)(2,1)}), bf16[16,9,8,108]{3,0,1,2:T(8,128)(2,1)S(1)}, u32[]{:S(2)}, u32[]{:S(2)}) async-start(bf16[16,9,8,108]{3,0,1,2:T(8,128)(2,1)} %copy.97), calls=%async_computation.2 | async-start | bytes 589824 | tf_op jit(solution)/shard_map/all_to_all | solution.py:143
  223.8 0.8 copy-start.6
  224.6 6.2 %copy-start.5 = (bf16[2,128,1280]{2,1,0:T(8,128)(2,1)}, bf16[2,128,1280]{2,1,0:T(8,128)(2,1)S(1)}, u32[]{:S(2)}) copy-start(bf16[2,128,1280]{2,1,0:T(8,128)(2,1)S(1)} %scatter_fusion.1) | copy-start | bytes 1966084
Sparse Core Ops, SparseCore 0:
  10.1 46.4 all-gather.3
  117.7 55.3 all-gather.5

commit v5 on v4

--- a/solution.py
+++ b/solution.py
@@ -82,7 +82,12 @@
     owner_start = starts[owner_req]
     owner_len = lengths[owner_req]
     my_length = owner_len[device]
-    weights = lax.all_gather(jnp.stack([gate_w, up_w]), "rb", axis=2, tiled=True)
+    inner_count = lax.axis_size("rb")
+    own_weights = jnp.stack([gate_w, up_w])
+    weights = lax.all_to_all(
+        jnp.broadcast_to(own_weights[None], (inner_count,) + own_weights.shape), "rb", 0, 0, tiled=True
+    )
+    weights = jnp.transpose(weights, (1, 2, 0, 3)).reshape(2, own_weights.shape[1], -1)
     query_f = queries.astype(jnp.float32)
     key_f = key_proj.astype(jnp.float32)
     query_sq, key_sq = lax.psum(
@@ -111,6 +116,7 @@
         "hqk,khd->qhd", probabilities, value_heads, preferred_element_type=jnp.float32
     )
     attended = attended.astype(jnp.bfloat16).reshape(slot_count, feature_count)
+    attended, weights = lax.optimization_barrier((attended, weights))
     attended_f = attended.astype(jnp.float32)
     attn_sq = lax.psum(jnp.sum(attended_f * attended_f, axis=1), "wt")
     layer_rows = (
@@ -128,10 +134,18 @@
     key_cache = jnp.zeros_like(key_pages).at[placement].set(key_pages)
     value_cache = jnp.zeros_like(value_pages).at[placement].set(value_pages)
     regrouped = deal_rows(layer_rows, owner_start, owner_len, device, owners, LIVE)
-    regrouped, weights = lax.optimization_barrier((regrouped, weights))
     outer = lax.axis_size("ra")
     inner = lax.axis_size("rb")
-    piece = lax.all_gather(regrouped, "ra", axis=0, tiled=True)
+    ring_pos = lax.axis_index("ra")
+    ahead, behind = regrouped, regrouped
+    arrived = {0: regrouped}
+    for step in range(1, outer // 2 + 1):
+        ahead = lax.ppermute(ahead, "ra", [(j, (j + 1) % outer) for j in range(outer)])
+        arrived[step] = ahead
+        if step < outer - step:
+            behind = lax.ppermute(behind, "ra", [(j, (j - 1) % outer) for j in range(outer)])
+            arrived[outer - step] = behind
+    piece = jnp.concatenate([arrived[k] for k in range(outer)], axis=0)
     stacked = jnp.einsum("tk,skn->tsn", piece, weights, preferred_element_type=jnp.float32)
     parts = lax.axis_size("wt")
     stacked = stacked.astype(jnp.bfloat16).reshape(outer, parts, LIVE // parts, 2, inner * unit_count)
@@ -141,6 +155,8 @@
     rows_here = gated.shape[1]
     gated = gated.reshape(outer, rows_here, inner, unit_count)
     gated = lax.all_to_all(gated, "rb", split_axis=2, concat_axis=2, tiled=True)
+    source_order = (ring_pos - jnp.arange(outer, dtype=jnp.int32)) % outer
+    gated = jnp.take(gated, source_order, axis=0)
     gated = jnp.transpose(gated, (0, 2, 1, 3)).reshape(outer * inner, rows_here, unit_count)
     return (gated, key_cache, value_cache)
 

time: 238 us -> 255 us (1.071)
  starting transfers between devices: 43.1 us -> 96.4 us
  waiting for transfers between devices: 107 us -> 75.3 us
  between operations: 14.5 us -> 1.32 us
  local copies, waits for them, and re-layouts: 36.4 us -> 46.3 us
  blocking collectives: 16.1 us -> 13 us
    all_gather x2 -> x0, waiting for transfers between devices: 55.6 us -> none  [the longest x1 55.6 us: per_device(): piece = lax.all_gather(regrouped, 'ra', axis=0, tiled=True)]
    ppermute x0 -> x15, starting transfers between devices: none -> 50 us  [the longest x7 27.9 us: per_device(): lax.ppermute(behind, 'ra', [(j, (j - 1) % outer) for j in range(outer)])]
    all_to_all x0 -> x1, waiting for transfers between devices: none -> 18.5 us  [per_device(): lax.all_to_all(jnp.broadcast_to(own_weights[None], (inner_count,) + own_w...]
    all_to_all x0 -> x1, starting transfers between devices: none -> 11.5 us  [per_device(): lax.all_to_all(jnp.broadcast_to(own_weights[None], (inner_count,) + own_w...]
    all_to_all x1, starting transfers between devices: 22.9 us -> 17 us  [deal_rows(): lax.all_to_all(picked, ('ra', 'rb'), split_axis=0, concat_axis=0, tiled=T...]
    ppermute x0 -> x15, waiting for transfers between devices: none -> 5.81 us  [the longest x8 5.77 us: per_device(): lax.ppermute(ahead, 'ra', [(j, (j + 1) % outer) for j in range(outer)])]
    reshape x0 -> x1, local copies, waits for them, and re-layouts: none -> 4.9 us  [per_device(): jnp.transpose(weights, (1, 2, 0, 3)).reshape(2, own_weights.shape[1], -1)]
    broadcast_in_dim x0 -> x1, local copies, waits for them, and re-layouts: none -> 4.37 us  [per_device(): jnp.broadcast_to(own_weights[None], (inner_count,) + own_weights.shape)]
  transfers between devices with their start and end apart: 5 -> 19, of which waited for: 4 -> 6; matrix products, arithmetic and copies ran while one was open for 16% -> 13% of each run, Pallas kernels for 0% -> 0%
where the time goes in v5:
time: 255 us; the launch traced here: 253 us
  starting transfers between devices  96.4 us (38%)
  waiting for transfers between devices  75.3 us (30%)
  local copies, waits for them, and re-layouts  46.3 us (18%)
  blocking collectives  13 us (5%)
  other arithmetic  10.8 us (4%)
  matrix products  10.2 us (4%)
    all_to_all x1, waiting for transfers between devices, deal_rows(): lax.all_to_all(picked, ('ra', 'rb'), split_axis=0, concat_axis=0, tiled=T...  35.8 us
    ppermute x7, starting transfers between devices, per_device(): lax.ppermute(behind, 'ra', [(j, (j - 1) % outer) for j in range(outer)])  27.9 us
    ppermute x8, starting transfers between devices, per_device(): lax.ppermute(ahead, 'ra', [(j, (j + 1) % outer) for j in range(outer)])  22.1 us
    all_to_all x1, waiting for transfers between devices, per_device(): lax.all_to_all(jnp.broadcast_to(own_weights[None], (inner_count,) + own_w...  18.5 us
    all_to_all x1, starting transfers between devices, deal_rows(): lax.all_to_all(picked, ('ra', 'rb'), split_axis=0, concat_axis=0, tiled=T...  17 us
    all_to_all x1, starting transfers between devices, per_device(): gated = lax.all_to_all(gated, 'rb', split_axis=2, concat_axis=2, tiled=True)  14.3 us
    all_to_all x1, starting transfers between devices, per_device(): lax.all_to_all(jnp.broadcast_to(own_weights[None], (inner_count,) + own_w...  11.5 us
    unnamed x40, local copies, waits for them, and re-layouts  10.1 us
  transfers between devices with their start and end apart: 19, of which 6 were waited for; matrix products, arithmetic and copies ran while one was open for 13% of the time, Pallas kernels for 0%

profile of v5, /device:TPU:1, one launch (start us, length us, event | category | flops | bytes accessed | tf_op | source)
XLA Modules:
  0.0 253.3 jit_solution(16332905158185459111)
XLA Ops:
  2.2 4.4 %broadcast_in_dim.108 = bf16[8,2,1280,108]{2,1,3,0:T(2,128)(2,1)} broadcast(bf16[2,1280,108]{1,0,2:T(2,128)(2,1)S(1)} %copy.110), dimensions={1,2,3} | broadcast | bytes 4976640 | tf_op jit(solution)/shard_map/broadcast_in_dim | solution.py:88
  6.5 11.5 %all-to-all-start = ((bf16[8,2,1280,108]{2,1,3,0:T(2,128)(2,1)}), bf16[8,2,1280,108]{2,1,3,0:T(2,128)(2,1)}, u32[]{:S(2)}, u32[]{:S(2)}) async-start(bf16[8,2,1280,108]{2,1,3,0:T(2,128)(2,1)} %broadcast_in_dim.108), calls=%async_computation | async-start | bytes 8847360 | tf_op jit(solution)/shard_map/all_to_all | solution.py:87
  19.5 6.8 %all-reduce = (f32[256]{0:T(256)S(1)}, f32[256]{0:T(256)S(1)}) all-reduce(f32[256]{0:T(256)S(1)} %fusion.5, f32[256]{0:T(256)S(1)} %fusion.3), channel_id=1, replica_groups=mesh['ra'=16,'rb'=8,'wt'=4] {'wt'}, use_global_device_ids=true, to_apply=%region_5.6 | all-reduce | flops 512 | bytes 4096 | tf_op jit(solution)/shard_map/psum | solution.py:93
  32.2 2.6 %copy.133 = f32[256,10,64]{2,0,1:T(8,128)} copy(f32[256,10,64]{0,2,1:T(8,128)} %get-tuple-element.28) | data formatting | bytes 1310720
  46.1 2.7 %fusion.45 = (f32[10,256]{1,0:T(8,128)S(1)}, f32[10,256,256]{1,2,0:T(8,128)}) fusion(pred[256,256]{0,1:T(8,128)(4,1)S(1)} %fusion.18, bf16[256,10,128]{2,0,1:T(8,128)(2,1)S(1)} %maximum_convert_fusion, bf16[256,10,64]{2,0,1:T(8,128)(2,1)S(1)} %get-tuple-element.25, bf16[256,10,64]{2,0,1:T(8,128)(2,1)S(1)} %get-tuple-element.24), kind=kOutput, calls=%fused_computation.111 | convolution fusion | flops 171704576 | bytes 4007936 | tf_op jit(solution)/shard_map/sub | solution.py:112
  48.8 2.1 convolution_convert_fusion.1
  50.9 18.5 %all-to-all-done = bf16[8,2,1280,108]{2,1,3,0:T(2,128)(2,1)} async-done(((bf16[8,2,1280,108]{2,1,3,0:T(2,128)(2,1)}), bf16[8,2,1280,108]{2,1,3,0:T(2,128)(2,1)}, u32[]{:S(2)}, u32[]{:S(2)}) %all-to-all-start) | async-done | bytes 4423712 | tf_op jit(solution)/shard_map/all_to_all | solution.py:87
  69.4 4.9 %copy.126 = bf16[2,1280,864]{1,2,0:T(8,128)(2,1)} copy(bf16[2,1280,864]{1,0,2:T(2,128)(2,1)} %bitcast.12) | data formatting | bytes 8847360 | tf_op jit(solution)/shard_map/reshape | solution.py:90
  74.7 6.2 %psum.23 = f32[256]{0:T(256)S(1)} all-reduce(f32[256]{0:T(256)S(1)} %fusion.7), channel_id=1, replica_groups=mesh['ra'=16,'rb'=8,'wt'=4] {'wt'}, use_global_device_ids=true, to_apply=%region_9.10 | all-reduce | flops 256 | bytes 2048 | tf_op jit(solution)/shard_map/psum | solution.py:121
  84.3 17.0 %all-to-all-start.1 = ((bf16[128,2,1280]{2,1,0:T(2,128)(2,1)}), bf16[128,2,1280]{2,1,0:T(2,128)(2,1)S(1)}, u32[]{:S(2)}, u32[]{:S(2)}) async-start(bf16[128,2,1280]{2,1,0:T(2,128)(2,1)} %broadcast_select_fusion), calls=%async_computation.1 | async-start | bytes 1310720 | tf_op jit(solution)/shard_map/all_to_all | solution.py:49
  102.0 35.8 %all-to-all-done.1 = bf16[128,2,1280]{2,1,0:T(2,128)(2,1)S(1)} async-done(((bf16[128,2,1280]{2,1,0:T(2,128)(2,1)}), bf16[128,2,1280]{2,1,0:T(2,128)(2,1)S(1)}, u32[]{:S(2)}, u32[]{:S(2)}) %all-to-all-start.1) | async-done | bytes 655392 | tf_op jit(solution)/shard_map/all_to_all | solution.py:49
  139.6 6.0 %collective-permute-start = (bf16[36,1280]{1,0:T(8,128)(2,1)S(1)}, bf16[36,1280]{1,0:T(8,128)(2,1)S(1)}, u32[]{:S(2)}, u32[]{:S(2)}) collective-permute-start(bf16[36,1280]{1,0:T(8,128)(2,1)S(1)} %scatter_custom_fusion.1), channel_id=1, source_target_pairs={{0,32},{32,64},{64,96},{96,128},{128,160},{160,192},{192,224},{224... | collective-permute-start | bytes 276488 | tf_op jit(solution)/shard_map/ppermute | solution.py:143
  145.6 1.9 collective-permute-start.8
  147.9 4.1 %collective-permute-start.1 = (bf16[36,1280]{1,0:T(8,128)(2,1)S(1)}, bf16[36,1280]{1,0:T(8,128)(2,1)S(1)}, u32[]{:S(2)}, u32[]{:S(2)}) collective-permute-start(bf16[36,1280]{1,0:T(8,128)(2,1)S(1)} %collective-permute-done), channel_id=1, source_target_pairs={{0,32},{32,64},{64,96},{96,128},{128,160},{160,192},{192,224},{224... | collective-permute-start | bytes 276488 | tf_op jit(solution)/shard_map/ppermute | solution.py:143
  152.0 3.1 %collective-permute-start.9 = (bf16[36,1280]{1,0:T(8,128)(2,1)S(1)}, bf16[36,1280]{1,0:T(8,128)(2,1)S(1)}, u32[]{:S(2)}, u32[]{:S(2)}) collective-permute-start(bf16[36,1280]{1,0:T(8,128)(2,1)S(1)} %collective-permute-done.8), channel_id=1, source_target_pairs={{0,480},{32,0},{64,32},{96,64},{128,96},{160,128},{192,160},{224,1... | collective-permute-start | bytes 276488 | tf_op jit(solution)/shard_map/ppermute | solution.py:146
  155.1 2.2 collective-permute-start.2
  157.4 4.3 %collective-permute-start.10 = (bf16[36,1280]{1,0:T(8,128)(2,1)S(1)}, bf16[36,1280]{1,0:T(8,128)(2,1)S(1)}, u32[]{:S(2)}, u32[]{:S(2)}) collective-permute-start(bf16[36,1280]{1,0:T(8,128)(2,1)S(1)} %collective-permute-done.9), channel_id=1, source_target_pairs={{0,480},{32,0},{64,32},{96,64},{128,96},{160,128},{192,160},{224,1... | collective-permute-start | bytes 276488 | tf_op jit(solution)/shard_map/ppermute | solution.py:146
  161.8 1.9 collective-permute-start.3
  163.7 4.6 %collective-permute-start.11 = (bf16[36,1280]{1,0:T(8,128)(2,1)S(1)}, bf16[36,1280]{1,0:T(8,128)(2,1)S(1)}, u32[]{:S(2)}, u32[]{:S(2)}) collective-permute-start(bf16[36,1280]{1,0:T(8,128)(2,1)S(1)} %collective-permute-done.10), channel_id=1, source_target_pairs={{0,480},{32,0},{64,32},{96,64},{128,96},{160,128},{192,160},{224,1... | collective-permute-start | bytes 276488 | tf_op jit(solution)/shard_map/ppermute | solution.py:146
  170.3 4.6 %collective-permute-start.12 = (bf16[36,1280]{1,0:T(8,128)(2,1)S(1)}, bf16[36,1280]{1,0:T(8,128)(2,1)S(1)}, u32[]{:S(2)}, u32[]{:S(2)}) collective-permute-start(bf16[36,1280]{1,0:T(8,128)(2,1)S(1)} %collective-permute-done.11), channel_id=1, source_target_pairs={{0,480},{32,0},{64,32},{96,64},{128,96},{160,128},{192,160},{224,1... | collective-permute-start | bytes 276488 | tf_op jit(solution)/shard_map/ppermute | solution.py:146
  176.9 4.6 %collective-permute-start.13 = (bf16[36,1280]{1,0:T(8,128)(2,1)S(1)}, bf16[36,1280]{1,0:T(8,128)(2,1)S(1)}, u32[]{:S(2)}, u32[]{:S(2)}) collective-permute-start(bf16[36,1280]{1,0:T(8,128)(2,1)S(1)} %collective-permute-done.12), channel_id=1, source_target_pairs={{0,480},{32,0},{64,32},{96,64},{128,96},{160,128},{192,160},{224,1... | collective-permute-start | bytes 276488 | tf_op jit(solution)/shard_map/ppermute | solution.py:146
  183.5 4.6 %collective-permute-start.14 = (bf16[36,1280]{1,0:T(8,128)(2,1)S(1)}, bf16[36,1280]{1,0:T(8,128)(2,1)S(1)}, u32[]{:S(2)}, u32[]{:S(2)}) collective-permute-start(bf16[36,1280]{1,0:T(8,128)(2,1)S(1)} %collective-permute-done.13), channel_id=1, source_target_pairs={{0,480},{32,0},{64,32},{96,64},{128,96},{160,128},{192,160},{224,1... | collective-permute-start | bytes 276488 | tf_op jit(solution)/shard_map/ppermute | solution.py:146
  188.2 2.1 collective-permute-start.7
  190.3 5.3 %collective-permute-done.7 = bf16[36,1280]{1,0:T(8,128)(2,1)S(1)} collective-permute-done((bf16[36,1280]{1,0:T(8,128)(2,1)S(1)}, bf16[36,1280]{1,0:T(8,128)(2,1)S(1)}, u32[]{:S(2)}, u32[]{:S(2)}) %collective-permute-start.7) | collective-permute-done | bytes 92192 | tf_op jit(solution)/shard_map/ppermute | solution.py:143
  197.2 5.4 %convolution_convert_fusion = bf16[576,2,864]{2,0,1:T(8,128)(2,1)S(1)} fusion(bf16[2,1280,864]{1,2,0:T(8,128)(2,1)} %copy.126, bf16[576,1280]{1,0:T(8,128)(2,1)S(1)} %concatenate.12), kind=kOutput, calls=%fused_computation.14 | convolution fusion | flops 2549035008 | bytes 7888896 | tf_op jit(solution)/shard_map/tk,skn->tsn/dot_general | solution.py:149
  202.6 2.1 copy.113
  204.7 2.7 %copy.114 = bf16[16,4,9,2,864]{4,3,2,0,1:T(2,128)(2,1)} copy(bf16[16,4,9,2,864]{4,3,2,1,0:T(2,128)(2,1)S(1)} %bitcast.45) | data formatting | bytes 3981312 | tf_op jit(solution)/shard_map/reshape | solution.py:151
  207.4 3.6 %all-to-all-start.2 = ((bf16[16,4,9,2,864]{4,3,2,0,1:T(2,128)(2,1)}), bf16[16,4,9,2,864]{4,3,2,0,1:T(2,128)(2,1)S(1)}, u32[]{:S(2)}, u32[]{:S(2)}) async-start(bf16[16,4,9,2,864]{4,3,2,0,1:T(2,128)(2,1)} %copy.114), calls=%async_computation.2 | async-start | bytes 4128768 | tf_op jit(solution)/shard_map/all_to_all | solution.py:152
  216.7 2.5 scatter_fusion
  220.1 8.5 %all-to-all-done.2 = bf16[16,4,9,2,864]{4,3,2,0,1:T(2,128)(2,1)S(1)} async-done(((bf16[16,4,9,2,864]{4,3,2,0,1:T(2,128)(2,1)}), bf16[16,4,9,2,864]{4,3,2,0,1:T(2,128)(2,1)S(1)}, u32[]{:S(2)}, u32[]{:S(2)}) %all-to-all-start.2) | async-done | bytes 1990688 | tf_op jit(solution)/shard_map/all_to_all | solution.py:152
  230.5 14.3 %all-to-all-start.3 = ((bf16[16,9,8,108]{3,0,1,2:T(8,128)(2,1)}), bf16[16,9,8,108]{3,0,1,2:T(8,128)(2,1)S(1)}, u32[]{:S(2)}, u32[]{:S(2)}) async-start(bf16[16,9,8,108]{3,0,1,2:T(8,128)(2,1)} %copy.119), calls=%async_computation.3 | async-start | bytes 589824 | tf_op jit(solution)/shard_map/all_to_all | solution.py:157
  244.8 6.8 %all-to-all-done.3 = bf16[16,9,8,108]{3,0,1,2:T(8,128)(2,1)S(1)} async-done(((bf16[16,9,8,108]{3,0,1,2:T(8,128)(2,1)}), bf16[16,9,8,108]{3,0,1,2:T(8,128)(2,1)S(1)}, u32[]{:S(2)}, u32[]{:S(2)}) %all-to-all-start.3) | async-done | bytes 248864 | tf_op jit(solution)/shard_map/all_to_all | solution.py:157
  (129 shorter events, 44.1 us)
Async XLA Ops:
  6.5 11.5 %copy-start.8 = (bf16[256,1280]{1,0:T(8,128)(2,1)S(1)}, bf16[256,1280]{1,0:T(8,128)(2,1)}, u32[]{:S(2)}) copy-start(bf16[256,1280]{1,0:T(8,128)(2,1)} %param.13) | copy-start | bytes 1966084
  6.5 62.8 %all-to-all-start = ((bf16[8,2,1280,108]{2,1,3,0:T(2,128)(2,1)}), bf16[8,2,1280,108]{2,1,3,0:T(2,128)(2,1)}, u32[]{:S(2)}, u32[]{:S(2)}) async-start(bf16[8,2,1280,108]{2,1,3,0:T(2,128)(2,1)} %broadcast_in_dim.108), calls=%async_computation | async-start | bytes 8847360 | tf_op jit(solution)/shard_map/all_to_all | solution.py:87
  18.2 8.1 %copy-start.11 = (f32[1280]{0:T(1024)S(1)}, f32[1280]{0:T(1024)}, u32[]{:S(2)}) copy-start(f32[1280]{0:T(1024)} %param.17) | copy-start | bytes 15364
  28.0 1.5 copy-start.12
  32.2 2.6 %copy-start.3 = (bf16[256,1280]{1,0:T(8,128)(2,1)S(1)}, bf16[256,1280]{1,0:T(8,128)(2,1)}, u32[]{:S(2)}) copy-start(bf16[256,1280]{1,0:T(8,128)(2,1)} %param.15) | copy-start | bytes 1966084
  32.2 3.7 %copy-start.14 = (s32[128]{0:T(128)S(1)}, s32[128]{0:T(128)}, u32[]{:S(2)}) copy-start(s32[128]{0:T(128)} %param.22) | copy-start | bytes 1540
  32.2 4.7 %copy-start = (s32[128]{0:T(128)S(1)}, s32[128]{0:T(128)}, u32[]{:S(2)}) copy-start(s32[128]{0:T(128)} %param.21) | copy-start | bytes 1540
  44.3 1.4 copy-start.1
  46.1 2.7 %copy-start.10 = (bf16[256,1280]{0,1:T(8,128)(2,1)S(1)}, bf16[256,1280]{0,1:T(8,128)(2,1)}, u32[]{:S(2)}) copy-start(bf16[256,1280]{0,1:T(8,128)(2,1)} %copy.108) | copy-start | bytes 1966084
  74.3 6.7 %copy-start.7 = (bf16[256,1280]{1,0:T(8,128)(2,1)S(1)}, bf16[256,1280]{1,0:T(8,128)(2,1)}, u32[]{:S(2)}) copy-start(bf16[256,1280]{1,0:T(8,128)(2,1)} %param.12) | copy-start | bytes 1966084
  74.3 6.7 %copy-start.13 = (f32[1280]{0:T(1024)S(1)}, f32[1280]{0:T(1024)}, u32[]{:S(2)}) copy-start(f32[1280]{0:T(1024)} %param.18) | copy-start | bytes 15364
  84.3 53.5 %all-to-all-start.1 = ((bf16[128,2,1280]{2,1,0:T(2,128)(2,1)}), bf16[128,2,1280]{2,1,0:T(2,128)(2,1)S(1)}, u32[]{:S(2)}, u32[]{:S(2)}) async-start(bf16[128,2,1280]{2,1,0:T(2,128)(2,1)} %broadcast_select_fusion), calls=%async_computation.1 | async-start | bytes 1310720 | tf_op jit(solution)/shard_map/all_to_all | solution.py:49
  139.6 8.3 %collective-permute-start = (bf16[36,1280]{1,0:T(8,128)(2,1)S(1)}, bf16[36,1280]{1,0:T(8,128)(2,1)S(1)}, u32[]{:S(2)}, u32[]{:S(2)}) collective-permute-start(bf16[36,1280]{1,0:T(8,128)(2,1)S(1)} %scatter_custom_fusion.1), channel_id=1, source_target_pairs={{0,32},{32,64},{64,96},{96,128},{128,160},{160,192},{192,224},{224... | collective-permute-start | bytes 276488 | tf_op jit(solution)/shard_map/ppermute | solution.py:143
  145.6 6.4 %collective-permute-start.8 = (bf16[36,1280]{1,0:T(8,128)(2,1)S(1)}, bf16[36,1280]{1,0:T(8,128)(2,1)S(1)}, u32[]{:S(2)}, u32[]{:S(2)}) collective-permute-start(bf16[36,1280]{1,0:T(8,128)(2,1)S(1)} %scatter_custom_fusion.1), channel_id=1, source_target_pairs={{0,480},{32,0},{64,32},{96,64},{128,96},{160,128},{192,160},{224,1... | collective-permute-start | bytes 276488 | tf_op jit(solution)/shard_map/ppermute | solution.py:146
  147.9 7.2 %collective-permute-start.1 = (bf16[36,1280]{1,0:T(8,128)(2,1)S(1)}, bf16[36,1280]{1,0:T(8,128)(2,1)S(1)}, u32[]{:S(2)}, u32[]{:S(2)}) collective-permute-start(bf16[36,1280]{1,0:T(8,128)(2,1)S(1)} %collective-permute-done), channel_id=1, source_target_pairs={{0,32},{32,64},{64,96},{96,128},{128,160},{160,192},{192,224},{224... | collective-permute-start | bytes 276488 | tf_op jit(solution)/shard_map/ppermute | solution.py:143
  152.0 5.4 %collective-permute-start.9 = (bf16[36,1280]{1,0:T(8,128)(2,1)S(1)}, bf16[36,1280]{1,0:T(8,128)(2,1)S(1)}, u32[]{:S(2)}, u32[]{:S(2)}) collective-permute-start(bf16[36,1280]{1,0:T(8,128)(2,1)S(1)} %collective-permute-done.8), channel_id=1, source_target_pairs={{0,480},{32,0},{64,32},{96,64},{128,96},{160,128},{192,160},{224,1... | collective-permute-start | bytes 276488 | tf_op jit(solution)/shard_map/ppermute | solution.py:146
  155.1 6.6 %collective-permute-start.2 = (bf16[36,1280]{1,0:T(8,128)(2,1)S(1)}, bf16[36,1280]{1,0:T(8,128)(2,1)S(1)}, u32[]{:S(2)}, u32[]{:S(2)}) collective-permute-start(bf16[36,1280]{1,0:T(8,128)(2,1)S(1)} %collective-permute-done.1), channel_id=1, source_target_pairs={{0,32},{32,64},{64,96},{96,128},{128,160},{160,192},{192,224},{224... | collective-permute-start | bytes 276488 | tf_op jit(solution)/shard_map/ppermute | solution.py:143
  157.4 6.3 %collective-permute-start.10 = (bf16[36,1280]{1,0:T(8,128)(2,1)S(1)}, bf16[36,1280]{1,0:T(8,128)(2,1)S(1)}, u32[]{:S(2)}, u32[]{:S(2)}) collective-permute-start(bf16[36,1280]{1,0:T(8,128)(2,1)S(1)} %collective-permute-done.9), channel_id=1, source_target_pairs={{0,480},{32,0},{64,32},{96,64},{128,96},{160,128},{192,160},{224,1... | collective-permute-start | bytes 276488 | tf_op jit(solution)/shard_map/ppermute | solution.py:146
  161.8 6.6 %collective-permute-start.3 = (bf16[36,1280]{1,0:T(8,128)(2,1)S(1)}, bf16[36,1280]{1,0:T(8,128)(2,1)S(1)}, u32[]{:S(2)}, u32[]{:S(2)}) collective-permute-start(bf16[36,1280]{1,0:T(8,128)(2,1)S(1)} %collective-permute-done.2), channel_id=1, source_target_pairs={{0,32},{32,64},{64,96},{96,128},{128,160},{160,192},{192,224},{224... | collective-permute-start | bytes 276488 | tf_op jit(solution)/shard_map/ppermute | solution.py:143
  163.7 6.6 %collective-permute-start.11 = (bf16[36,1280]{1,0:T(8,128)(2,1)S(1)}, bf16[36,1280]{1,0:T(8,128)(2,1)S(1)}, u32[]{:S(2)}, u32[]{:S(2)}) collective-permute-start(bf16[36,1280]{1,0:T(8,128)(2,1)S(1)} %collective-permute-done.10), channel_id=1, source_target_pairs={{0,480},{32,0},{64,32},{96,64},{128,96},{160,128},{192,160},{224,1... | collective-permute-start | bytes 276488 | tf_op jit(solution)/shard_map/ppermute | solution.py:146
  168.4 6.6 %collective-permute-start.4 = (bf16[36,1280]{1,0:T(8,128)(2,1)S(1)}, bf16[36,1280]{1,0:T(8,128)(2,1)S(1)}, u32[]{:S(2)}, u32[]{:S(2)}) collective-permute-start(bf16[36,1280]{1,0:T(8,128)(2,1)S(1)} %collective-permute-done.3), channel_id=1, source_target_pairs={{0,32},{32,64},{64,96},{96,128},{128,160},{160,192},{192,224},{224... | collective-permute-start | bytes 276488 | tf_op jit(solution)/shard_map/ppermute | solution.py:143
  170.3 6.6 %collective-permute-start.12 = (bf16[36,1280]{1,0:T(8,128)(2,1)S(1)}, bf16[36,1280]{1,0:T(8,128)(2,1)S(1)}, u32[]{:S(2)}, u32[]{:S(2)}) collective-permute-start(bf16[36,1280]{1,0:T(8,128)(2,1)S(1)} %collective-permute-done.11), channel_id=1, source_target_pairs={{0,480},{32,0},{64,32},{96,64},{128,96},{160,128},{192,160},{224,1... | collective-permute-start | bytes 276488 | tf_op jit(solution)/shard_map/ppermute | solution.py:146
  175.0 6.6 %collective-permute-start.5 = (bf16[36,1280]{1,0:T(8,128)(2,1)S(1)}, bf16[36,1280]{1,0:T(8,128)(2,1)S(1)}, u32[]{:S(2)}, u32[]{:S(2)}) collective-permute-start(bf16[36,1280]{1,0:T(8,128)(2,1)S(1)} %collective-permute-done.4), channel_id=1, source_target_pairs={{0,32},{32,64},{64,96},{96,128},{128,160},{160,192},{192,224},{224... | collective-permute-start | bytes 276488 | tf_op jit(solution)/shard_map/ppermute | solution.py:143
  176.9 6.6 %collective-permute-start.13 = (bf16[36,1280]{1,0:T(8,128)(2,1)S(1)}, bf16[36,1280]{1,0:T(8,128)(2,1)S(1)}, u32[]{:S(2)}, u32[]{:S(2)}) collective-permute-start(bf16[36,1280]{1,0:T(8,128)(2,1)S(1)} %collective-permute-done.12), channel_id=1, source_target_pairs={{0,480},{32,0},{64,32},{96,64},{128,96},{160,128},{192,160},{224,1... | collective-permute-start | bytes 276488 | tf_op jit(solution)/shard_map/ppermute | solution.py:146
  181.6 6.6 %collective-permute-start.6 = (bf16[36,1280]{1,0:T(8,128)(2,1)S(1)}, bf16[36,1280]{1,0:T(8,128)(2,1)S(1)}, u32[]{:S(2)}, u32[]{:S(2)}) collective-permute-start(bf16[36,1280]{1,0:T(8,128)(2,1)S(1)} %collective-permute-done.5), channel_id=1, source_target_pairs={{0,32},{32,64},{64,96},{96,128},{128,160},{160,192},{192,224},{224... | collective-permute-start | bytes 276488 | tf_op jit(solution)/shard_map/ppermute | solution.py:143
  183.5 6.8 %collective-permute-start.14 = (bf16[36,1280]{1,0:T(8,128)(2,1)S(1)}, bf16[36,1280]{1,0:T(8,128)(2,1)S(1)}, u32[]{:S(2)}, u32[]{:S(2)}) collective-permute-start(bf16[36,1280]{1,0:T(8,128)(2,1)S(1)} %collective-permute-done.13), channel_id=1, source_target_pairs={{0,480},{32,0},{64,32},{96,64},{128,96},{160,128},{192,160},{224,1... | collective-permute-start | bytes 276488 | tf_op jit(solution)/shard_map/ppermute | solution.py:146
  188.2 7.5 %collective-permute-start.7 = (bf16[36,1280]{1,0:T(8,128)(2,1)S(1)}, bf16[36,1280]{1,0:T(8,128)(2,1)S(1)}, u32[]{:S(2)}, u32[]{:S(2)}) collective-permute-start(bf16[36,1280]{1,0:T(8,128)(2,1)S(1)} %collective-permute-done.6), channel_id=1, source_target_pairs={{0,32},{32,64},{64,96},{96,128},{128,160},{160,192},{192,224},{224... | collective-permute-start | bytes 276488 | tf_op jit(solution)/shard_map/ppermute | solution.py:143
  207.4 21.1 %all-to-all-start.2 = ((bf16[16,4,9,2,864]{4,3,2,0,1:T(2,128)(2,1)}), bf16[16,4,9,2,864]{4,3,2,0,1:T(2,128)(2,1)S(1)}, u32[]{:S(2)}, u32[]{:S(2)}) async-start(bf16[16,4,9,2,864]{4,3,2,0,1:T(2,128)(2,1)} %copy.114), calls=%async_computation.2 | async-start | bytes 4128768 | tf_op jit(solution)/shard_map/all_to_all | solution.py:152
  211.1 3.5 %copy-start.15 = (s32[1,2]{1,0:T(1,128)S(1)}, s32[1,2]{1,0:T(1,128)}, u32[]{:S(2)}) copy-start(s32[1,2]{1,0:T(1,128)} %param.23) | copy-start | bytes 28
  215.8 3.4 %copy-start.4 = (bf16[256,1280]{1,0:T(8,128)(2,1)S(1)}, bf16[256,1280]{1,0:T(8,128)(2,1)}, u32[]{:S(2)}) copy-start(bf16[256,1280]{1,0:T(8,128)(2,1)} %param.15) | copy-start | bytes 1966084
  220.1 8.8 %copy-start.5 = (bf16[2,128,1280]{2,1,0:T(8,128)(2,1)}, bf16[2,128,1280]{2,1,0:T(8,128)(2,1)S(1)}, u32[]{:S(2)}) copy-start(bf16[2,128,1280]{2,1,0:T(8,128)(2,1)S(1)} %scatter_fusion.1) | copy-start | bytes 1966084
  230.5 21.1 %all-to-all-start.3 = ((bf16[16,9,8,108]{3,0,1,2:T(8,128)(2,1)}), bf16[16,9,8,108]{3,0,1,2:T(8,128)(2,1)S(1)}, u32[]{:S(2)}, u32[]{:S(2)}) async-start(bf16[16,9,8,108]{3,0,1,2:T(8,128)(2,1)} %copy.119), calls=%async_computation.3 | async-start | bytes 589824 | tf_op jit(solution)/shard_map/all_to_all | solution.py:157
  (3 other events, 3.8 us)

commit v6 on v4

--- a/solution.py
+++ b/solution.py
@@ -146,7 +146,7 @@
 
 
 def solution(mesh):
-    inner = 8
+    inner = 16
     outer = mesh.shape["req"] // inner
     split = Mesh(mesh.devices.reshape(outer, inner, mesh.shape["wt"]), ("ra", "rb", "wt"))
     req = ("ra", "rb")

time: 238 us -> 209 us (0.88)
  waiting for transfers between devices: 107 us -> 58.6 us
  blocking collectives: 16.1 us -> 44 us
  starting transfers between devices: 43.1 us -> 37 us
  local copies, waits for them, and re-layouts: 36.4 us -> 33.6 us
    all_gather x1 -> x0, waiting for transfers between devices: 55.6 us -> none  [per_device(): piece = lax.all_gather(regrouped, 'ra', axis=0, tiled=True)]
    all_gather x0 -> x1, blocking collectives: none -> 28.7 us  [per_device(): piece = lax.all_gather(regrouped, 'ra', axis=0, tiled=True)]
    all_to_all x1, waiting for transfers between devices: 10.4 us -> 17.6 us  [per_device(): lax.all_to_all(stacked, 'wt', split_axis=1, concat_axis=1, tiled=True)]
    all_to_all x1, starting transfers between devices: 16.2 us -> 9.65 us  [per_device(): gated = lax.all_to_all(gated, 'rb', split_axis=2, concat_axis=2, tiled=True)]
    unnamed x43 -> x45, local copies, waits for them, and re-layouts: 12.6 us -> 9.94 us
  transfers between devices with their start and end apart: 5 -> 4, of which waited for: 4 -> 3; matrix products, arithmetic and copies ran while one was open for 16% -> 17% of each run, Pallas kernels for 0% -> 0%
where the time goes in v6:
time: 209 us; the launch traced here: 208 us
  waiting for transfers between devices  58.6 us (28%)
  blocking collectives  44 us (21%)
  starting transfers between devices  37 us (18%)
  local copies, waits for them, and re-layouts  33.6 us (16%)
  between operations  14.6 us (7%)
  matrix products  11.3 us (5%)
  other arithmetic  9.31 us (4%)
    all_to_all x1, waiting for transfers between devices, deal_rows(): lax.all_to_all(picked, ('ra', 'rb'), split_axis=0, concat_axis=0, tiled=T...  35.8 us
    all_gather x1, blocking collectives, per_device(): piece = lax.all_gather(regrouped, 'ra', axis=0, tiled=True)  28.7 us
    all_to_all x1, starting transfers between devices, deal_rows(): lax.all_to_all(picked, ('ra', 'rb'), split_axis=0, concat_axis=0, tiled=T...  23.7 us
    all_to_all x1, waiting for transfers between devices, per_device(): lax.all_to_all(stacked, 'wt', split_axis=1, concat_axis=1, tiled=True)  17.6 us
    unnamed x45, local copies, waits for them, and re-layouts  9.94 us
    all_to_all x1, starting transfers between devices, per_device(): gated = lax.all_to_all(gated, 'rb', split_axis=2, concat_axis=2, tiled=True)  9.65 us
    psum x1, blocking collectives, per_device(): lax.psum((jnp.sum(query_f * query_f, axis=1), jnp.sum(key_f * key_f, axis...  9.31 us
    dot_general x1, matrix products, per_device(): jnp.einsum('tk,skn->tsn', piece, weights, preferred_element_type=jnp.floa...  6.38 us
  transfers between devices with their start and end apart: 4, of which 3 were waited for; matrix products, arithmetic and copies ran while one was open for 17% of the time, Pallas kernels for 0%

profile of v6, /device:TPU:1, one launch (start us, length us, event | category | flops | bytes accessed | tf_op | source)
XLA Modules:
  0.0 208.4 jit_solution(2233329357819239836)
XLA Ops:
  7.2 1.2 pad_maximum_fusion
  8.4 1.2 copy.89
  10.6 9.3 %all-reduce = (f32[256]{0:T(256)S(1)}, f32[256]{0:T(256)S(1)}) all-reduce(f32[256]{0:T(256)S(1)} %fusion.10, f32[256]{0:T(256)S(1)} %fusion.8), channel_id=1, replica_groups=mesh['ra'=8,'rb'=16,'wt'=4] {'wt'}, use_global_device_ids=true, to_apply=%region_5.6 | all-reduce | flops 512 | bytes 4096 | tf_op jit(solution)/shard_map/psum | solution.py:88
  20.1 1.0 fusion.42
  21.5 1.5 copy.111
  23.3 0.9 fusion.41
  24.2 1.5 copy.108
  25.7 2.6 %copy.109 = f32[256,10,64]{2,0,1:T(8,128)} copy(f32[256,10,64]{0,2,1:T(8,128)} %get-tuple-element.25) | data formatting | bytes 1310720
  28.4 1.1 copy.86
  29.5 1.0 scatter_custom_fusion
  30.5 1.2 gather_fusion.1
  35.7 2.7 %fusion.43 = (f32[10,256]{1,0:T(8,128)S(1)}, f32[10,256,256]{1,2,0:T(8,128)}) fusion(pred[256,256]{0,1:T(8,128)(4,1)S(1)} %fusion.19, bf16[256,10,128]{2,0,1:T(8,128)(2,1)S(1)} %maximum_convert_fusion, bf16[256,10,64]{2,0,1:T(8,128)(2,1)S(1)} %get-tuple-element.22, bf16[256,10,64]{2,0,1:T(8,128)(2,1)S(1)} %get-tuple-element.21), kind=kOutput, calls=%fused_computation.93 | convolution fusion | flops 171704576 | bytes 4007936 | tf_op jit(solution)/shard_map/sub | solution.py:107
  38.4 2.2 %multiply_reduce_fusion = (f32[256]{0:T(256)S(1)}, f32[10,256,128]{1,2,0:T(8,128)S(1)}) fusion(bf16[256,10,128]{0,2,1:T(8,128)(2,1)S(1)} %bitcast.42, f32[10,256,256]{1,2,0:T(8,128)} %get-tuple-element.36, f32[10,256]{1,0:T(8,128)S(1)} %get-tuple-element.35), kind=kOutput, calls=%fused_computation.28 | convolution fusion | flops 170393344 | bytes 4598784 | tf_op jit(solution)/shard_map/hqk,khd->qhd/dot_general | solution.py:110
  41.5 1.2 gather_fusion
  44.2 6.0 %psum.23 = f32[256]{0:T(256)S(1)} all-reduce(f32[256]{0:T(256)S(1)} %get-tuple-element.37), channel_id=1, replica_groups=mesh['ra'=8,'rb'=16,'wt'=4] {'wt'}, use_global_device_ids=true, to_apply=%region_9.10 | all-reduce | flops 256 | bytes 2048 | tf_op jit(solution)/shard_map/psum | solution.py:115
  50.5 1.2 gather_fusion.2
  52.9 1.5 broadcast_select_fusion
  54.4 23.7 %all-to-all-start = ((bf16[128,2,1280]{2,1,0:T(2,128)(2,1)}), bf16[128,2,1280]{2,1,0:T(2,128)(2,1)S(1)}, u32[]{:S(2)}, u32[]{:S(2)}) async-start(bf16[128,2,1280]{2,1,0:T(2,128)(2,1)} %broadcast_select_fusion), calls=%async_computation | async-start | bytes 1310720 | tf_op jit(solution)/shard_map/all_to_all | solution.py:49
  78.7 35.8 %all-to-all-done = bf16[128,2,1280]{2,1,0:T(2,128)(2,1)S(1)} async-done(((bf16[128,2,1280]{2,1,0:T(2,128)(2,1)}), bf16[128,2,1280]{2,1,0:T(2,128)(2,1)S(1)}, u32[]{:S(2)}, u32[]{:S(2)}) %all-to-all-start) | async-done | bytes 655392 | tf_op jit(solution)/shard_map/all_to_all | solution.py:49
  114.8 1.6 scatter_custom_fusion.1
  116.4 28.7 %all-gather = bf16[8,36,1280]{2,1,0:T(8,128)(2,1)S(1)} all-gather(bf16[1,36,1280]{2,1,0:T(8,128)(2,1)S(1)} %bitcast.43), channel_id=1, replica_groups=mesh['ra'=8,'rb'=16,'wt'=4] {'ra'}, dimensions={0}, use_global_device_ids=true | all-gather | bytes 829440 | tf_op jit(solution)/shard_map/all_gather | solution.py:134
  145.2 6.4 %fusion.3 = bf16[288,2,1728]{2,0,1:T(8,128)(2,1)S(1)} fusion(bf16[288,1280,1]{1,0,2:T(8,128)(2,1)S(1)} %reshape.493, bf16[2,1280,1728]{1,0,2:T(2,128)(2,1)} %all-gather.3.cloned.1.call-done), kind=kOutput, calls=%fused_computation.11 | convolution fusion | flops 2549035008 | bytes 11575296 | tf_op jit(solution)/shard_map/tk,skn->tsn/dot_general | solution.py:135
  151.6 2.1 %copy.91 = bf16[288,2,1728]{2,1,0:T(2,128)(2,1)S(1)} copy(bf16[288,2,1728]{2,0,1:T(8,128)(2,1)S(1)} %fusion.3) | data formatting | bytes 3981312 | tf_op jit(solution)/shard_map/convert_element_type | solution.py:137
  153.7 2.8 %copy.92 = bf16[8,4,9,2,1728]{4,3,2,0,1:T(2,128)(2,1)} copy(bf16[8,4,9,2,1728]{4,3,2,1,0:T(2,128)(2,1)S(1)} %bitcast.35) | data formatting | bytes 3981312 | tf_op jit(solution)/shard_map/reshape | solution.py:137
  156.5 3.6 %all-to-all-start.1 = ((bf16[8,4,9,2,1728]{4,3,2,0,1:T(2,128)(2,1)}), bf16[8,4,9,2,1728]{4,3,2,0,1:T(2,128)(2,1)S(1)}, u32[]{:S(2)}, u32[]{:S(2)}) async-start(bf16[8,4,9,2,1728]{4,3,2,0,1:T(2,128)(2,1)} %copy.92), calls=%async_computation.1 | async-start | bytes 4128768 | tf_op jit(solution)/shard_map/all_to_all | solution.py:138
  160.1 1.6 copy.105
  161.7 1.2 reshape.497
  163.6 17.6 %all-to-all-done.1 = bf16[8,4,9,2,1728]{4,3,2,0,1:T(2,128)(2,1)S(1)} async-done(((bf16[8,4,9,2,1728]{4,3,2,0,1:T(2,128)(2,1)}), bf16[8,4,9,2,1728]{4,3,2,0,1:T(2,128)(2,1)S(1)}, u32[]{:S(2)}, u32[]{:S(2)}) %all-to-all-start.1) | async-done | bytes 1990688 | tf_op jit(solution)/shard_map/all_to_all | solution.py:138
  182.8 0.8 copy.97
  183.6 9.7 %all-to-all-start.2 = ((bf16[8,9,16,108]{3,0,1,2:T(8,128)(2,1)}), bf16[8,9,16,108]{3,0,1,2:T(8,128)(2,1)S(1)}, u32[]{:S(2)}, u32[]{:S(2)}) async-start(bf16[8,9,16,108]{3,0,1,2:T(8,128)(2,1)} %copy.97), calls=%async_computation.2 | async-start | bytes 589824 | tf_op jit(solution)/shard_map/all_to_all | solution.py:143
  195.4 5.2 %all-to-all-done.2 = bf16[8,9,16,108]{3,0,1,2:T(8,128)(2,1)S(1)} async-done(((bf16[8,9,16,108]{3,0,1,2:T(8,128)(2,1)}), bf16[8,9,16,108]{3,0,1,2:T(8,128)(2,1)S(1)}, u32[]{:S(2)}, u32[]{:S(2)}) %all-to-all-start.2) | async-done | bytes 248864 | tf_op jit(solution)/shard_map/all_to_all | solution.py:143
  200.7 0.9 copy.101
  (97 shorter events, 14.9 us)
Async XLA Ops:
  7.2 109.2 %all-gather.3.cloned.1.call-start = ((), (), s32[]{:S(2)}) async-start(), calls=%async_computation.3 | async-start | bytes 9400320 | tf_op jit(solution)/shard_map/all_gather | solution.py:85
  7.2 2.4 %copy-start.9 = (bf16[256,1280]{1,0:T(8,128)(2,1)S(1)}, bf16[256,1280]{1,0:T(8,128)(2,1)}, u32[]{:S(2)}) copy-start(bf16[256,1280]{1,0:T(8,128)(2,1)} %param.14) | copy-start | bytes 1966084
  8.4 1.5 copy-start.10
  9.9 10.0 %copy-start.13 = (f32[1280]{0:T(1024)S(1)}, f32[1280]{0:T(1024)}, u32[]{:S(2)}) copy-start(f32[1280]{0:T(1024)} %param.17) | copy-start | bytes 15364
  21.5 1.5 copy-start.14
  25.7 2.6 %copy-start.3 = (bf16[256,1280]{1,0:T(8,128)(2,1)S(1)}, bf16[256,1280]{1,0:T(8,128)(2,1)}, u32[]{:S(2)}) copy-start(bf16[256,1280]{1,0:T(8,128)(2,1)} %param.15) | copy-start | bytes 1966084
  25.7 3.7 %copy-start.16 = (s32[128]{0:T(128)S(1)}, s32[128]{0:T(128)}, u32[]{:S(2)}) copy-start(s32[128]{0:T(128)} %param.22) | copy-start | bytes 1540
  25.7 4.7 %copy-start = (s32[128]{0:T(128)S(1)}, s32[128]{0:T(128)}, u32[]{:S(2)}) copy-start(s32[128]{0:T(128)} %param.21) | copy-start | bytes 1540
  33.5 1.3 copy-start.2
  33.9 1.5 copy-start.1
  34.2 1.4 copy-start.8
  35.7 2.8 %copy-start.11 = (bf16[256,1280]{0,1:T(8,128)(2,1)S(1)}, bf16[256,1280]{0,1:T(8,128)(2,1)}, u32[]{:S(2)}) copy-start(bf16[256,1280]{0,1:T(8,128)(2,1)} %copy.86) | copy-start | bytes 1966084
  40.6 9.6 %copy-start.12 = (bf16[256,1280]{1,0:T(8,128)(2,1)S(1)}, bf16[256,1280]{1,0:T(8,128)(2,1)}, u32[]{:S(2)}) copy-start(bf16[256,1280]{1,0:T(8,128)(2,1)} %param.12) | copy-start | bytes 1966084
  40.6 9.6 %copy-start.15 = (f32[1280]{0:T(1024)S(1)}, f32[1280]{0:T(1024)}, u32[]{:S(2)}) copy-start(f32[1280]{0:T(1024)} %param.18) | copy-start | bytes 15364
  54.4 60.1 %all-to-all-start = ((bf16[128,2,1280]{2,1,0:T(2,128)(2,1)}), bf16[128,2,1280]{2,1,0:T(2,128)(2,1)S(1)}, u32[]{:S(2)}, u32[]{:S(2)}) async-start(bf16[128,2,1280]{2,1,0:T(2,128)(2,1)} %broadcast_select_fusion), calls=%async_computation | async-start | bytes 1310720 | tf_op jit(solution)/shard_map/all_to_all | solution.py:49
  156.5 24.7 %all-to-all-start.1 = ((bf16[8,4,9,2,1728]{4,3,2,0,1:T(2,128)(2,1)}), bf16[8,4,9,2,1728]{4,3,2,0,1:T(2,128)(2,1)S(1)}, u32[]{:S(2)}, u32[]{:S(2)}) async-start(bf16[8,4,9,2,1728]{4,3,2,0,1:T(2,128)(2,1)} %copy.92), calls=%async_computation.1 | async-start | bytes 4128768 | tf_op jit(solution)/shard_map/all_to_all | solution.py:138
  160.1 3.5 %copy-start.17 = (s32[1,2]{1,0:T(1,128)S(1)}, s32[1,2]{1,0:T(1,128)}, u32[]{:S(2)}) copy-start(s32[1,2]{1,0:T(1,128)} %param.23) | copy-start | bytes 28
  182.6 10.6 %copy-start.5 = (bf16[2,128,1280]{2,1,0:T(8,128)(2,1)S(1)}, bf16[2,128,1280]{2,1,0:T(8,128)(2,1)}, u32[]{:S(2)}) copy-start(bf16[2,128,1280]{2,1,0:T(8,128)(2,1)} %reshape.497) | copy-start | bytes 1966084
  183.6 17.0 %all-to-all-start.2 = ((bf16[8,9,16,108]{3,0,1,2:T(8,128)(2,1)}), bf16[8,9,16,108]{3,0,1,2:T(8,128)(2,1)S(1)}, u32[]{:S(2)}, u32[]{:S(2)}) async-start(bf16[8,9,16,108]{3,0,1,2:T(8,128)(2,1)} %copy.97), calls=%async_computation.2 | async-start | bytes 589824 | tf_op jit(solution)/shard_map/all_to_all | solution.py:143
  193.4 1.1 copy-start.4
  194.4 0.9 copy-start.7
  195.4 6.2 %copy-start.6 = (bf16[2,128,1280]{2,1,0:T(8,128)(2,1)}, bf16[2,128,1280]{2,1,0:T(8,128)(2,1)S(1)}, u32[]{:S(2)}) copy-start(bf16[2,128,1280]{2,1,0:T(8,128)(2,1)S(1)} %scatter_fusion.1) | copy-start | bytes 1966084
Sparse Core Ops, SparseCore 0:
  10.1 67.7 all-gather.2

commit v7 on v6

--- a/solution.py
+++ b/solution.py
@@ -82,7 +82,8 @@
     owner_start = starts[owner_req]
     owner_len = lengths[owner_req]
     my_length = owner_len[device]
-    weights = lax.all_gather(jnp.stack([gate_w, up_w]), "rb", axis=2, tiled=True)
+    halves = jnp.stack([gate_w, up_w]).reshape(2, 2, gate_w.shape[0] // 2, gate_w.shape[1])
+    weights = lax.all_gather(halves, "rb", axis=3, tiled=True)
     query_f = queries.astype(jnp.float32)
     key_f = key_proj.astype(jnp.float32)
     query_sq, key_sq = lax.psum(
@@ -127,12 +128,17 @@
     placement = page_table[0]
     key_cache = jnp.zeros_like(key_pages).at[placement].set(key_pages)
     value_cache = jnp.zeros_like(value_pages).at[placement].set(value_pages)
-    regrouped = deal_rows(layer_rows, owner_start, owner_len, device, owners, LIVE)
-    regrouped, weights = lax.optimization_barrier((regrouped, weights))
+    half = feature_count // 2
+    first = deal_rows(layer_rows[:, :half], owner_start, owner_len, device, owners, LIVE)
+    second = deal_rows(layer_rows[:, half:], owner_start, owner_len, device, owners, LIVE)
+    first, weights = lax.optimization_barrier((first, weights))
     outer = lax.axis_size("ra")
     inner = lax.axis_size("rb")
-    piece = lax.all_gather(regrouped, "ra", axis=0, tiled=True)
-    stacked = jnp.einsum("tk,skn->tsn", piece, weights, preferred_element_type=jnp.float32)
+    piece_a = lax.all_gather(first, "ra", axis=0, tiled=True)
+    piece_b = lax.all_gather(second, "ra", axis=0, tiled=True)
+    stacked = jnp.einsum(
+        "tk,skn->tsn", piece_a, weights[:, 0], preferred_element_type=jnp.float32
+    ) + jnp.einsum("tk,skn->tsn", piece_b, weights[:, 1], preferred_element_type=jnp.float32)
     parts = lax.axis_size("wt")
     stacked = stacked.astype(jnp.bfloat16).reshape(outer, parts, LIVE // parts, 2, inner * unit_count)
     stacked = lax.all_to_all(stacked, "wt", split_axis=1, concat_axis=1, tiled=True)

time: 209 us -> 250 us (1.20)
  blocking collectives: 44 us -> 122 us
  waiting for transfers between devices: 58.6 us -> 17.1 us
  local copies, waits for them, and re-layouts: 33.6 us -> 47.1 us
  starting transfers between devices: 37 us -> 28.8 us
    all_to_all x0 -> x1, blocking collectives: none -> 46.4 us  [deal_rows(): lax.all_to_all(picked, ('ra', 'rb'), split_axis=0, concat_axis=0, tiled=T...]
    all_to_all x1, waiting for transfers between devices: 35.8 us -> 0.01 us  [deal_rows(): lax.all_to_all(picked, ('ra', 'rb'), split_axis=0, concat_axis=0, tiled=T...]
    all_gather x1 -> x2, blocking collectives: 28.7 us -> 60 us  [the longest x1 35.9 us: per_device(): piece_b = lax.all_gather(second, 'ra', axis=0, tiled=True)]
    all_to_all x1, starting transfers between devices: 23.7 us -> 8.57 us  [deal_rows(): lax.all_to_all(picked, ('ra', 'rb'), split_axis=0, concat_axis=0, tiled=T...]
    optimization_barrier x0 -> x1, local copies, waits for them, and re-layouts: none -> 8.06 us  [per_device(): first, weights = lax.optimization_barrier((first, weights))]
    all_to_all x1, starting transfers between devices: 9.65 us -> 16.6 us  [per_device(): gated = lax.all_to_all(gated, 'rb', split_axis=2, concat_axis=2, tiled=True)]
    all_to_all x1, waiting for transfers between devices: 17.6 us -> 11.8 us  [per_device(): lax.all_to_all(stacked, 'wt', split_axis=1, concat_axis=1, tiled=True)]
    unnamed x45 -> x48, local copies, waits for them, and re-layouts: 9.94 us -> 10.6 us
  transfers between devices with their start and end apart: 4 -> 4, of which waited for: 3 -> 2; matrix products, arithmetic and copies ran while one was open for 17% -> 15% of each run, Pallas kernels for 0% -> 0%
where the time goes in v7:
time: 250 us; the launch traced here: 249 us
  blocking collectives  122 us (49%)
  local copies, waits for them, and re-layouts  47.1 us (19%)
  starting transfers between devices  28.8 us (12%)
  waiting for transfers between devices  17.1 us (7%)
  between operations  14.7 us (6%)
  matrix products  11 us (4%)
  other arithmetic  8.82 us (4%)
    all_to_all x1, blocking collectives, deal_rows(): lax.all_to_all(picked, ('ra', 'rb'), split_axis=0, concat_axis=0, tiled=T...  46.4 us
    all_gather x1, blocking collectives, per_device(): piece_b = lax.all_gather(second, 'ra', axis=0, tiled=True)  35.9 us
    all_gather x1, blocking collectives, per_device(): piece_a = lax.all_gather(first, 'ra', axis=0, tiled=True)  24.1 us
    all_to_all x1, starting transfers between devices, per_device(): gated = lax.all_to_all(gated, 'rb', split_axis=2, concat_axis=2, tiled=True)  16.6 us
    all_to_all x1, waiting for transfers between devices, per_device(): lax.all_to_all(stacked, 'wt', split_axis=1, concat_axis=1, tiled=True)  11.8 us
    unnamed x48, local copies, waits for them, and re-layouts  10.6 us
    psum x1, blocking collectives, per_device(): lax.psum((jnp.sum(query_f * query_f, axis=1), jnp.sum(key_f * key_f, axis...  9.29 us
    all_to_all x1, starting transfers between devices, deal_rows(): lax.all_to_all(picked, ('ra', 'rb'), split_axis=0, concat_axis=0, tiled=T...  8.57 us
  transfers between devices with their start and end apart: 4, of which 2 were waited for; matrix products, arithmetic and copies ran while one was open for 15% of the time, Pallas kernels for 0%

profile of v7, /device:TPU:1, one launch (start us, length us, event | category | flops | bytes accessed | tf_op | source)
XLA Modules:
  0.0 249.5 jit_solution(14046930214266549376)
XLA Ops:
  8.2 1.0 stack.9
  10.1 1.2 copy.71
  12.2 9.3 %all-reduce = (f32[256]{0:T(256)S(1)}, f32[256]{0:T(256)S(1)}) all-reduce(f32[256]{0:T(256)S(1)} %fusion.7, f32[256]{0:T(256)S(1)} %fusion.5), channel_id=1, replica_groups=mesh['ra'=8,'rb'=16,'wt'=4] {'wt'}, use_global_device_ids=true, to_apply=%region_5.6 | all-reduce | flops 512 | bytes 4096 | tf_op jit(solution)/shard_map/psum | solution.py:89
  23.2 1.5 copy.94
  25.9 1.5 copy.91
  27.4 2.6 %copy.92 = f32[256,10,64]{2,0,1:T(8,128)} copy(f32[256,10,64]{0,2,1:T(8,128)} %get-tuple-element.22) | data formatting | bytes 1310720
  30.0 1.1 copy.68
  32.1 1.2 gather_fusion.1
  37.4 2.7 %fusion.43 = (f32[10,256]{1,0:T(8,128)S(1)}, f32[10,256,256]{1,2,0:T(8,128)}) fusion(pred[256,256]{0,1:T(8,128)(4,1)S(1)} %fusion.16, bf16[256,10,128]{2,0,1:T(8,128)(2,1)S(1)} %maximum_convert_fusion, bf16[256,10,64]{2,0,1:T(8,128)(2,1)S(1)} %get-tuple-element.19, bf16[256,10,64]{2,0,1:T(8,128)(2,1)S(1)} %get-tuple-element.18), kind=kOutput, calls=%fused_computation.101 | convolution fusion | flops 171704576 | bytes 4007936 | tf_op jit(solution)/shard_map/sub | solution.py:108
  40.1 2.2 multiply_reduce_fusion
  43.2 1.2 gather_fusion
  45.9 6.2 %psum.23 = f32[256]{0:T(256)S(1)} all-reduce(f32[256]{0:T(256)S(1)} %get-tuple-element.38), channel_id=1, replica_groups=mesh['ra'=8,'rb'=16,'wt'=4] {'wt'}, use_global_device_ids=true, to_apply=%region_9.10 | all-reduce | flops 256 | bytes 2048 | tf_op jit(solution)/shard_map/psum | solution.py:116
  52.5 1.2 gather_fusion.3
  53.8 1.2 gather_fusion.2
  56.0 1.4 broadcast_select_fusion.3
  57.4 46.4 %all_to_all.20 = bf16[128,2,640]{2,1,0:T(2,128)(2,1)S(1)} all-to-all(bf16[128,2,640]{2,1,0:T(2,128)(2,1)S(1)} %get-tuple-element.31), channel_id=1, replica_groups=mesh['ra'=8,'rb'=16,'wt'=4] {'ra','rb'}, dimensions={0} | all-to-all | bytes 655360 | tf_op jit(solution)/shard_map/all_to_all | solution.py:49
  103.8 8.6 %all-to-all-start = ((bf16[128,2,640]{2,1,0:T(2,128)(2,1)}), bf16[128,2,640]{2,1,0:T(2,128)(2,1)S(1)}, u32[]{:S(2)}, u32[]{:S(2)}) async-start(bf16[128,2,640]{2,1,0:T(2,128)(2,1)} %get-tuple-element.30), calls=%async_computation | async-start | bytes 655360 | tf_op jit(solution)/shard_map/all_to_all | solution.py:49
  113.2 1.6 scatter_custom_fusion.2
  114.8 35.9 %all-gather.1 = bf16[8,36,640]{2,1,0:T(8,128)(2,1)S(1)} all-gather(bf16[1,36,640]{2,1,0:T(8,128)(2,1)S(1)} %bitcast.56), channel_id=1, replica_groups=mesh['ra'=8,'rb'=16,'wt'=4] {'ra'}, dimensions={0}, use_global_device_ids=true | all-gather | bytes 414720 | tf_op jit(solution)/shard_map/all_gather | solution.py:138
  150.9 1.6 scatter_custom_fusion.1
  152.5 8.1 %copy.72 = bf16[2,2,640,1728]{2,3,0,1:T(8,128)(2,1)} copy(bf16[2,2,640,1728]{2,1,0,3:T(2,128)(2,1)} %all-gather.4.cloned.1.call-done) | data formatting | bytes 17694720 | tf_op jit(solution)/shard_map/optimization_barrier | solution.py:134
  160.6 24.1 %all-gather = bf16[8,36,640]{2,1,0:T(8,128)(2,1)S(1)} all-gather(bf16[1,36,640]{2,1,0:T(8,128)(2,1)S(1)} %bitcast.55), channel_id=1, replica_groups=mesh['ra'=8,'rb'=16,'wt'=4] {'ra'}, dimensions={0}, use_global_device_ids=true | all-gather | bytes 414720 | tf_op jit(solution)/shard_map/all_gather | solution.py:137
  184.8 4.2 %fusion.1 = f32[288,2,1728]{2,0,1:T(8,128)S(1)} fusion(bf16[288,640,1]{1,0,2:T(8,128)(2,1)S(1)} %reshape.523, bf16[2,2,640,1728]{2,3,0,1:T(8,128)(2,1)} %copy.72), kind=kOutput, calls=%fused_computation.11 | convolution fusion | flops 1274019840 | bytes 8773632 | tf_op jit(solution)/shard_map/tk,skn->tsn/dot_general | solution.py:141
  189.6 1.8 add_convert_fusion
  191.4 2.1 copy.74
  193.5 2.8 %copy.75 = bf16[8,4,9,2,1728]{4,3,2,0,1:T(2,128)(2,1)} copy(bf16[8,4,9,2,1728]{4,3,2,1,0:T(2,128)(2,1)S(1)} %bitcast.47) | data formatting | bytes 3981312 | tf_op jit(solution)/shard_map/reshape | solution.py:143
  196.3 3.6 %all-to-all-start.2 = ((bf16[8,4,9,2,1728]{4,3,2,0,1:T(2,128)(2,1)}), bf16[8,4,9,2,1728]{4,3,2,0,1:T(2,128)(2,1)S(1)}, u32[]{:S(2)}, u32[]{:S(2)}) async-start(bf16[8,4,9,2,1728]{4,3,2,0,1:T(2,128)(2,1)} %copy.75), calls=%async_computation.2 | async-start | bytes 4128768 | tf_op jit(solution)/shard_map/all_to_all | solution.py:144
  199.9 1.6 copy.88
  201.5 1.2 reshape.528
  203.4 11.8 %all-to-all-done.2 = bf16[8,4,9,2,1728]{4,3,2,0,1:T(2,128)(2,1)S(1)} async-done(((bf16[8,4,9,2,1728]{4,3,2,0,1:T(2,128)(2,1)}), bf16[8,4,9,2,1728]{4,3,2,0,1:T(2,128)(2,1)S(1)}, u32[]{:S(2)}, u32[]{:S(2)}) %all-to-all-start.2) | async-done | bytes 1990688 | tf_op jit(solution)/shard_map/all_to_all | solution.py:144
  217.7 16.6 %all-to-all-start.3 = ((bf16[8,9,16,108]{3,0,1,2:T(8,128)(2,1)}), bf16[8,9,16,108]{3,0,1,2:T(8,128)(2,1)S(1)}, u32[]{:S(2)}, u32[]{:S(2)}) async-start(bf16[8,9,16,108]{3,0,1,2:T(8,128)(2,1)} %copy.80), calls=%async_computation.3 | async-start | bytes 589824 | tf_op jit(solution)/shard_map/all_to_all | solution.py:149
  236.4 5.2 %all-to-all-done.3 = bf16[8,9,16,108]{3,0,1,2:T(8,128)(2,1)S(1)} async-done(((bf16[8,9,16,108]{3,0,1,2:T(8,128)(2,1)}), bf16[8,9,16,108]{3,0,1,2:T(8,128)(2,1)S(1)}, u32[]{:S(2)}, u32[]{:S(2)}) %all-to-all-start.3) | async-done | bytes 248864 | tf_op jit(solution)/shard_map/all_to_all | solution.py:149
  (111 shorter events, 22.0 us)
Async XLA Ops:
  7.2 145.4 %all-gather.4.cloned.1.call-start = ((), (), s32[]{:S(2)}) async-start(), calls=%async_computation.4 | async-start | bytes 9400320 | tf_op jit(solution)/shard_map/all_gather | solution.py:86
  9.3 2.0 copy-start.10
  10.1 1.5 copy-start.11
  11.6 10.0 %copy-start.14 = (f32[1280]{0:T(1024)S(1)}, f32[1280]{0:T(1024)}, u32[]{:S(2)}) copy-start(f32[1280]{0:T(1024)} %param.17) | copy-start | bytes 15364
  23.2 1.5 copy-start.15
  27.4 2.6 %copy-start.4 = (bf16[256,1280]{1,0:T(8,128)(2,1)S(1)}, bf16[256,1280]{1,0:T(8,128)(2,1)}, u32[]{:S(2)}) copy-start(bf16[256,1280]{1,0:T(8,128)(2,1)} %param.15) | copy-start | bytes 1966084
  27.4 3.7 %copy-start.17 = (s32[128]{0:T(128)S(1)}, s32[128]{0:T(128)}, u32[]{:S(2)}) copy-start(s32[128]{0:T(128)} %param.22) | copy-start | bytes 1540
  27.4 4.7 %copy-start = (s32[128]{0:T(128)S(1)}, s32[128]{0:T(128)}, u32[]{:S(2)}) copy-start(s32[128]{0:T(128)} %param.21) | copy-start | bytes 1540
  35.1 1.3 copy-start.3
  35.5 1.5 copy-start.2
  35.9 1.4 copy-start.9
  37.4 2.8 %copy-start.12 = (bf16[256,1280]{0,1:T(8,128)(2,1)S(1)}, bf16[256,1280]{0,1:T(8,128)(2,1)}, u32[]{:S(2)}) copy-start(bf16[256,1280]{0,1:T(8,128)(2,1)} %copy.68) | copy-start | bytes 1966084
  42.3 9.8 %copy-start.13 = (bf16[256,1280]{1,0:T(8,128)(2,1)S(1)}, bf16[256,1280]{1,0:T(8,128)(2,1)}, u32[]{:S(2)}) copy-start(bf16[256,1280]{1,0:T(8,128)(2,1)} %param.12) | copy-start | bytes 1966084
  42.3 9.8 %copy-start.16 = (f32[1280]{0:T(1024)S(1)}, f32[1280]{0:T(1024)}, u32[]{:S(2)}) copy-start(f32[1280]{0:T(1024)} %param.18) | copy-start | bytes 15364
  103.8 46.9 %all-to-all-start = ((bf16[128,2,640]{2,1,0:T(2,128)(2,1)}), bf16[128,2,640]{2,1,0:T(2,128)(2,1)S(1)}, u32[]{:S(2)}, u32[]{:S(2)}) async-start(bf16[128,2,640]{2,1,0:T(2,128)(2,1)} %get-tuple-element.30), calls=%async_computation | async-start | bytes 655360 | tf_op jit(solution)/shard_map/all_to_all | solution.py:49
  184.8 4.8 %copy-start.1 = (bf16[2,2,640,1728]{2,3,0,1:T(8,128)(2,1)S(1)}, bf16[2,2,640,1728]{2,3,0,1:T(8,128)(2,1)}, u32[]{:S(2)}) copy-start(bf16[2,2,640,1728]{2,3,0,1:T(8,128)(2,1)} %copy.72) | copy-start | bytes 26542084
  196.3 18.9 %all-to-all-start.2 = ((bf16[8,4,9,2,1728]{4,3,2,0,1:T(2,128)(2,1)}), bf16[8,4,9,2,1728]{4,3,2,0,1:T(2,128)(2,1)S(1)}, u32[]{:S(2)}, u32[]{:S(2)}) async-start(bf16[8,4,9,2,1728]{4,3,2,0,1:T(2,128)(2,1)} %copy.75), calls=%async_computation.2 | async-start | bytes 4128768 | tf_op jit(solution)/shard_map/all_to_all | solution.py:144
  199.9 3.5 %copy-start.18 = (s32[1,2]{1,0:T(1,128)S(1)}, s32[1,2]{1,0:T(1,128)}, u32[]{:S(2)}) copy-start(s32[1,2]{1,0:T(1,128)} %param.23) | copy-start | bytes 28
  216.7 17.6 %copy-start.6 = (bf16[2,128,1280]{2,1,0:T(8,128)(2,1)S(1)}, bf16[2,128,1280]{2,1,0:T(8,128)(2,1)}, u32[]{:S(2)}) copy-start(bf16[2,128,1280]{2,1,0:T(8,128)(2,1)} %reshape.528) | copy-start | bytes 1966084
  217.7 24.0 %all-to-all-start.3 = ((bf16[8,9,16,108]{3,0,1,2:T(8,128)(2,1)}), bf16[8,9,16,108]{3,0,1,2:T(8,128)(2,1)S(1)}, u32[]{:S(2)}, u32[]{:S(2)}) async-start(bf16[8,9,16,108]{3,0,1,2:T(8,128)(2,1)} %copy.80), calls=%async_computation.3 | async-start | bytes 589824 | tf_op jit(solution)/shard_map/all_to_all | solution.py:149
  234.4 1.1 copy-start.5
  235.5 0.9 copy-start.8
  236.4 6.2 %copy-start.7 = (bf16[2,128,1280]{2,1,0:T(8,128)(2,1)}, bf16[2,128,1280]{2,1,0:T(8,128)(2,1)S(1)}, u32[]{:S(2)}) copy-start(bf16[2,128,1280]{2,1,0:T(8,128)(2,1)S(1)} %scatter_fusion.1) | copy-start | bytes 1966084
Sparse Core Ops, SparseCore 0:
  11.4 67.7 all-gather.3

commit v8 on v6

--- a/solution.py
+++ b/solution.py
@@ -134,14 +134,16 @@
     piece = lax.all_gather(regrouped, "ra", axis=0, tiled=True)
     stacked = jnp.einsum("tk,skn->tsn", piece, weights, preferred_element_type=jnp.float32)
     parts = lax.axis_size("wt")
-    stacked = stacked.astype(jnp.bfloat16).reshape(outer, parts, LIVE // parts, 2, inner * unit_count)
-    stacked = lax.all_to_all(stacked, "wt", split_axis=1, concat_axis=1, tiled=True)
+    rows_here = LIVE // parts
+    stacked = stacked.astype(jnp.bfloat16).reshape(outer, parts, rows_here, 2, inner, unit_count)
+    stacked = jnp.transpose(stacked, (4, 1, 0, 2, 3, 5)).reshape(
+        inner * parts, outer, rows_here, 2, unit_count
+    )
+    stacked = lax.all_to_all(stacked, ("rb", "wt"), split_axis=0, concat_axis=0, tiled=True)
+    stacked = stacked.reshape(inner, parts, outer, rows_here, 2, unit_count)
     summed = jnp.sum(stacked.astype(jnp.float32), axis=1)
-    gated = (jax.nn.silu(summed[:, :, 0]) * summed[:, :, 1]).astype(jnp.bfloat16)
-    rows_here = gated.shape[1]
-    gated = gated.reshape(outer, rows_here, inner, unit_count)
-    gated = lax.all_to_all(gated, "rb", split_axis=2, concat_axis=2, tiled=True)
-    gated = jnp.transpose(gated, (0, 2, 1, 3)).reshape(outer * inner, rows_here, unit_count)
+    gated = (jax.nn.silu(summed[:, :, :, 0]) * summed[:, :, :, 1]).astype(jnp.bfloat16)
+    gated = jnp.transpose(gated, (1, 0, 2, 3)).reshape(outer * inner, rows_here, unit_count)
     return (gated, key_cache, value_cache)
 
 

time: 209 us -> 214 us (1.024)
  local copies, waits for them, and re-layouts: 33.6 us -> 39.2 us
  waiting for transfers between devices: 58.6 us -> 55 us
  other arithmetic: 9.31 us -> 12.4 us
    reshape x1 -> x2, local copies, waits for them, and re-layouts: 2.76 us -> 8.92 us  [per_device(): stacked.astype(jnp.bfloat16)]
    all_to_all x2 -> x1, waiting for transfers between devices: 22.8 us -> 19.2 us  [per_device(): lax.all_to_all(stacked, ('rb', 'wt'), split_axis=0, concat_axis=0, tiled=...]
    convert_element_type x2 -> x0, local copies, waits for them, and re-layouts: 2.9 us -> none  [the longest x1 2.12 us: per_device(): stacked.astype(jnp.bfloat16)]
    all_to_all x2 -> x1, starting transfers between devices: 13.3 us -> 12.1 us  [per_device(): lax.all_to_all(stacked, ('rb', 'wt'), split_axis=0, concat_axis=0, tiled=...]
    unnamed x45 -> x41, local copies, waits for them, and re-layouts: 9.94 us -> 9.64 us
  transfers between devices with their start and end apart: 4 -> 3, of which waited for: 3 -> 2; matrix products, arithmetic and copies ran while one was open for 17% -> 20% of each run, Pallas kernels for 0% -> 0%
where the time goes in v8:
time: 214 us
  waiting for transfers between devices  55 us (26%)
  blocking collectives  44 us (21%)
  local copies, waits for them, and re-layouts  39.2 us (18%)
  starting transfers between devices  35.8 us (17%)
  between operations  14.5 us (7%)
  matrix products  12.7 us (6%)
  other arithmetic  12.4 us (6%)
    all_to_all x1, waiting for transfers between devices, deal_rows(): lax.all_to_all(picked, ('ra', 'rb'), split_axis=0, concat_axis=0, tiled=T...  35.8 us
    all_gather x1, blocking collectives, per_device(): piece = lax.all_gather(regrouped, 'ra', axis=0, tiled=True)  28.7 us
    all_to_all x1, starting transfers between devices, deal_rows(): lax.all_to_all(picked, ('ra', 'rb'), split_axis=0, concat_axis=0, tiled=T...  23.7 us
    all_to_all x1, waiting for transfers between devices, per_device(): lax.all_to_all(stacked, ('rb', 'wt'), split_axis=0, concat_axis=0, tiled=...  19.2 us
    all_to_all x1, starting transfers between devices, per_device(): lax.all_to_all(stacked, ('rb', 'wt'), split_axis=0, concat_axis=0, tiled=...  12.1 us
    unnamed x41, local copies, waits for them, and re-layouts  9.64 us
    psum x1, blocking collectives, per_device(): lax.psum((jnp.sum(query_f * query_f, axis=1), jnp.sum(key_f * key_f, axis...  9.31 us
    reshape x2, local copies, waits for them, and re-layouts, per_device(): stacked.astype(jnp.bfloat16)  8.92 us
  transfers between devices with their start and end apart: 3, of which 2 were waited for; matrix products, arithmetic and copies ran while one was open for 20% of the time, Pallas kernels for 0%

profile of v8, /device:TPU:1, one launch (start us, length us, event | category | flops | bytes accessed | tf_op | source)
XLA Modules:
  0.0 213.5 jit_solution(14915801384528514197)
XLA Ops:
  7.2 1.2 pad_maximum_fusion
  8.4 1.2 copy.81
  10.6 9.3 %all-reduce = (f32[256]{0:T(256)S(1)}, f32[256]{0:T(256)S(1)}) all-reduce(f32[256]{0:T(256)S(1)} %fusion.10, f32[256]{0:T(256)S(1)} %fusion.8), channel_id=1, replica_groups=mesh['ra'=8,'rb'=16,'wt'=4] {'wt'}, use_global_device_ids=true, to_apply=%region_5.6 | all-reduce | flops 512 | bytes 4096 | tf_op jit(solution)/shard_map/psum | solution.py:88
  20.1 1.0 fusion.45
  21.5 1.5 copy.95
  23.3 0.9 fusion.44
  24.2 1.5 copy.92
  25.7 2.6 %copy.93 = f32[256,10,64]{2,0,1:T(8,128)} copy(f32[256,10,64]{0,2,1:T(8,128)} %get-tuple-element.25) | data formatting | bytes 1310720
  28.4 1.1 copy.78
  29.4 1.0 scatter_custom_fusion
  30.5 1.2 gather_fusion.1
  35.7 2.8 %fusion.46 = (f32[10,256]{1,0:T(8,128)S(1)}, f32[10,256,256]{1,2,0:T(8,128)}) fusion(pred[256,256]{0,1:T(8,128)(4,1)S(1)} %fusion.22, bf16[256,10,128]{2,0,1:T(8,128)(2,1)S(1)} %maximum_convert_fusion, bf16[256,10,64]{2,0,1:T(8,128)(2,1)S(1)} %get-tuple-element.22, bf16[256,10,64]{2,0,1:T(8,128)(2,1)S(1)} %get-tuple-element.21), kind=kOutput, calls=%fused_computation.95 | convolution fusion | flops 171704576 | bytes 4007936 | tf_op jit(solution)/shard_map/sub | solution.py:107
  38.5 2.2 %multiply_reduce_fusion = (f32[256]{0:T(256)S(1)}, f32[10,256,128]{1,2,0:T(8,128)S(1)}) fusion(bf16[256,10,128]{0,2,1:T(8,128)(2,1)S(1)} %bitcast.57, f32[10,256,256]{1,2,0:T(8,128)} %get-tuple-element.34, f32[10,256]{1,0:T(8,128)S(1)} %get-tuple-element.33), kind=kOutput, calls=%fused_computation.28 | convolution fusion | flops 170393344 | bytes 4598784 | tf_op jit(solution)/shard_map/hqk,khd->qhd/dot_general | solution.py:110
  41.5 1.2 gather_fusion
  44.2 6.0 %psum.23 = f32[256]{0:T(256)S(1)} all-reduce(f32[256]{0:T(256)S(1)} %get-tuple-element.35), channel_id=1, replica_groups=mesh['ra'=8,'rb'=16,'wt'=4] {'wt'}, use_global_device_ids=true, to_apply=%region_9.10 | all-reduce | flops 256 | bytes 2048 | tf_op jit(solution)/shard_map/psum | solution.py:115
  50.5 1.2 gather_fusion.2
  52.9 1.5 broadcast_select_fusion
  54.4 23.7 %all-to-all-start = ((bf16[128,2,1280]{2,1,0:T(2,128)(2,1)}), bf16[128,2,1280]{2,1,0:T(2,128)(2,1)S(1)}, u32[]{:S(2)}, u32[]{:S(2)}) async-start(bf16[128,2,1280]{2,1,0:T(2,128)(2,1)} %broadcast_select_fusion), calls=%async_computation | async-start | bytes 1310720 | tf_op jit(solution)/shard_map/all_to_all | solution.py:49
  78.7 35.8 %all-to-all-done = bf16[128,2,1280]{2,1,0:T(2,128)(2,1)S(1)} async-done(((bf16[128,2,1280]{2,1,0:T(2,128)(2,1)}), bf16[128,2,1280]{2,1,0:T(2,128)(2,1)S(1)}, u32[]{:S(2)}, u32[]{:S(2)}) %all-to-all-start) | async-done | bytes 655392 | tf_op jit(solution)/shard_map/all_to_all | solution.py:49
  114.8 1.6 scatter_custom_fusion.1
  116.4 28.7 %all-gather = bf16[8,36,1280]{2,1,0:T(8,128)(2,1)S(1)} all-gather(bf16[1,36,1280]{2,1,0:T(8,128)(2,1)S(1)} %bitcast.58), channel_id=1, replica_groups=mesh['ra'=8,'rb'=16,'wt'=4] {'ra'}, dimensions={0}, use_global_device_ids=true | all-gather | bytes 829440 | tf_op jit(solution)/shard_map/all_gather | solution.py:134
  145.2 7.8 %fusion.3 = bf16[288,2,1728]{2,0,1:T(8,128)(2,1)} fusion(bf16[288,1280,1]{1,0,2:T(8,128)(2,1)S(1)} %reshape.498, bf16[2,1280,1728]{1,0,2:T(2,128)(2,1)} %all-gather.3.cloned.1.call-done), kind=kOutput, calls=%fused_computation.11 | convolution fusion | flops 2549035008 | bytes 11575296 | tf_op jit(solution)/shard_map/tk,skn->tsn/dot_general | solution.py:135
  153.0 6.0 %reshape.430 = bf16[8,4,9,2,16,108]{5,4,2,1,0,3:T(8,128)(2,1)S(1)} reshape(bf16[288,2,1728]{2,0,1:T(8,128)(2,1)} %fusion.3) | data formatting | bytes 3981312 | tf_op jit(solution)/shard_map/reshape | solution.py:138
  159.0 2.9 %copy.83 = bf16[8,4,9,2,16,108]{5,0,3,2,1,4:T(8,128)(2,1)} copy(bf16[8,4,9,2,16,108]{5,4,2,1,0,3:T(8,128)(2,1)S(1)} %reshape.430) | data formatting | bytes 3981312 | tf_op jit(solution)/shard_map/reshape | solution.py:138
  161.9 12.1 %all-to-all-start.1 = ((bf16[64,8,9,2,108]{4,1,3,2,0:T(8,128)(2,1)}), bf16[64,8,9,2,108]{4,1,3,2,0:T(8,128)(2,1)S(1)}, u32[]{:S(2)}, u32[]{:S(2)}) async-start(bf16[64,8,9,2,108]{4,1,3,2,0:T(8,128)(2,1)} %bitcast.51), calls=%async_computation.1 | async-start | bytes 4718592 | tf_op jit(solution)/shard_map/all_to_all | solution.py:142
  174.0 1.6 copy.90
  175.6 1.2 reshape.500
  177.5 2.0 broadcast_select_fusion.2
  180.4 2.7 %scatter_fusion = bf16[2,128,1280]{2,1,0:T(8,128)(2,1)} fusion(bf16[2,128,1280]{2,1,0:T(8,128)(2,1)} %broadcast.359.clone, s32[2]{0:T(128)S(1)} %fusion.34, bf16[2,128,1280]{2,1,0:T(8,128)(2,1)} %broadcast_select_fusion.2), kind=kCustom, calls=%fused_computation.5 | custom fusion | bytes 1966088 | tf_op jit(solution)/shard_map/scatter | solution.py:128
  183.1 1.0 broadcast_select_fusion.1
  184.1 1.7 scatter_fusion.1
  185.9 19.2 %all-to-all-done.1 = bf16[64,8,9,2,108]{4,1,3,2,0:T(8,128)(2,1)S(1)} async-done(((bf16[64,8,9,2,108]{4,1,3,2,0:T(8,128)(2,1)}), bf16[64,8,9,2,108]{4,1,3,2,0:T(8,128)(2,1)S(1)}, u32[]{:S(2)}, u32[]{:S(2)}) %all-to-all-start.1) | async-done | bytes 1990688 | tf_op jit(solution)/shard_map/all_to_all | solution.py:142
  (87 shorter events, 13.7 us)
Async XLA Ops:
  7.2 109.2 %all-gather.3.cloned.1.call-start = ((), (), s32[]{:S(2)}) async-start(), calls=%async_computation.2 | async-start | bytes 9400320 | tf_op jit(solution)/shard_map/all_gather | solution.py:85
  7.2 2.4 %copy-start.7 = (bf16[256,1280]{1,0:T(8,128)(2,1)S(1)}, bf16[256,1280]{1,0:T(8,128)(2,1)}, u32[]{:S(2)}) copy-start(bf16[256,1280]{1,0:T(8,128)(2,1)} %param.14) | copy-start | bytes 1966084
  8.4 1.5 copy-start.8
  9.9 10.0 %copy-start.11 = (f32[1280]{0:T(1024)S(1)}, f32[1280]{0:T(1024)}, u32[]{:S(2)}) copy-start(f32[1280]{0:T(1024)} %param.17) | copy-start | bytes 15364
  21.5 1.5 copy-start.12
  25.7 2.6 %copy-start.3 = (bf16[256,1280]{1,0:T(8,128)(2,1)S(1)}, bf16[256,1280]{1,0:T(8,128)(2,1)}, u32[]{:S(2)}) copy-start(bf16[256,1280]{1,0:T(8,128)(2,1)} %param.15) | copy-start | bytes 1966084
  25.7 3.7 %copy-start.14 = (s32[128]{0:T(128)S(1)}, s32[128]{0:T(128)}, u32[]{:S(2)}) copy-start(s32[128]{0:T(128)} %param.22) | copy-start | bytes 1540
  25.7 4.7 %copy-start = (s32[128]{0:T(128)S(1)}, s32[128]{0:T(128)}, u32[]{:S(2)}) copy-start(s32[128]{0:T(128)} %param.21) | copy-start | bytes 1540
  33.5 1.3 copy-start.2
  33.8 1.5 copy-start.1
  34.2 1.4 copy-start.6
  35.7 2.8 %copy-start.9 = (bf16[256,1280]{0,1:T(8,128)(2,1)S(1)}, bf16[256,1280]{0,1:T(8,128)(2,1)}, u32[]{:S(2)}) copy-start(bf16[256,1280]{0,1:T(8,128)(2,1)} %copy.78) | copy-start | bytes 1966084
  40.6 9.6 %copy-start.10 = (bf16[256,1280]{1,0:T(8,128)(2,1)S(1)}, bf16[256,1280]{1,0:T(8,128)(2,1)}, u32[]{:S(2)}) copy-start(bf16[256,1280]{1,0:T(8,128)(2,1)} %param.12) | copy-start | bytes 1966084
  40.7 9.6 %copy-start.13 = (f32[1280]{0:T(1024)S(1)}, f32[1280]{0:T(1024)}, u32[]{:S(2)}) copy-start(f32[1280]{0:T(1024)} %param.18) | copy-start | bytes 15364
  54.4 60.1 %all-to-all-start = ((bf16[128,2,1280]{2,1,0:T(2,128)(2,1)}), bf16[128,2,1280]{2,1,0:T(2,128)(2,1)S(1)}, u32[]{:S(2)}, u32[]{:S(2)}) async-start(bf16[128,2,1280]{2,1,0:T(2,128)(2,1)} %broadcast_select_fusion), calls=%async_computation | async-start | bytes 1310720 | tf_op jit(solution)/shard_map/all_to_all | solution.py:49
  161.9 43.1 %all-to-all-start.1 = ((bf16[64,8,9,2,108]{4,1,3,2,0:T(8,128)(2,1)}), bf16[64,8,9,2,108]{4,1,3,2,0:T(8,128)(2,1)S(1)}, u32[]{:S(2)}, u32[]{:S(2)}) async-start(bf16[64,8,9,2,108]{4,1,3,2,0:T(8,128)(2,1)} %bitcast.51), calls=%async_computation.1 | async-start | bytes 4718592 | tf_op jit(solution)/shard_map/all_to_all | solution.py:142
  174.0 3.5 %copy-start.15 = (s32[1,2]{1,0:T(1,128)S(1)}, s32[1,2]{1,0:T(1,128)}, u32[]{:S(2)}) copy-start(s32[1,2]{1,0:T(1,128)} %param.23) | copy-start | bytes 28
  179.5 3.6 %copy-start.4 = (bf16[256,1280]{1,0:T(8,128)(2,1)S(1)}, bf16[256,1280]{1,0:T(8,128)(2,1)}, u32[]{:S(2)}) copy-start(bf16[256,1280]{1,0:T(8,128)(2,1)} %param.15) | copy-start | bytes 1966084
  185.9 19.7 %copy-start.5 = (bf16[2,128,1280]{2,1,0:T(8,128)(2,1)}, bf16[2,128,1280]{2,1,0:T(8,128)(2,1)S(1)}, u32[]{:S(2)}) copy-start(bf16[2,128,1280]{2,1,0:T(8,128)(2,1)S(1)} %scatter_fusion.1) | copy-start | bytes 1966084
Sparse Core Ops, SparseCore 0:
  10.1 67.7 all-gather.2

commit v9 on v6

--- a/solution.py
+++ b/solution.py
@@ -132,11 +132,11 @@
     outer = lax.axis_size("ra")
     inner = lax.axis_size("rb")
     piece = lax.all_gather(regrouped, "ra", axis=0, tiled=True)
-    stacked = jnp.einsum("tk,skn->tsn", piece, weights, preferred_element_type=jnp.float32)
     parts = lax.axis_size("wt")
-    stacked = stacked.astype(jnp.bfloat16).reshape(outer, parts, LIVE // parts, 2, inner * unit_count)
-    stacked = lax.all_to_all(stacked, "wt", split_axis=1, concat_axis=1, tiled=True)
-    summed = jnp.sum(stacked.astype(jnp.float32), axis=1)
+    piece = jnp.transpose(piece.reshape(outer, parts, LIVE // parts, feature_count), (1, 0, 2, 3))
+    stacked = jnp.einsum("wrtk,skn->wrtsn", piece, weights, preferred_element_type=jnp.float32)
+    stacked = lax.all_to_all(stacked.astype(jnp.bfloat16), "wt", split_axis=0, concat_axis=0, tiled=True)
+    summed = jnp.sum(stacked.astype(jnp.float32), axis=0)
     gated = (jax.nn.silu(summed[:, :, 0]) * summed[:, :, 1]).astype(jnp.bfloat16)
     rows_here = gated.shape[1]
     gated = gated.reshape(outer, rows_here, inner, unit_count)

time: 209 us -> 209 us (level)
  local copies, waits for them, and re-layouts: 33.6 us -> 31.3 us
  matrix products: 11.3 us -> 13.6 us
    reshape x1 -> x0, local copies, waits for them, and re-layouts: 2.76 us -> none  [per_device(): stacked.astype(jnp.bfloat16)]
    dot_general x1, matrix products: 6.38 us -> 8.71 us  [per_device(): jnp.einsum('wrtk,skn->wrtsn', piece, weights, preferred_element_type=jnp....]
    unnamed x45 -> x44, local copies, waits for them, and re-layouts: 9.94 us -> 9.8 us
where the time goes in v9:
time: 209 us
  waiting for transfers between devices  58.6 us (28%)
  blocking collectives  44 us (21%)
  starting transfers between devices  37 us (18%)
  local copies, waits for them, and re-layouts  31.3 us (15%)
  between operations  14.6 us (7%)
  matrix products  13.6 us (7%)
  other arithmetic  9.41 us (5%)
    all_to_all x1, waiting for transfers between devices, deal_rows(): lax.all_to_all(picked, ('ra', 'rb'), split_axis=0, concat_axis=0, tiled=T...  35.8 us
    all_gather x1, blocking collectives, per_device(): piece = lax.all_gather(regrouped, 'ra', axis=0, tiled=True)  28.7 us
    all_to_all x1, starting transfers between devices, deal_rows(): lax.all_to_all(picked, ('ra', 'rb'), split_axis=0, concat_axis=0, tiled=T...  23.7 us
    all_to_all x1, waiting for transfers between devices, per_device(): lax.all_to_all(stacked.astype(jnp.bfloat16), 'wt', split_axis=0, concat_a...  17.6 us
    unnamed x44, local copies, waits for them, and re-layouts  9.8 us
    all_to_all x1, starting transfers between devices, per_device(): gated = lax.all_to_all(gated, 'rb', split_axis=2, concat_axis=2, tiled=True)  9.66 us
    psum x1, blocking collectives, per_device(): lax.psum((jnp.sum(query_f * query_f, axis=1), jnp.sum(key_f * key_f, axis...  9.31 us
    dot_general x1, matrix products, per_device(): jnp.einsum('wrtk,skn->wrtsn', piece, weights, preferred_element_type=jnp....  8.71 us
  transfers between devices with their start and end apart: 4, of which 3 were waited for; matrix products, arithmetic and copies ran while one was open for 17% of the time, Pallas kernels for 0%

profile of v9, /device:TPU:1, one launch (start us, length us, event | category | flops | bytes accessed | tf_op | source)
XLA Modules:
  0.0 208.5 jit_solution(431246039303287525)
XLA Ops:
  7.2 1.2 pad_maximum_fusion
  8.4 1.2 copy.106
  10.6 9.3 %all-reduce = (f32[256]{0:T(256)S(1)}, f32[256]{0:T(256)S(1)}) all-reduce(f32[256]{0:T(256)S(1)} %fusion.10, f32[256]{0:T(256)S(1)} %fusion.8), channel_id=1, replica_groups=mesh['ra'=8,'rb'=16,'wt'=4] {'wt'}, use_global_device_ids=true, to_apply=%region_5.6 | all-reduce | flops 512 | bytes 4096 | tf_op jit(solution)/shard_map/psum | solution.py:88
  20.1 1.0 fusion.44
  21.5 1.5 copy.132
  23.3 0.9 fusion.43
  24.2 1.5 copy.129
  25.7 2.6 %copy.130 = f32[256,10,64]{2,0,1:T(8,128)} copy(f32[256,10,64]{0,2,1:T(8,128)} %get-tuple-element.28) | data formatting | bytes 1310720
  28.4 1.1 copy.103
  29.5 1.0 scatter_custom_fusion
  30.5 1.2 gather_fusion.1
  35.7 2.7 %fusion.46 = (f32[10,256]{1,0:T(8,128)S(1)}, f32[10,256,256]{1,2,0:T(8,128)}) fusion(pred[256,256]{0,1:T(8,128)(4,1)S(1)} %fusion.21, bf16[256,10,128]{2,0,1:T(8,128)(2,1)S(1)} %maximum_convert_fusion, bf16[256,10,64]{2,0,1:T(8,128)(2,1)S(1)} %get-tuple-element.25, bf16[256,10,64]{2,0,1:T(8,128)(2,1)S(1)} %get-tuple-element.24), kind=kOutput, calls=%fused_computation.94 | convolution fusion | flops 171704576 | bytes 4007936 | tf_op jit(solution)/shard_map/sub | solution.py:107
  38.4 2.2 %multiply_reduce_fusion = (f32[256]{0:T(256)S(1)}, f32[10,256,128]{1,2,0:T(8,128)S(1)}) fusion(bf16[256,10,128]{0,2,1:T(8,128)(2,1)S(1)} %bitcast.49, f32[10,256,256]{1,2,0:T(8,128)} %get-tuple-element.39, f32[10,256]{1,0:T(8,128)S(1)} %get-tuple-element.38), kind=kOutput, calls=%fused_computation.30 | convolution fusion | flops 170393344 | bytes 4598784 | tf_op jit(solution)/shard_map/hqk,khd->qhd/dot_general | solution.py:110
  41.5 1.2 gather_fusion
  44.2 6.0 %psum.23 = f32[256]{0:T(256)S(1)} all-reduce(f32[256]{0:T(256)S(1)} %get-tuple-element.40), channel_id=1, replica_groups=mesh['ra'=8,'rb'=16,'wt'=4] {'wt'}, use_global_device_ids=true, to_apply=%region_9.10 | all-reduce | flops 256 | bytes 2048 | tf_op jit(solution)/shard_map/psum | solution.py:115
  50.5 1.3 gather_fusion.2
  52.9 1.5 broadcast_select_fusion
  54.4 23.7 %all-to-all-start = ((bf16[128,2,1280]{2,1,0:T(2,128)(2,1)}), bf16[128,2,1280]{2,1,0:T(2,128)(2,1)S(1)}, u32[]{:S(2)}, u32[]{:S(2)}) async-start(bf16[128,2,1280]{2,1,0:T(2,128)(2,1)} %broadcast_select_fusion), calls=%async_computation | async-start | bytes 1310720 | tf_op jit(solution)/shard_map/all_to_all | solution.py:49
  78.7 35.8 %all-to-all-done = bf16[128,2,1280]{2,1,0:T(2,128)(2,1)S(1)} async-done(((bf16[128,2,1280]{2,1,0:T(2,128)(2,1)}), bf16[128,2,1280]{2,1,0:T(2,128)(2,1)S(1)}, u32[]{:S(2)}, u32[]{:S(2)}) %all-to-all-start) | async-done | bytes 655392 | tf_op jit(solution)/shard_map/all_to_all | solution.py:49
  114.8 1.6 scatter_custom_fusion.1
  116.4 28.7 %all-gather = bf16[8,36,1280]{2,1,0:T(8,128)(2,1)S(1)} all-gather(bf16[1,36,1280]{2,1,0:T(8,128)(2,1)S(1)} %bitcast.50), channel_id=1, replica_groups=mesh['ra'=8,'rb'=16,'wt'=4] {'ra'}, dimensions={0}, use_global_device_ids=true | all-gather | bytes 829440 | tf_op jit(solution)/shard_map/all_gather | solution.py:134
  145.2 8.7 %fusion.3 = bf16[4,8,9,2,1728]{4,2,3,1,0:T(8,128)(2,1)S(1)} fusion(bf16[2,1280,1728,1,1]{1,0,2,4,3:T(2,128)(2,1)} %bitcast.54, bf16[8,4,9,1280]{3,0,2,1:T(8,128)(2,1)S(1)} %bitcast.48), kind=kOutput, calls=%fused_computation.11 | convolution fusion | flops 2549035008 | bytes 11575296 | tf_op jit(solution)/shard_map/wrtk,skn->wrtsn/dot_general | solution.py:137
  153.9 2.6 %copy.110 = bf16[4,8,9,2,1728]{4,1,3,2,0:T(8,128)(2,1)} copy(bf16[4,8,9,2,1728]{4,2,3,1,0:T(8,128)(2,1)S(1)} %fusion.3) | data formatting | bytes 3981312 | tf_op jit(solution)/shard_map/convert_element_type | solution.py:138
  156.5 3.6 %all-to-all-start.1 = ((bf16[4,8,9,2,1728]{4,1,3,2,0:T(8,128)(2,1)}), bf16[4,8,9,2,1728]{4,1,3,2,0:T(8,128)(2,1)S(1)}, u32[]{:S(2)}, u32[]{:S(2)}) async-start(bf16[4,8,9,2,1728]{4,1,3,2,0:T(8,128)(2,1)} %copy.110), calls=%async_computation.1 | async-start | bytes 4128768 | tf_op jit(solution)/shard_map/all_to_all | solution.py:138
  160.1 1.6 copy.126
  161.7 1.2 reshape.498
  163.6 17.6 %all-to-all-done.1 = bf16[4,8,9,2,1728]{4,1,3,2,0:T(8,128)(2,1)S(1)} async-done(((bf16[4,8,9,2,1728]{4,1,3,2,0:T(8,128)(2,1)}), bf16[4,8,9,2,1728]{4,1,3,2,0:T(8,128)(2,1)S(1)}, u32[]{:S(2)}, u32[]{:S(2)}) %all-to-all-start.1) | async-done | bytes 1990688 | tf_op jit(solution)/shard_map/all_to_all | solution.py:138
  182.9 0.8 copy.114
  183.7 9.7 %all-to-all-start.2 = ((bf16[8,9,16,108]{3,0,1,2:T(8,128)(2,1)}), bf16[8,9,16,108]{3,0,1,2:T(8,128)(2,1)S(1)}, u32[]{:S(2)}, u32[]{:S(2)}) async-start(bf16[8,9,16,108]{3,0,1,2:T(8,128)(2,1)} %copy.114), calls=%async_computation.2 | async-start | bytes 589824 | tf_op jit(solution)/shard_map/all_to_all | solution.py:143
  193.5 0.7 scatter_fusion
  195.5 5.2 %all-to-all-done.2 = bf16[8,9,16,108]{3,0,1,2:T(8,128)(2,1)S(1)} async-done(((bf16[8,9,16,108]{3,0,1,2:T(8,128)(2,1)}), bf16[8,9,16,108]{3,0,1,2:T(8,128)(2,1)S(1)}, u32[]{:S(2)}, u32[]{:S(2)}) %all-to-all-start.2) | async-done | bytes 248864 | tf_op jit(solution)/shard_map/all_to_all | solution.py:143
  200.8 0.9 copy.118
  (96 shorter events, 14.2 us)
Async XLA Ops:
  7.2 109.2 %all-gather.3.cloned.1.call-start = ((), (), s32[]{:S(2)}) async-start(), calls=%async_computation.3 | async-start | bytes 9400320 | tf_op jit(solution)/shard_map/all_gather | solution.py:85
  7.2 2.4 %copy-start.9 = (bf16[256,1280]{1,0:T(8,128)(2,1)S(1)}, bf16[256,1280]{1,0:T(8,128)(2,1)}, u32[]{:S(2)}) copy-start(bf16[256,1280]{1,0:T(8,128)(2,1)} %param.14) | copy-start | bytes 1966084
  8.4 1.5 copy-start.10
  9.9 10.0 %copy-start.13 = (f32[1280]{0:T(1024)S(1)}, f32[1280]{0:T(1024)}, u32[]{:S(2)}) copy-start(f32[1280]{0:T(1024)} %param.17) | copy-start | bytes 15364
  21.5 1.5 copy-start.14
  25.7 2.6 %copy-start.3 = (bf16[256,1280]{1,0:T(8,128)(2,1)S(1)}, bf16[256,1280]{1,0:T(8,128)(2,1)}, u32[]{:S(2)}) copy-start(bf16[256,1280]{1,0:T(8,128)(2,1)} %param.15) | copy-start | bytes 1966084
  25.7 3.7 %copy-start.16 = (s32[128]{0:T(128)S(1)}, s32[128]{0:T(128)}, u32[]{:S(2)}) copy-start(s32[128]{0:T(128)} %param.22) | copy-start | bytes 1540
  25.7 4.7 %copy-start = (s32[128]{0:T(128)S(1)}, s32[128]{0:T(128)}, u32[]{:S(2)}) copy-start(s32[128]{0:T(128)} %param.21) | copy-start | bytes 1540
  33.5 1.3 copy-start.2
  33.9 1.5 copy-start.1
  34.2 1.4 copy-start.8
  35.7 2.8 %copy-start.11 = (bf16[256,1280]{0,1:T(8,128)(2,1)S(1)}, bf16[256,1280]{0,1:T(8,128)(2,1)}, u32[]{:S(2)}) copy-start(bf16[256,1280]{0,1:T(8,128)(2,1)} %copy.103) | copy-start | bytes 1966084
  40.6 9.6 %copy-start.12 = (bf16[256,1280]{1,0:T(8,128)(2,1)S(1)}, bf16[256,1280]{1,0:T(8,128)(2,1)}, u32[]{:S(2)}) copy-start(bf16[256,1280]{1,0:T(8,128)(2,1)} %param.12) | copy-start | bytes 1966084
  40.6 9.6 %copy-start.15 = (f32[1280]{0:T(1024)S(1)}, f32[1280]{0:T(1024)}, u32[]{:S(2)}) copy-start(f32[1280]{0:T(1024)} %param.18) | copy-start | bytes 15364
  54.4 60.1 %all-to-all-start = ((bf16[128,2,1280]{2,1,0:T(2,128)(2,1)}), bf16[128,2,1280]{2,1,0:T(2,128)(2,1)S(1)}, u32[]{:S(2)}, u32[]{:S(2)}) async-start(bf16[128,2,1280]{2,1,0:T(2,128)(2,1)} %broadcast_select_fusion), calls=%async_computation | async-start | bytes 1310720 | tf_op jit(solution)/shard_map/all_to_all | solution.py:49
  156.5 24.7 %all-to-all-start.1 = ((bf16[4,8,9,2,1728]{4,1,3,2,0:T(8,128)(2,1)}), bf16[4,8,9,2,1728]{4,1,3,2,0:T(8,128)(2,1)S(1)}, u32[]{:S(2)}, u32[]{:S(2)}) async-start(bf16[4,8,9,2,1728]{4,1,3,2,0:T(8,128)(2,1)} %copy.110), calls=%async_computation.1 | async-start | bytes 4128768 | tf_op jit(solution)/shard_map/all_to_all | solution.py:138
  160.1 3.5 %copy-start.17 = (s32[1,2]{1,0:T(1,128)S(1)}, s32[1,2]{1,0:T(1,128)}, u32[]{:S(2)}) copy-start(s32[1,2]{1,0:T(1,128)} %param.23) | copy-start | bytes 28
  182.7 10.6 %copy-start.5 = (bf16[2,128,1280]{2,1,0:T(8,128)(2,1)S(1)}, bf16[2,128,1280]{2,1,0:T(8,128)(2,1)}, u32[]{:S(2)}) copy-start(bf16[2,128,1280]{2,1,0:T(8,128)(2,1)} %reshape.498) | copy-start | bytes 1966084
  183.7 17.1 %all-to-all-start.2 = ((bf16[8,9,16,108]{3,0,1,2:T(8,128)(2,1)}), bf16[8,9,16,108]{3,0,1,2:T(8,128)(2,1)S(1)}, u32[]{:S(2)}, u32[]{:S(2)}) async-start(bf16[8,9,16,108]{3,0,1,2:T(8,128)(2,1)} %copy.114), calls=%async_computation.2 | async-start | bytes 589824 | tf_op jit(solution)/shard_map/all_to_all | solution.py:143
  193.5 1.1 copy-start.4
  194.6 0.9 copy-start.7
  195.5 6.2 %copy-start.6 = (bf16[2,128,1280]{2,1,0:T(8,128)(2,1)}, bf16[2,128,1280]{2,1,0:T(8,128)(2,1)S(1)}, u32[]{:S(2)}) copy-start(bf16[2,128,1280]{2,1,0:T(8,128)(2,1)S(1)} %scatter_fusion.1) | copy-start | bytes 1966084
Sparse Core Ops, SparseCore 0:
  10.1 67.7 all-gather.2

commit v10 on v9

--- a/solution.py
+++ b/solution.py
@@ -131,7 +131,9 @@
     regrouped, weights = lax.optimization_barrier((regrouped, weights))
     outer = lax.axis_size("ra")
     inner = lax.axis_size("rb")
-    piece = lax.all_gather(regrouped, "ra", axis=0, tiled=True)
+    piece = lax.all_to_all(
+        jnp.broadcast_to(regrouped[None], (outer,) + regrouped.shape), "ra", 0, 0, tiled=True
+    )
     parts = lax.axis_size("wt")
     piece = jnp.transpose(piece.reshape(outer, parts, LIVE // parts, feature_count), (1, 0, 2, 3))
     stacked = jnp.einsum("wrtk,skn->wrtsn", piece, weights, preferred_element_type=jnp.float32)

time: 209 us -> 229 us (1.096)
  blocking collectives: 44 us -> 58 us
  starting transfers between devices: 37 us -> 47.9 us
  waiting for transfers between devices: 58.6 us -> 53.2 us
    all_to_all x0 -> x1, blocking collectives: none -> 42.7 us  [per_device(): lax.all_to_all(jnp.broadcast_to(regrouped[None], (outer,) + regrouped.sha...]
    all_gather x1 -> x0, blocking collectives: 28.7 us -> none  [per_device(): piece = lax.all_gather(regrouped, 'ra', axis=0, tiled=True)]
    all_to_all x1, starting transfers between devices: 9.66 us -> 20.6 us  [per_device(): gated = lax.all_to_all(gated, 'rb', split_axis=2, concat_axis=2, tiled=True)]
    all_to_all x1, waiting for transfers between devices: 17.6 us -> 12.2 us  [per_device(): lax.all_to_all(stacked.astype(jnp.bfloat16), 'wt', split_axis=0, concat_a...]
  transfers between devices with their start and end apart: 4 -> 4, of which waited for: 3 -> 3; matrix products, arithmetic and copies ran while one was open for 17% -> 16% of each run, Pallas kernels for 0% -> 0%
where the time goes in v10:
time: 229 us; the launch traced here: 228 us
  blocking collectives  58 us (25%)
  waiting for transfers between devices  53.2 us (23%)
  starting transfers between devices  47.9 us (21%)
  local copies, waits for them, and re-layouts  31.4 us (14%)
  between operations  14.6 us (6%)
  matrix products  13.6 us (6%)
  other arithmetic  9.41 us (4%)
    all_to_all x1, blocking collectives, per_device(): lax.all_to_all(jnp.broadcast_to(regrouped[None], (outer,) + regrouped.sha...  42.7 us
    all_to_all x1, waiting for transfers between devices, deal_rows(): lax.all_to_all(picked, ('ra', 'rb'), split_axis=0, concat_axis=0, tiled=T...  35.8 us
    all_to_all x1, starting transfers between devices, deal_rows(): lax.all_to_all(picked, ('ra', 'rb'), split_axis=0, concat_axis=0, tiled=T...  23.7 us
    all_to_all x1, starting transfers between devices, per_device(): gated = lax.all_to_all(gated, 'rb', split_axis=2, concat_axis=2, tiled=True)  20.6 us
    all_to_all x1, waiting for transfers between devices, per_device(): lax.all_to_all(stacked.astype(jnp.bfloat16), 'wt', split_axis=0, concat_a...  12.2 us
    unnamed x44, local copies, waits for them, and re-layouts  9.8 us
    psum x1, blocking collectives, per_device(): lax.psum((jnp.sum(query_f * query_f, axis=1), jnp.sum(key_f * key_f, axis...  9.31 us
    dot_general x1, matrix products, per_device(): jnp.einsum('wrtk,skn->wrtsn', piece, weights, preferred_element_type=jnp....  8.71 us
  transfers between devices with their start and end apart: 4, of which 3 were waited for; matrix products, arithmetic and copies ran while one was open for 16% of the time, Pallas kernels for 0%

profile of v10, /device:TPU:1, one launch (start us, length us, event | category | flops | bytes accessed | tf_op | source)
XLA Modules:
  0.0 228.2 jit_solution(8926998026586686431)
XLA Ops:
  7.2 1.2 pad_maximum_fusion
  8.4 1.2 copy.91
  10.6 9.3 %all-reduce = (f32[256]{0:T(256)S(1)}, f32[256]{0:T(256)S(1)}) all-reduce(f32[256]{0:T(256)S(1)} %fusion.10, f32[256]{0:T(256)S(1)} %fusion.8), channel_id=1, replica_groups=mesh['ra'=8,'rb'=16,'wt'=4] {'wt'}, use_global_device_ids=true, to_apply=%region_5.6 | all-reduce | flops 512 | bytes 4096 | tf_op jit(solution)/shard_map/psum | solution.py:88
  20.1 1.0 fusion.44
  21.5 1.5 copy.117
  23.3 0.9 fusion.43
  24.2 1.5 copy.114
  25.7 2.6 %copy.115 = f32[256,10,64]{2,0,1:T(8,128)} copy(f32[256,10,64]{0,2,1:T(8,128)} %get-tuple-element.25) | data formatting | bytes 1310720
  28.4 1.1 copy.88
  29.5 1.0 scatter_custom_fusion
  30.5 1.2 gather_fusion.1
  35.7 2.7 %fusion.46 = (f32[10,256]{1,0:T(8,128)S(1)}, f32[10,256,256]{1,2,0:T(8,128)}) fusion(pred[256,256]{0,1:T(8,128)(4,1)S(1)} %fusion.21, bf16[256,10,128]{2,0,1:T(8,128)(2,1)S(1)} %maximum_convert_fusion, bf16[256,10,64]{2,0,1:T(8,128)(2,1)S(1)} %get-tuple-element.22, bf16[256,10,64]{2,0,1:T(8,128)(2,1)S(1)} %get-tuple-element.21), kind=kOutput, calls=%fused_computation.94 | convolution fusion | flops 171704576 | bytes 4007936 | tf_op jit(solution)/shard_map/sub | solution.py:107
  38.4 2.2 multiply_reduce_fusion
  41.5 1.2 gather_fusion
  44.2 6.0 %psum.23 = f32[256]{0:T(256)S(1)} all-reduce(f32[256]{0:T(256)S(1)} %get-tuple-element.37), channel_id=1, replica_groups=mesh['ra'=8,'rb'=16,'wt'=4] {'wt'}, use_global_device_ids=true, to_apply=%region_9.10 | all-reduce | flops 256 | bytes 2048 | tf_op jit(solution)/shard_map/psum | solution.py:115
  50.5 1.3 gather_fusion.2
  52.9 1.5 broadcast_select_fusion
  54.4 23.7 %all-to-all-start = ((bf16[128,2,1280]{2,1,0:T(2,128)(2,1)}), bf16[128,2,1280]{2,1,0:T(2,128)(2,1)S(1)}, u32[]{:S(2)}, u32[]{:S(2)}) async-start(bf16[128,2,1280]{2,1,0:T(2,128)(2,1)} %broadcast_select_fusion), calls=%async_computation | async-start | bytes 1310720 | tf_op jit(solution)/shard_map/all_to_all | solution.py:49
  78.7 35.8 %all-to-all-done = bf16[128,2,1280]{2,1,0:T(2,128)(2,1)S(1)} async-done(((bf16[128,2,1280]{2,1,0:T(2,128)(2,1)}), bf16[128,2,1280]{2,1,0:T(2,128)(2,1)S(1)}, u32[]{:S(2)}, u32[]{:S(2)}) %all-to-all-start) | async-done | bytes 655392 | tf_op jit(solution)/shard_map/all_to_all | solution.py:49
  114.8 1.6 scatter_custom_fusion.1
  116.5 42.7 %all_to_all.20 = bf16[8,36,1280]{2,1,0:T(8,128)(2,1)S(1)} all-to-all(bf16[8,36,1280]{2,1,0:T(8,128)(2,1)S(1)} %broadcast_in_dim.98), channel_id=1, replica_groups=mesh['ra'=8,'rb'=16,'wt'=4] {'ra'}, dimensions={0} | all-to-all | bytes 1474560 | tf_op jit(solution)/shard_map/all_to_all | solution.py:134
  159.3 8.7 %fusion.3 = bf16[4,8,9,2,1728]{4,2,3,1,0:T(8,128)(2,1)S(1)} fusion(bf16[2,1280,1728,1,1]{1,0,2,4,3:T(2,128)(2,1)} %bitcast.52, bf16[8,4,9,1280]{3,0,2,1:T(8,128)(2,1)S(1)} %bitcast.47), kind=kOutput, calls=%fused_computation.11 | convolution fusion | flops 2549035008 | bytes 11575296 | tf_op jit(solution)/shard_map/wrtk,skn->wrtsn/dot_general | solution.py:139
  168.0 2.6 %copy.95 = bf16[4,8,9,2,1728]{4,1,3,2,0:T(8,128)(2,1)} copy(bf16[4,8,9,2,1728]{4,2,3,1,0:T(8,128)(2,1)S(1)} %fusion.3) | data formatting | bytes 3981312 | tf_op jit(solution)/shard_map/convert_element_type | solution.py:140
  170.6 3.6 %all-to-all-start.2 = ((bf16[4,8,9,2,1728]{4,1,3,2,0:T(8,128)(2,1)}), bf16[4,8,9,2,1728]{4,1,3,2,0:T(8,128)(2,1)S(1)}, u32[]{:S(2)}, u32[]{:S(2)}) async-start(bf16[4,8,9,2,1728]{4,1,3,2,0:T(8,128)(2,1)} %copy.95), calls=%async_computation.2 | async-start | bytes 4128768 | tf_op jit(solution)/shard_map/all_to_all | solution.py:140
  174.2 1.6 copy.111
  175.8 1.2 reshape.496
  177.7 12.2 %all-to-all-done.2 = bf16[4,8,9,2,1728]{4,1,3,2,0:T(8,128)(2,1)S(1)} async-done(((bf16[4,8,9,2,1728]{4,1,3,2,0:T(8,128)(2,1)}), bf16[4,8,9,2,1728]{4,1,3,2,0:T(8,128)(2,1)S(1)}, u32[]{:S(2)}, u32[]{:S(2)}) %all-to-all-start.2) | async-done | bytes 1990688 | tf_op jit(solution)/shard_map/all_to_all | solution.py:140
  191.6 0.8 copy.99
  192.4 20.6 %all-to-all-start.3 = ((bf16[8,9,16,108]{3,0,1,2:T(8,128)(2,1)}), bf16[8,9,16,108]{3,0,1,2:T(8,128)(2,1)S(1)}, u32[]{:S(2)}, u32[]{:S(2)}) async-start(bf16[8,9,16,108]{3,0,1,2:T(8,128)(2,1)} %copy.99), calls=%async_computation.3 | async-start | bytes 589824 | tf_op jit(solution)/shard_map/all_to_all | solution.py:145
  214.4 0.7 scatter_fusion.1
  215.1 5.2 %all-to-all-done.3 = bf16[8,9,16,108]{3,0,1,2:T(8,128)(2,1)S(1)} async-done(((bf16[8,9,16,108]{3,0,1,2:T(8,128)(2,1)}), bf16[8,9,16,108]{3,0,1,2:T(8,128)(2,1)S(1)}, u32[]{:S(2)}, u32[]{:S(2)}) %all-to-all-start.3) | async-done | bytes 248864 | tf_op jit(solution)/shard_map/all_to_all | solution.py:145
  220.4 0.9 copy.103
  (97 shorter events, 14.3 us)
Async XLA Ops:
  7.2 109.2 %all-gather.2.cloned.1.call-start = ((), (), s32[]{:S(2)}) async-start(), calls=%async_computation.4 | async-start | bytes 9400320 | tf_op jit(solution)/shard_map/all_gather | solution.py:85
  7.2 2.4 %copy-start.9 = (bf16[256,1280]{1,0:T(8,128)(2,1)S(1)}, bf16[256,1280]{1,0:T(8,128)(2,1)}, u32[]{:S(2)}) copy-start(bf16[256,1280]{1,0:T(8,128)(2,1)} %param.14) | copy-start | bytes 1966084
  8.4 1.5 copy-start.10
  9.9 10.0 %copy-start.13 = (f32[1280]{0:T(1024)S(1)}, f32[1280]{0:T(1024)}, u32[]{:S(2)}) copy-start(f32[1280]{0:T(1024)} %param.17) | copy-start | bytes 15364
  21.5 1.5 copy-start.14
  25.7 2.6 %copy-start.3 = (bf16[256,1280]{1,0:T(8,128)(2,1)S(1)}, bf16[256,1280]{1,0:T(8,128)(2,1)}, u32[]{:S(2)}) copy-start(bf16[256,1280]{1,0:T(8,128)(2,1)} %param.15) | copy-start | bytes 1966084
  25.7 3.7 %copy-start.16 = (s32[128]{0:T(128)S(1)}, s32[128]{0:T(128)}, u32[]{:S(2)}) copy-start(s32[128]{0:T(128)} %param.22) | copy-start | bytes 1540
  25.7 4.7 %copy-start = (s32[128]{0:T(128)S(1)}, s32[128]{0:T(128)}, u32[]{:S(2)}) copy-start(s32[128]{0:T(128)} %param.21) | copy-start | bytes 1540
  33.5 1.3 copy-start.2
  33.9 1.5 copy-start.1
  34.2 1.4 copy-start.8
  35.7 2.8 %copy-start.11 = (bf16[256,1280]{0,1:T(8,128)(2,1)S(1)}, bf16[256,1280]{0,1:T(8,128)(2,1)}, u32[]{:S(2)}) copy-start(bf16[256,1280]{0,1:T(8,128)(2,1)} %copy.88) | copy-start | bytes 1966084
  40.6 9.6 %copy-start.12 = (bf16[256,1280]{1,0:T(8,128)(2,1)S(1)}, bf16[256,1280]{1,0:T(8,128)(2,1)}, u32[]{:S(2)}) copy-start(bf16[256,1280]{1,0:T(8,128)(2,1)} %param.12) | copy-start | bytes 1966084
  40.6 9.6 %copy-start.15 = (f32[1280]{0:T(1024)S(1)}, f32[1280]{0:T(1024)}, u32[]{:S(2)}) copy-start(f32[1280]{0:T(1024)} %param.18) | copy-start | bytes 15364
  54.4 60.1 %all-to-all-start = ((bf16[128,2,1280]{2,1,0:T(2,128)(2,1)}), bf16[128,2,1280]{2,1,0:T(2,128)(2,1)S(1)}, u32[]{:S(2)}, u32[]{:S(2)}) async-start(bf16[128,2,1280]{2,1,0:T(2,128)(2,1)} %broadcast_select_fusion), calls=%async_computation | async-start | bytes 1310720 | tf_op jit(solution)/shard_map/all_to_all | solution.py:49
  170.6 19.3 %all-to-all-start.2 = ((bf16[4,8,9,2,1728]{4,1,3,2,0:T(8,128)(2,1)}), bf16[4,8,9,2,1728]{4,1,3,2,0:T(8,128)(2,1)S(1)}, u32[]{:S(2)}, u32[]{:S(2)}) async-start(bf16[4,8,9,2,1728]{4,1,3,2,0:T(8,128)(2,1)} %copy.95), calls=%async_computation.2 | async-start | bytes 4128768 | tf_op jit(solution)/shard_map/all_to_all | solution.py:140
  174.2 3.5 %copy-start.17 = (s32[1,2]{1,0:T(1,128)S(1)}, s32[1,2]{1,0:T(1,128)}, u32[]{:S(2)}) copy-start(s32[1,2]{1,0:T(1,128)} %param.23) | copy-start | bytes 28
  191.4 21.6 %copy-start.5 = (bf16[2,128,1280]{2,1,0:T(8,128)(2,1)S(1)}, bf16[2,128,1280]{2,1,0:T(8,128)(2,1)}, u32[]{:S(2)}) copy-start(bf16[2,128,1280]{2,1,0:T(8,128)(2,1)} %reshape.496) | copy-start | bytes 1966084
  192.4 28.0 %all-to-all-start.3 = ((bf16[8,9,16,108]{3,0,1,2:T(8,128)(2,1)}), bf16[8,9,16,108]{3,0,1,2:T(8,128)(2,1)S(1)}, u32[]{:S(2)}, u32[]{:S(2)}) async-start(bf16[8,9,16,108]{3,0,1,2:T(8,128)(2,1)} %copy.99), calls=%async_computation.3 | async-start | bytes 589824 | tf_op jit(solution)/shard_map/all_to_all | solution.py:145
  213.1 1.1 copy-start.4
  214.2 0.9 copy-start.7
  215.1 6.2 %copy-start.6 = (bf16[2,128,1280]{2,1,0:T(8,128)(2,1)}, bf16[2,128,1280]{2,1,0:T(8,128)(2,1)S(1)}, u32[]{:S(2)}) copy-start(bf16[2,128,1280]{2,1,0:T(8,128)(2,1)S(1)} %scatter_fusion.1) | copy-start | bytes 1966084
Sparse Core Ops, SparseCore 0:
  10.1 67.7 all-gather.1

commit v11 on v9

--- a/solution.py
+++ b/solution.py
@@ -22,13 +22,10 @@
 
 def rotate(heads_in, cosine, sine_table):
     half_width = heads_in.shape[-1] // 2
-    leading = heads_in[..., :half_width]
-    trailing = heads_in[..., half_width:]
-    cos_b = cosine[:, None, :]
-    sin_b = sine_table[:, None, :]
-    return jnp.concatenate(
-        [leading * cos_b - trailing * sin_b, trailing * cos_b + leading * sin_b], axis=-1
-    )
+    swapped = jnp.concatenate([heads_in[..., half_width:], heads_in[..., :half_width]], axis=-1)
+    cos_full = jnp.concatenate([cosine, cosine], axis=-1)[:, None, :]
+    sin_signed = jnp.concatenate([-sine_table, sine_table], axis=-1)[:, None, :]
+    return heads_in * cos_full + swapped * sin_signed
 
 
 def deal_rows(source, owner_start, owner_len, device, owners, live_rows):

time: 209 us -> 216 us (1.033)
  waiting for transfers between devices: 58.6 us -> 32.7 us
  blocking collectives: 44 us -> 67.6 us
  other arithmetic: 9.41 us -> 16.2 us
  local copies, waits for them, and re-layouts: 31.3 us -> 37.4 us
  starting transfers between devices: 37 us -> 33.4 us
    all_to_all x0 -> x1, blocking collectives: none -> 23.6 us  [per_device(): lax.all_to_all(stacked.astype(jnp.bfloat16), 'wt', split_axis=0, concat_a...]
    all_to_all x1 -> x0, waiting for transfers between devices: 17.6 us -> none  [per_device(): lax.all_to_all(stacked.astype(jnp.bfloat16), 'wt', split_axis=0, concat_a...]
    all_to_all x1, waiting for transfers between devices: 35.8 us -> 28.7 us  [deal_rows(): lax.all_to_all(picked, ('ra', 'rb'), split_axis=0, concat_axis=0, tiled=T...]
    unnamed x44 -> x46, local copies, waits for them, and re-layouts: 9.8 us -> 4.82 us
    all_to_all x1 -> x0, starting transfers between devices: 3.6 us -> none  [per_device(): lax.all_to_all(stacked.astype(jnp.bfloat16), 'wt', split_axis=0, concat_a...]
    convert_element_type x2 -> x0, local copies, waits for them, and re-layouts: 2.79 us -> none  [per_device(): rotate(key_n.reshape(slot_count, head_count, HD), cosine, sine_table)]
    sub x1 -> x0, matrix products: 2.74 us -> none  [per_device(): expd = jnp.exp(scores - row_peak)]
    gather x2, local copies, waits for them, and re-layouts: 1.5 us -> 4.08 us  [deal_rows(): source[jnp.minimum(local_index, slot_count - 1)]]
  transfers between devices with their start and end apart: 4 -> 3, of which waited for: 3 -> 2; matrix products, arithmetic and copies ran while one was open for 17% -> 20% of each run, Pallas kernels for 0% -> 0%
where the time goes in v11:
time: 216 us; the launch traced here: 215 us
  blocking collectives  67.6 us (31%)
  local copies, waits for them, and re-layouts  37.4 us (17%)
  starting transfers between devices  33.4 us (15%)
  waiting for transfers between devices  32.7 us (15%)
  other arithmetic  16.2 us (8%)
  between operations  14.6 us (7%)
  matrix products  13.2 us (6%)
    all_gather x1, blocking collectives, per_device(): piece = lax.all_gather(regrouped, 'ra', axis=0, tiled=True)  28.7 us
    all_to_all x1, waiting for transfers between devices, deal_rows(): lax.all_to_all(picked, ('ra', 'rb'), split_axis=0, concat_axis=0, tiled=T...  28.7 us
    all_to_all x1, blocking collectives, per_device(): lax.all_to_all(stacked.astype(jnp.bfloat16), 'wt', split_axis=0, concat_a...  23.6 us
    all_to_all x1, starting transfers between devices, deal_rows(): lax.all_to_all(picked, ('ra', 'rb'), split_axis=0, concat_axis=0, tiled=T...  23.4 us
    all_to_all x1, starting transfers between devices, per_device(): gated = lax.all_to_all(gated, 'rb', split_axis=2, concat_axis=2, tiled=True)  9.94 us
    psum x1, blocking collectives, per_device(): lax.psum((jnp.sum(query_f * query_f, axis=1), jnp.sum(key_f * key_f, axis...  9.29 us
    dot_general x1, matrix products, per_device(): jnp.einsum('wrtk,skn->wrtsn', piece, weights, preferred_element_type=jnp....  8.71 us
    psum x1, blocking collectives, per_device(): attn_sq = lax.psum(jnp.sum(attended_f * attended_f, axis=1), 'wt')  6.01 us
  transfers between devices with their start and end apart: 3, of which 2 were waited for; matrix products, arithmetic and copies ran while one was open for 20% of the time, Pallas kernels for 0%

profile of v11, /device:TPU:1, one launch (start us, length us, event | category | flops | bytes accessed | tf_op | source)
XLA Modules:
  0.0 215.1 jit_solution(12734638910726122545)
XLA Ops:
  7.2 1.2 pad_maximum_fusion
  8.4 1.2 copy.108
  12.1 1.2 gather_fusion.1
  14.8 9.3 %all-reduce = (f32[256]{0:T(256)S(1)}, f32[256]{0:T(256)S(1)}) all-reduce(f32[256]{0:T(256)S(1)} %fusion.10, f32[256]{0:T(256)S(1)} %fusion.8), channel_id=1, replica_groups=mesh['ra'=8,'rb'=16,'wt'=4] {'wt'}, use_global_device_ids=true, to_apply=%region_5.6 | all-reduce | flops 512 | bytes 4096 | tf_op jit(solution)/shard_map/psum | solution.py:85
  28.9 3.8 %multiply_reduce_fusion = (f32[256]{0:T(256)S(1)}, f32[10,256,128]{1,2,0:T(8,128)}) fusion(bf16[256,10,128]{0,2,1:T(8,128)(2,1)S(1)} %bitcast.58, f32[10,256]{1,0:T(8,128)S(1)} %fusion.47, f32[10,256,256]{1,2,0:T(8,128)} %copy-done.1, pred[256,256]{0,1:T(8,128)(4,1)} %copy-done.7), kind=kOutput, calls=%fused_computation.36 | convolution fusion | flops 172362240 | bytes 4664320 | tf_op jit(solution)/shard_map/hqk,khd->qhd/dot_general | solution.py:107
  32.7 2.9 %copy.107 = f32[256,1280]{1,0:T(8,128)} copy(f32[256,1280]{0,1:T(8,128)} %bitcast.61) | data formatting | bytes 2621440 | tf_op jit(solution)/shard_map/convert_element_type | solution.py:111
  36.0 1.4 gather_fusion
  38.0 1.2 and_select_fusion.1
  39.5 6.0 %psum.23 = f32[256]{0:T(256)S(1)} all-reduce(f32[256]{0:T(256)S(1)} %get-tuple-element.37), channel_id=1, replica_groups=mesh['ra'=8,'rb'=16,'wt'=4] {'wt'}, use_global_device_ids=true, to_apply=%region_9.10 | all-reduce | flops 256 | bytes 2048 | tf_op jit(solution)/shard_map/psum | solution.py:112
  45.5 1.9 add_convert_fusion
  47.4 2.1 gather_fusion.2
  49.5 2.0 reshape.414
  51.5 2.0 add_compare_fusion.1
  53.4 1.4 copy.100
  54.8 2.2 %broadcast_select_fusion = bf16[128,2,1280]{2,1,0:T(2,128)(2,1)} fusion(bf16[128,2,1280]{2,1,0:T(2,128)(2,1)S(1)} %reshape.414, pred[128,2]{1,0:T(8,128)(4,1)} %copy.100), kind=kLoop, calls=%fused_computation.41 | loop fusion | flops 327680 | bytes 1310976 | tf_op jit(solution)/shard_map/jit(_where)/select_n | solution.py:41
  57.0 23.4 %all-to-all-start = ((bf16[128,2,1280]{2,1,0:T(2,128)(2,1)}), bf16[128,2,1280]{2,1,0:T(2,128)(2,1)S(1)}, u32[]{:S(2)}, u32[]{:S(2)}) async-start(bf16[128,2,1280]{2,1,0:T(2,128)(2,1)} %broadcast_select_fusion), calls=%async_computation | async-start | bytes 1310720 | tf_op jit(solution)/shard_map/all_to_all | solution.py:46
  80.4 1.4 copy.98
  81.8 1.4 lt.106
  83.3 1.3 fusion.31
  84.6 1.4 copy.99
  87.0 1.2 compare_select_fusion.1
  88.2 28.7 %all-to-all-done = bf16[128,2,1280]{2,1,0:T(2,128)(2,1)S(1)} async-done(((bf16[128,2,1280]{2,1,0:T(2,128)(2,1)}), bf16[128,2,1280]{2,1,0:T(2,128)(2,1)S(1)}, u32[]{:S(2)}, u32[]{:S(2)}) %all-to-all-start) | async-done | bytes 655392 | tf_op jit(solution)/shard_map/all_to_all | solution.py:46
  117.9 2.2 %scatter_custom_fusion.1 = bf16[36,1280]{1,0:T(8,128)(2,1)S(1)} fusion(s32[256]{0:T(256)} %bitcast.68, bf16[256,1280]{1,0:T(8,128)(2,1)} %reshape.433, bf16[]{:T(256)} %constant.37.clone.1), kind=kCustom, calls=%fused_computation.57 | custom fusion | bytes 92672 | tf_op jit(solution)/shard_map/scatter | solution.py:54
  120.1 28.7 %all-gather = bf16[8,36,1280]{2,1,0:T(8,128)(2,1)S(1)} all-gather(bf16[1,36,1280]{2,1,0:T(8,128)(2,1)S(1)} %bitcast.65), channel_id=1, replica_groups=mesh['ra'=8,'rb'=16,'wt'=4] {'ra'}, dimensions={0}, use_global_device_ids=true | all-gather | bytes 829440 | tf_op jit(solution)/shard_map/all_gather | solution.py:131
  148.9 8.7 %fusion.3 = bf16[4,8,9,2,1728]{4,2,3,1,0:T(8,128)(2,1)S(1)} fusion(bf16[2,1280,1728,1,1]{1,0,2,4,3:T(2,128)(2,1)} %bitcast.69, bf16[8,4,9,1280]{3,0,2,1:T(8,128)(2,1)S(1)} %bitcast.64), kind=kOutput, calls=%fused_computation.11 | convolution fusion | flops 2549035008 | bytes 11575296 | tf_op jit(solution)/shard_map/wrtk,skn->wrtsn/dot_general | solution.py:134
  157.6 1.3 copy.112
  158.9 23.6 %all_to_all.15 = bf16[4,8,9,2,1728]{4,1,3,2,0:T(8,128)(2,1)S(1)} all-to-all(bf16[4,8,9,2,1728]{4,1,3,2,0:T(8,128)(2,1)S(1)} %copy.112), channel_id=1, replica_groups=mesh['ra'=8,'rb'=16,'wt'=4] {'wt'}, dimensions={0} | all-to-all | bytes 3981312 | tf_op jit(solution)/shard_map/all_to_all | solution.py:135
  183.9 1.6 reshape.465
  185.5 2.5 %reshape.466 = f32[8,9,16,108]{3,2,0,1:T(8,128)} reshape(f32[8,9,1,1728]{3,0,2,1:T(8,128)} %get-tuple-element.29) | data formatting | bytes 995328 | tf_op jit(solution)/shard_map/squeeze | solution.py:137
  187.9 1.2 multiply_convert_fusion
  190.0 9.9 %all-to-all-start.2 = ((bf16[8,9,16,108]{3,0,1,2:T(8,128)(2,1)}), bf16[8,9,16,108]{3,0,1,2:T(8,128)(2,1)S(1)}, u32[]{:S(2)}, u32[]{:S(2)}) async-start(bf16[8,9,16,108]{3,0,1,2:T(8,128)(2,1)} %copy.116), calls=%async_computation.2 | async-start | bytes 589824 | tf_op jit(solution)/shard_map/all_to_all | solution.py:140
  203.2 4.0 %all-to-all-done.2 = bf16[8,9,16,108]{3,0,1,2:T(8,128)(2,1)S(1)} async-done(((bf16[8,9,16,108]{3,0,1,2:T(8,128)(2,1)}), bf16[8,9,16,108]{3,0,1,2:T(8,128)(2,1)S(1)}, u32[]{:S(2)}, u32[]{:S(2)}) %all-to-all-start.2) | async-done | bytes 248864 | tf_op jit(solution)/shard_map/all_to_all | solution.py:140
  (96 shorter events, 18.2 us)
Async XLA Ops:
  7.2 113.0 %all-gather.3.cloned.1.call-start = ((), (), s32[]{:S(2)}) async-start(), calls=%async_computation.3 | async-start | bytes 9400320 | tf_op jit(solution)/shard_map/all_gather | solution.py:82
  7.2 2.4 %copy-start.4 = (bf16[256,1280]{1,0:T(8,128)(2,1)S(1)}, bf16[256,1280]{1,0:T(8,128)(2,1)}, u32[]{:S(2)}) copy-start(bf16[256,1280]{1,0:T(8,128)(2,1)} %param.14) | copy-start | bytes 1966084
  8.4 1.5 copy-start.5
  9.7 1.1 copy-start.6
  9.9 1.1 copy-start.19
  9.9 2.1 copy-start
  11.0 14.3 %copy-start.8 = (f32[1280]{0:T(1024)S(1)}, f32[1280]{0:T(1024)}, u32[]{:S(2)}) copy-start(f32[1280]{0:T(1024)} %param.17) | copy-start | bytes 15364
  12.1 13.1 %copy-start.10 = (s32[1024]{0:T(1024)}, s32[1024]{0:T(1024)S(1)}, u32[]{:S(2)}) copy-start(s32[1024]{0:T(1024)S(1)} %pad_clamp_fusion.1) | copy-start | bytes 12292
  13.3 0.5 copy-start.18
  24.8 0.8 copy-start.16
  25.3 2.0 copy-start.7
  25.6 0.7 copy-start.9
  27.3 1.6 copy-start.1
  37.4 1.8 copy-start.15
  38.0 7.5 %copy-start.13 = (s32[2]{0:T(128)}, s32[2]{0:T(128)S(1)}, u32[]{:S(2)}) copy-start(s32[2]{0:T(128)S(1)} %iota_multiply_fusion.1) | copy-start | bytes 28
  39.2 6.2 %copy-start.11 = (s32[128]{0:T(128)}, s32[128]{0:T(128)S(1)}, u32[]{:S(2)}) copy-start(s32[128]{0:T(128)S(1)} %get-tuple-element.39) | copy-start | bytes 1540
  49.5 2.0 copy-start.12
  54.8 28.5 %copy-start.14 = (s32[2]{0:T(128)S(1)}, s32[2]{0:T(128)}, u32[]{:S(2)}) copy-start(s32[2]{0:T(128)} %copy-done.13) | copy-start | bytes 28
  57.0 59.8 %all-to-all-start = ((bf16[128,2,1280]{2,1,0:T(2,128)(2,1)}), bf16[128,2,1280]{2,1,0:T(2,128)(2,1)S(1)}, u32[]{:S(2)}, u32[]{:S(2)}) async-start(bf16[128,2,1280]{2,1,0:T(2,128)(2,1)} %broadcast_select_fusion), calls=%async_computation | async-start | bytes 1310720 | tf_op jit(solution)/shard_map/all_to_all | solution.py:46
  190.0 17.3 %all-to-all-start.2 = ((bf16[8,9,16,108]{3,0,1,2:T(8,128)(2,1)}), bf16[8,9,16,108]{3,0,1,2:T(8,128)(2,1)S(1)}, u32[]{:S(2)}, u32[]{:S(2)}) async-start(bf16[8,9,16,108]{3,0,1,2:T(8,128)(2,1)} %copy.116), calls=%async_computation.2 | async-start | bytes 589824 | tf_op jit(solution)/shard_map/all_to_all | solution.py:140
  199.9 0.6 copy-start.17
  201.0 0.7 copy-start.20
  202.4 0.8 copy-start.3
  203.2 5.0 %copy-start.2 = (bf16[2,128,1280]{2,1,0:T(8,128)(2,1)}, bf16[2,128,1280]{2,1,0:T(8,128)(2,1)S(1)}, u32[]{:S(2)}) copy-start(bf16[2,128,1280]{2,1,0:T(8,128)(2,1)S(1)} %scatter_fusion.1) | copy-start | bytes 1966084
Sparse Core Ops, SparseCore 0:
  10.7 67.7 all-gather.2

commit v12 on v9

--- a/solution.py
+++ b/solution.py
@@ -128,7 +128,7 @@
     key_cache = jnp.zeros_like(key_pages).at[placement].set(key_pages)
     value_cache = jnp.zeros_like(value_pages).at[placement].set(value_pages)
     regrouped = deal_rows(layer_rows, owner_start, owner_len, device, owners, LIVE)
-    regrouped, weights = lax.optimization_barrier((regrouped, weights))
+
     outer = lax.axis_size("ra")
     inner = lax.axis_size("rb")
     piece = lax.all_gather(regrouped, "ra", axis=0, tiled=True)

time: 209 us -> 209 us (level)
  no operation moved by 1% of the time
where the time goes in v12:
time: 209 us
  waiting for transfers between devices  58.6 us (28%)
  blocking collectives  44 us (21%)
  starting transfers between devices  37 us (18%)
  local copies, waits for them, and re-layouts  31.3 us (15%)
  between operations  14.6 us (7%)
  matrix products  13.6 us (7%)
  other arithmetic  9.41 us (5%)
    all_to_all x1, waiting for transfers between devices, deal_rows(): lax.all_to_all(picked, ('ra', 'rb'), split_axis=0, concat_axis=0, tiled=T...  35.8 us
    all_gather x1, blocking collectives, per_device(): piece = lax.all_gather(regrouped, 'ra', axis=0, tiled=True)  28.7 us
    all_to_all x1, starting transfers between devices, deal_rows(): lax.all_to_all(picked, ('ra', 'rb'), split_axis=0, concat_axis=0, tiled=T...  23.7 us
    all_to_all x1, waiting for transfers between devices, per_device(): lax.all_to_all(stacked.astype(jnp.bfloat16), 'wt', split_axis=0, concat_a...  17.6 us
    unnamed x44, local copies, waits for them, and re-layouts  9.8 us
    all_to_all x1, starting transfers between devices, per_device(): gated = lax.all_to_all(gated, 'rb', split_axis=2, concat_axis=2, tiled=True)  9.66 us
    psum x1, blocking collectives, per_device(): lax.psum((jnp.sum(query_f * query_f, axis=1), jnp.sum(key_f * key_f, axis...  9.31 us
    dot_general x1, matrix products, per_device(): jnp.einsum('wrtk,skn->wrtsn', piece, weights, preferred_element_type=jnp....  8.71 us
  transfers between devices with their start and end apart: 4, of which 3 were waited for; matrix products, arithmetic and copies ran while one was open for 17% of the time, Pallas kernels for 0%

profile of v12, /device:TPU:1, one launch (start us, length us, event | category | flops | bytes accessed | tf_op | source)
XLA Modules:
  0.0 208.5 jit_solution(15688153868581470836)
XLA Ops:
  7.2 1.2 pad_maximum_fusion
  8.4 1.2 copy.108
  10.6 9.3 %all-reduce = (f32[256]{0:T(256)S(1)}, f32[256]{0:T(256)S(1)}) all-reduce(f32[256]{0:T(256)S(1)} %fusion.10, f32[256]{0:T(256)S(1)} %fusion.8), channel_id=1, replica_groups=mesh['ra'=8,'rb'=16,'wt'=4] {'wt'}, use_global_device_ids=true, to_apply=%region_5.6 | all-reduce | flops 512 | bytes 4096 | tf_op jit(solution)/shard_map/psum | solution.py:88
  20.1 1.0 fusion.44
  21.5 1.5 copy.132
  23.3 0.9 fusion.43
  24.2 1.5 copy.129
  25.7 2.6 %copy.130 = f32[256,10,64]{2,0,1:T(8,128)} copy(f32[256,10,64]{0,2,1:T(8,128)} %get-tuple-element.24) | data formatting | bytes 1310720
  28.4 1.1 copy.103
  29.5 1.0 scatter_custom_fusion
  30.5 1.2 gather_fusion.1
  35.7 2.7 %fusion.46 = (f32[10,256]{1,0:T(8,128)S(1)}, f32[10,256,256]{1,2,0:T(8,128)}) fusion(pred[256,256]{0,1:T(8,128)(4,1)S(1)} %fusion.21, bf16[256,10,128]{2,0,1:T(8,128)(2,1)S(1)} %maximum_convert_fusion, bf16[256,10,64]{2,0,1:T(8,128)(2,1)S(1)} %get-tuple-element.21, bf16[256,10,64]{2,0,1:T(8,128)(2,1)S(1)} %get-tuple-element.20), kind=kOutput, calls=%fused_computation.94 | convolution fusion | flops 171704576 | bytes 4007936 | tf_op jit(solution)/shard_map/sub | solution.py:107
  38.4 2.2 %multiply_reduce_fusion = (f32[256]{0:T(256)S(1)}, f32[10,256,128]{1,2,0:T(8,128)S(1)}) fusion(bf16[256,10,128]{0,2,1:T(8,128)(2,1)S(1)} %bitcast.49, f32[10,256,256]{1,2,0:T(8,128)} %get-tuple-element.35, f32[10,256]{1,0:T(8,128)S(1)} %get-tuple-element.34), kind=kOutput, calls=%fused_computation.30 | convolution fusion | flops 170393344 | bytes 4598784 | tf_op jit(solution)/shard_map/hqk,khd->qhd/dot_general | solution.py:110
  41.5 1.2 gather_fusion
  44.2 6.0 %psum.23 = f32[256]{0:T(256)S(1)} all-reduce(f32[256]{0:T(256)S(1)} %get-tuple-element.36), channel_id=1, replica_groups=mesh['ra'=8,'rb'=16,'wt'=4] {'wt'}, use_global_device_ids=true, to_apply=%region_9.10 | all-reduce | flops 256 | bytes 2048 | tf_op jit(solution)/shard_map/psum | solution.py:115
  50.5 1.3 gather_fusion.2
  52.9 1.5 broadcast_select_fusion
  54.4 23.7 %all-to-all-start = ((bf16[128,2,1280]{2,1,0:T(2,128)(2,1)}), bf16[128,2,1280]{2,1,0:T(2,128)(2,1)S(1)}, u32[]{:S(2)}, u32[]{:S(2)}) async-start(bf16[128,2,1280]{2,1,0:T(2,128)(2,1)} %broadcast_select_fusion), calls=%async_computation | async-start | bytes 1310720 | tf_op jit(solution)/shard_map/all_to_all | solution.py:49
  78.7 35.8 %all-to-all-done = bf16[128,2,1280]{2,1,0:T(2,128)(2,1)S(1)} async-done(((bf16[128,2,1280]{2,1,0:T(2,128)(2,1)}), bf16[128,2,1280]{2,1,0:T(2,128)(2,1)S(1)}, u32[]{:S(2)}, u32[]{:S(2)}) %all-to-all-start) | async-done | bytes 655392 | tf_op jit(solution)/shard_map/all_to_all | solution.py:49
  114.8 1.6 scatter_custom_fusion.1
  116.4 28.7 %all-gather = bf16[8,36,1280]{2,1,0:T(8,128)(2,1)S(1)} all-gather(bf16[1,36,1280]{2,1,0:T(8,128)(2,1)S(1)} %bitcast.50), channel_id=1, replica_groups=mesh['ra'=8,'rb'=16,'wt'=4] {'ra'}, dimensions={0}, use_global_device_ids=true | all-gather | bytes 829440 | tf_op jit(solution)/shard_map/all_gather | solution.py:134
  145.2 8.7 %fusion.3 = bf16[4,8,9,2,1728]{4,2,3,1,0:T(8,128)(2,1)S(1)} fusion(bf16[2,1280,1728,1,1]{1,0,2,4,3:T(2,128)(2,1)} %bitcast.54, bf16[8,4,9,1280]{3,0,2,1:T(8,128)(2,1)S(1)} %bitcast.48), kind=kOutput, calls=%fused_computation.11 | convolution fusion | flops 2549035008 | bytes 11575296 | tf_op jit(solution)/shard_map/wrtk,skn->wrtsn/dot_general | solution.py:137
  153.9 2.6 %copy.110 = bf16[4,8,9,2,1728]{4,1,3,2,0:T(8,128)(2,1)} copy(bf16[4,8,9,2,1728]{4,2,3,1,0:T(8,128)(2,1)S(1)} %fusion.3) | data formatting | bytes 3981312 | tf_op jit(solution)/shard_map/convert_element_type | solution.py:138
  156.5 3.6 %all-to-all-start.1 = ((bf16[4,8,9,2,1728]{4,1,3,2,0:T(8,128)(2,1)}), bf16[4,8,9,2,1728]{4,1,3,2,0:T(8,128)(2,1)S(1)}, u32[]{:S(2)}, u32[]{:S(2)}) async-start(bf16[4,8,9,2,1728]{4,1,3,2,0:T(8,128)(2,1)} %copy.110), calls=%async_computation.1 | async-start | bytes 4128768 | tf_op jit(solution)/shard_map/all_to_all | solution.py:138
  160.1 1.6 copy.126
  161.7 1.2 reshape.498
  163.6 17.6 %all-to-all-done.1 = bf16[4,8,9,2,1728]{4,1,3,2,0:T(8,128)(2,1)S(1)} async-done(((bf16[4,8,9,2,1728]{4,1,3,2,0:T(8,128)(2,1)}), bf16[4,8,9,2,1728]{4,1,3,2,0:T(8,128)(2,1)S(1)}, u32[]{:S(2)}, u32[]{:S(2)}) %all-to-all-start.1) | async-done | bytes 1990688 | tf_op jit(solution)/shard_map/all_to_all | solution.py:138
  182.9 0.8 copy.114
  183.7 9.7 %all-to-all-start.2 = ((bf16[8,9,16,108]{3,0,1,2:T(8,128)(2,1)}), bf16[8,9,16,108]{3,0,1,2:T(8,128)(2,1)S(1)}, u32[]{:S(2)}, u32[]{:S(2)}) async-start(bf16[8,9,16,108]{3,0,1,2:T(8,128)(2,1)} %copy.114), calls=%async_computation.2 | async-start | bytes 589824 | tf_op jit(solution)/shard_map/all_to_all | solution.py:143
  194.7 0.7 scatter_fusion.1
  195.5 5.2 %all-to-all-done.2 = bf16[8,9,16,108]{3,0,1,2:T(8,128)(2,1)S(1)} async-done(((bf16[8,9,16,108]{3,0,1,2:T(8,128)(2,1)}), bf16[8,9,16,108]{3,0,1,2:T(8,128)(2,1)S(1)}, u32[]{:S(2)}, u32[]{:S(2)}) %all-to-all-start.2) | async-done | bytes 248864 | tf_op jit(solution)/shard_map/all_to_all | solution.py:143
  200.8 0.9 copy.118
  (96 shorter events, 14.2 us)
Async XLA Ops:
  7.2 138.0 %all-gather.3.cloned.1.call-start = ((), (), s32[]{:S(2)}) async-start(), calls=%async_computation.3 | async-start | bytes 9400320 | tf_op jit(solution)/shard_map/all_gather | solution.py:85
  7.2 2.4 %copy-start.9 = (bf16[256,1280]{1,0:T(8,128)(2,1)S(1)}, bf16[256,1280]{1,0:T(8,128)(2,1)}, u32[]{:S(2)}) copy-start(bf16[256,1280]{1,0:T(8,128)(2,1)} %param.14) | copy-start | bytes 1966084
  8.4 1.5 copy-start.10
  9.9 10.0 %copy-start.13 = (f32[1280]{0:T(1024)S(1)}, f32[1280]{0:T(1024)}, u32[]{:S(2)}) copy-start(f32[1280]{0:T(1024)} %param.17) | copy-start | bytes 15364
  21.5 1.5 copy-start.14
  25.7 2.6 %copy-start.3 = (bf16[256,1280]{1,0:T(8,128)(2,1)S(1)}, bf16[256,1280]{1,0:T(8,128)(2,1)}, u32[]{:S(2)}) copy-start(bf16[256,1280]{1,0:T(8,128)(2,1)} %param.15) | copy-start | bytes 1966084
  25.7 3.7 %copy-start.16 = (s32[128]{0:T(128)S(1)}, s32[128]{0:T(128)}, u32[]{:S(2)}) copy-start(s32[128]{0:T(128)} %param.22) | copy-start | bytes 1540
  25.7 4.7 %copy-start = (s32[128]{0:T(128)S(1)}, s32[128]{0:T(128)}, u32[]{:S(2)}) copy-start(s32[128]{0:T(128)} %param.21) | copy-start | bytes 1540
  33.5 1.3 copy-start.2
  33.9 1.5 copy-start.1
  34.2 1.4 copy-start.8
  35.7 2.8 %copy-start.11 = (bf16[256,1280]{0,1:T(8,128)(2,1)S(1)}, bf16[256,1280]{0,1:T(8,128)(2,1)}, u32[]{:S(2)}) copy-start(bf16[256,1280]{0,1:T(8,128)(2,1)} %copy.103) | copy-start | bytes 1966084
  40.6 9.6 %copy-start.12 = (bf16[256,1280]{1,0:T(8,128)(2,1)S(1)}, bf16[256,1280]{1,0:T(8,128)(2,1)}, u32[]{:S(2)}) copy-start(bf16[256,1280]{1,0:T(8,128)(2,1)} %param.12) | copy-start | bytes 1966084
  40.6 9.6 %copy-start.15 = (f32[1280]{0:T(1024)S(1)}, f32[1280]{0:T(1024)}, u32[]{:S(2)}) copy-start(f32[1280]{0:T(1024)} %param.18) | copy-start | bytes 15364
  54.4 60.1 %all-to-all-start = ((bf16[128,2,1280]{2,1,0:T(2,128)(2,1)}), bf16[128,2,1280]{2,1,0:T(2,128)(2,1)S(1)}, u32[]{:S(2)}, u32[]{:S(2)}) async-start(bf16[128,2,1280]{2,1,0:T(2,128)(2,1)} %broadcast_select_fusion), calls=%async_computation | async-start | bytes 1310720 | tf_op jit(solution)/shard_map/all_to_all | solution.py:49
  156.5 24.7 %all-to-all-start.1 = ((bf16[4,8,9,2,1728]{4,1,3,2,0:T(8,128)(2,1)}), bf16[4,8,9,2,1728]{4,1,3,2,0:T(8,128)(2,1)S(1)}, u32[]{:S(2)}, u32[]{:S(2)}) async-start(bf16[4,8,9,2,1728]{4,1,3,2,0:T(8,128)(2,1)} %copy.110), calls=%async_computation.1 | async-start | bytes 4128768 | tf_op jit(solution)/shard_map/all_to_all | solution.py:138
  160.1 3.5 %copy-start.17 = (s32[1,2]{1,0:T(1,128)S(1)}, s32[1,2]{1,0:T(1,128)}, u32[]{:S(2)}) copy-start(s32[1,2]{1,0:T(1,128)} %param.23) | copy-start | bytes 28
  182.7 10.6 %copy-start.5 = (bf16[2,128,1280]{2,1,0:T(8,128)(2,1)S(1)}, bf16[2,128,1280]{2,1,0:T(8,128)(2,1)}, u32[]{:S(2)}) copy-start(bf16[2,128,1280]{2,1,0:T(8,128)(2,1)} %reshape.498) | copy-start | bytes 1966084
  183.7 17.1 %all-to-all-start.2 = ((bf16[8,9,16,108]{3,0,1,2:T(8,128)(2,1)}), bf16[8,9,16,108]{3,0,1,2:T(8,128)(2,1)S(1)}, u32[]{:S(2)}, u32[]{:S(2)}) async-start(bf16[8,9,16,108]{3,0,1,2:T(8,128)(2,1)} %copy.114), calls=%async_computation.2 | async-start | bytes 589824 | tf_op jit(solution)/shard_map/all_to_all | solution.py:143
  193.5 1.1 copy-start.4
  194.6 0.9 copy-start.7
  195.5 6.2 %copy-start.6 = (bf16[2,128,1280]{2,1,0:T(8,128)(2,1)}, bf16[2,128,1280]{2,1,0:T(8,128)(2,1)S(1)}, u32[]{:S(2)}) copy-start(bf16[2,128,1280]{2,1,0:T(8,128)(2,1)S(1)} %scatter_fusion.1) | copy-start | bytes 1966084
Sparse Core Ops, SparseCore 0:
  10.1 67.7 all-gather.2

commit v13 on v9

--- a/solution.py
+++ b/solution.py
@@ -131,9 +131,8 @@
     regrouped, weights = lax.optimization_barrier((regrouped, weights))
     outer = lax.axis_size("ra")
     inner = lax.axis_size("rb")
-    piece = lax.all_gather(regrouped, "ra", axis=0, tiled=True)
     parts = lax.axis_size("wt")
-    piece = jnp.transpose(piece.reshape(outer, parts, LIVE // parts, feature_count), (1, 0, 2, 3))
+    piece = lax.all_gather(regrouped.reshape(parts, LIVE // parts, feature_count), "ra", axis=1)
     stacked = jnp.einsum("wrtk,skn->wrtsn", piece, weights, preferred_element_type=jnp.float32)
     stacked = lax.all_to_all(stacked.astype(jnp.bfloat16), "wt", split_axis=0, concat_axis=0, tiled=True)
     summed = jnp.sum(stacked.astype(jnp.float32), axis=0)

time: 209 us -> 215 us (1.029)
  blocking collectives: 44 us -> 50.5 us
    all_gather x1, blocking collectives: 28.7 us -> 35.2 us  [per_device(): lax.all_gather(regrouped.reshape(parts, LIVE // parts, feature_count), 'r...]
where the time goes in v13:
time: 215 us
  waiting for transfers between devices  59.5 us (28%)
  blocking collectives  50.5 us (23%)
  starting transfers between devices  35.7 us (17%)
  local copies, waits for them, and re-layouts  31.3 us (15%)
  between operations  14.6 us (7%)
  matrix products  13.7 us (6%)
  other arithmetic  9.41 us (4%)
    all_to_all x1, waiting for transfers between devices, deal_rows(): lax.all_to_all(picked, ('ra', 'rb'), split_axis=0, concat_axis=0, tiled=T...  35.8 us
    all_gather x1, blocking collectives, per_device(): lax.all_gather(regrouped.reshape(parts, LIVE // parts, feature_count), 'r...  35.2 us
    all_to_all x1, starting transfers between devices, deal_rows(): lax.all_to_all(picked, ('ra', 'rb'), split_axis=0, concat_axis=0, tiled=T...  23.7 us
    all_to_all x1, waiting for transfers between devices, per_device(): lax.all_to_all(stacked.astype(jnp.bfloat16), 'wt', split_axis=0, concat_a...  18.4 us
    unnamed x44, local copies, waits for them, and re-layouts  9.8 us
    psum x1, blocking collectives, per_device(): lax.psum((jnp.sum(query_f * query_f, axis=1), jnp.sum(key_f * key_f, axis...  9.31 us
    dot_general x1, matrix products, per_device(): jnp.einsum('wrtk,skn->wrtsn', piece, weights, preferred_element_type=jnp....  8.75 us
    all_to_all x1, starting transfers between devices, per_device(): gated = lax.all_to_all(gated, 'rb', split_axis=2, concat_axis=2, tiled=True)  8.38 us
  transfers between devices with their start and end apart: 4, of which 3 were waited for; matrix products, arithmetic and copies ran while one was open for 17% of the time, Pallas kernels for 0%

profile of v13, /device:TPU:1, one launch (start us, length us, event | category | flops | bytes accessed | tf_op | source)
XLA Modules:
  0.0 214.6 jit_solution(6104726391722311532)
XLA Ops:
  7.2 1.2 pad_maximum_fusion
  8.4 1.2 copy.89
  10.6 9.3 %all-reduce = (f32[256]{0:T(256)S(1)}, f32[256]{0:T(256)S(1)}) all-reduce(f32[256]{0:T(256)S(1)} %fusion.10, f32[256]{0:T(256)S(1)} %fusion.8), channel_id=1, replica_groups=mesh['ra'=8,'rb'=16,'wt'=4] {'wt'}, use_global_device_ids=true, to_apply=%region_5.6 | all-reduce | flops 512 | bytes 4096 | tf_op jit(solution)/shard_map/psum | solution.py:88
  20.1 1.0 fusion.43
  21.5 1.5 copy.114
  23.3 0.9 fusion.42
  24.2 1.5 copy.111
  25.7 2.6 %copy.112 = f32[256,10,64]{2,0,1:T(8,128)} copy(f32[256,10,64]{0,2,1:T(8,128)} %get-tuple-element.25) | data formatting | bytes 1310720
  28.4 1.1 copy.86
  29.5 1.0 scatter_custom_fusion
  30.5 1.2 gather_fusion.1
  35.7 2.7 %fusion.45 = (f32[10,256]{1,0:T(8,128)S(1)}, f32[10,256,256]{1,2,0:T(8,128)}) fusion(pred[256,256]{0,1:T(8,128)(4,1)S(1)} %fusion.20, bf16[256,10,128]{2,0,1:T(8,128)(2,1)S(1)} %maximum_convert_fusion, bf16[256,10,64]{2,0,1:T(8,128)(2,1)S(1)} %get-tuple-element.22, bf16[256,10,64]{2,0,1:T(8,128)(2,1)S(1)} %get-tuple-element.21), kind=kOutput, calls=%fused_computation.93 | convolution fusion | flops 171704576 | bytes 4007936 | tf_op jit(solution)/shard_map/sub | solution.py:107
  38.4 2.2 %multiply_reduce_fusion = (f32[256]{0:T(256)S(1)}, f32[10,256,128]{1,2,0:T(8,128)S(1)}) fusion(bf16[256,10,128]{0,2,1:T(8,128)(2,1)S(1)} %bitcast.45, f32[10,256,256]{1,2,0:T(8,128)} %get-tuple-element.36, f32[10,256]{1,0:T(8,128)S(1)} %get-tuple-element.35), kind=kOutput, calls=%fused_computation.29 | convolution fusion | flops 170393344 | bytes 4598784 | tf_op jit(solution)/shard_map/hqk,khd->qhd/dot_general | solution.py:110
  41.5 1.2 gather_fusion
  44.2 6.0 %psum.23 = f32[256]{0:T(256)S(1)} all-reduce(f32[256]{0:T(256)S(1)} %get-tuple-element.37), channel_id=1, replica_groups=mesh['ra'=8,'rb'=16,'wt'=4] {'wt'}, use_global_device_ids=true, to_apply=%region_9.10 | all-reduce | flops 256 | bytes 2048 | tf_op jit(solution)/shard_map/psum | solution.py:115
  50.5 1.3 gather_fusion.2
  52.9 1.5 broadcast_select_fusion
  54.4 23.7 %all-to-all-start = ((bf16[128,2,1280]{2,1,0:T(2,128)(2,1)}), bf16[128,2,1280]{2,1,0:T(2,128)(2,1)S(1)}, u32[]{:S(2)}, u32[]{:S(2)}) async-start(bf16[128,2,1280]{2,1,0:T(2,128)(2,1)} %broadcast_select_fusion), calls=%async_computation | async-start | bytes 1310720 | tf_op jit(solution)/shard_map/all_to_all | solution.py:49
  78.7 35.8 %all-to-all-done = bf16[128,2,1280]{2,1,0:T(2,128)(2,1)S(1)} async-done(((bf16[128,2,1280]{2,1,0:T(2,128)(2,1)}), bf16[128,2,1280]{2,1,0:T(2,128)(2,1)S(1)}, u32[]{:S(2)}, u32[]{:S(2)}) %all-to-all-start) | async-done | bytes 655392 | tf_op jit(solution)/shard_map/all_to_all | solution.py:49
  114.8 1.6 scatter_custom_fusion.1
  116.4 35.2 %all_gather.7 = bf16[4,8,9,1280]{3,2,1,0:T(8,128)(2,1)S(1)} all-gather(bf16[4,1,9,1280]{3,2,1,0:T(8,128)(2,1)S(1)} %bitcast.46), channel_id=1, replica_groups=mesh['ra'=8,'rb'=16,'wt'=4] {'ra'}, dimensions={1}, use_global_device_ids=true | all-gather | bytes 829440 | tf_op jit(solution)/shard_map/all_gather | solution.py:135
  151.6 8.7 %fusion.3 = bf16[4,8,9,2,1728]{4,2,3,1,0:T(8,128)(2,1)S(1)} fusion(bf16[2,1280,1728,1,1]{1,0,2,4,3:T(2,128)(2,1)} %bitcast.50, bf16[4,8,9,1280]{3,2,1,0:T(8,128)(2,1)S(1)} %all_gather.7), kind=kOutput, calls=%fused_computation.11 | convolution fusion | flops 2549035008 | bytes 11575296 | tf_op jit(solution)/shard_map/wrtk,skn->wrtsn/dot_general | solution.py:136
  160.4 2.6 %copy.92 = bf16[4,8,9,2,1728]{4,1,3,2,0:T(8,128)(2,1)} copy(bf16[4,8,9,2,1728]{4,2,3,1,0:T(8,128)(2,1)S(1)} %fusion.3) | data formatting | bytes 3981312 | tf_op jit(solution)/shard_map/convert_element_type | solution.py:137
  163.0 3.6 %all-to-all-start.1 = ((bf16[4,8,9,2,1728]{4,1,3,2,0:T(8,128)(2,1)}), bf16[4,8,9,2,1728]{4,1,3,2,0:T(8,128)(2,1)S(1)}, u32[]{:S(2)}, u32[]{:S(2)}) async-start(bf16[4,8,9,2,1728]{4,1,3,2,0:T(8,128)(2,1)} %copy.92), calls=%async_computation.1 | async-start | bytes 4128768 | tf_op jit(solution)/shard_map/all_to_all | solution.py:137
  166.6 1.6 copy.108
  168.2 1.2 reshape.491
  170.1 18.4 %all-to-all-done.1 = bf16[4,8,9,2,1728]{4,1,3,2,0:T(8,128)(2,1)S(1)} async-done(((bf16[4,8,9,2,1728]{4,1,3,2,0:T(8,128)(2,1)}), bf16[4,8,9,2,1728]{4,1,3,2,0:T(8,128)(2,1)S(1)}, u32[]{:S(2)}, u32[]{:S(2)}) %all-to-all-start.1) | async-done | bytes 1990688 | tf_op jit(solution)/shard_map/all_to_all | solution.py:137
  190.2 0.8 copy.96
  191.0 8.4 %all-to-all-start.2 = ((bf16[8,9,16,108]{3,0,1,2:T(8,128)(2,1)}), bf16[8,9,16,108]{3,0,1,2:T(8,128)(2,1)S(1)}, u32[]{:S(2)}, u32[]{:S(2)}) async-start(bf16[8,9,16,108]{3,0,1,2:T(8,128)(2,1)} %copy.96), calls=%async_computation.2 | async-start | bytes 589824 | tf_op jit(solution)/shard_map/all_to_all | solution.py:142
  199.6 0.7 scatter_fusion
  201.5 5.3 %all-to-all-done.2 = bf16[8,9,16,108]{3,0,1,2:T(8,128)(2,1)S(1)} async-done(((bf16[8,9,16,108]{3,0,1,2:T(8,128)(2,1)}), bf16[8,9,16,108]{3,0,1,2:T(8,128)(2,1)S(1)}, u32[]{:S(2)}, u32[]{:S(2)}) %all-to-all-start.2) | async-done | bytes 248864 | tf_op jit(solution)/shard_map/all_to_all | solution.py:142
  206.9 0.9 copy.100
  (96 shorter events, 14.1 us)
Async XLA Ops:
  7.2 109.2 %all-gather.2.cloned.1.call-start = ((), (), s32[]{:S(2)}) async-start(), calls=%async_computation.3 | async-start | bytes 9400320 | tf_op jit(solution)/shard_map/all_gather | solution.py:85
  7.2 2.4 %copy-start.9 = (bf16[256,1280]{1,0:T(8,128)(2,1)S(1)}, bf16[256,1280]{1,0:T(8,128)(2,1)}, u32[]{:S(2)}) copy-start(bf16[256,1280]{1,0:T(8,128)(2,1)} %param.14) | copy-start | bytes 1966084
  8.4 1.5 copy-start.10
  9.9 10.0 %copy-start.13 = (f32[1280]{0:T(1024)S(1)}, f32[1280]{0:T(1024)}, u32[]{:S(2)}) copy-start(f32[1280]{0:T(1024)} %param.17) | copy-start | bytes 15364
  21.5 1.5 copy-start.14
  25.7 2.6 %copy-start.3 = (bf16[256,1280]{1,0:T(8,128)(2,1)S(1)}, bf16[256,1280]{1,0:T(8,128)(2,1)}, u32[]{:S(2)}) copy-start(bf16[256,1280]{1,0:T(8,128)(2,1)} %param.15) | copy-start | bytes 1966084
  25.7 3.7 %copy-start.16 = (s32[128]{0:T(128)S(1)}, s32[128]{0:T(128)}, u32[]{:S(2)}) copy-start(s32[128]{0:T(128)} %param.22) | copy-start | bytes 1540
  25.7 4.7 %copy-start = (s32[128]{0:T(128)S(1)}, s32[128]{0:T(128)}, u32[]{:S(2)}) copy-start(s32[128]{0:T(128)} %param.21) | copy-start | bytes 1540
  33.5 1.3 copy-start.2
  33.9 1.5 copy-start.1
  34.2 1.4 copy-start.8
  35.7 2.8 %copy-start.11 = (bf16[256,1280]{0,1:T(8,128)(2,1)S(1)}, bf16[256,1280]{0,1:T(8,128)(2,1)}, u32[]{:S(2)}) copy-start(bf16[256,1280]{0,1:T(8,128)(2,1)} %copy.86) | copy-start | bytes 1966084
  40.6 9.6 %copy-start.12 = (bf16[256,1280]{1,0:T(8,128)(2,1)S(1)}, bf16[256,1280]{1,0:T(8,128)(2,1)}, u32[]{:S(2)}) copy-start(bf16[256,1280]{1,0:T(8,128)(2,1)} %param.12) | copy-start | bytes 1966084
  40.6 9.6 %copy-start.15 = (f32[1280]{0:T(1024)S(1)}, f32[1280]{0:T(1024)}, u32[]{:S(2)}) copy-start(f32[1280]{0:T(1024)} %param.18) | copy-start | bytes 15364
  54.4 60.1 %all-to-all-start = ((bf16[128,2,1280]{2,1,0:T(2,128)(2,1)}), bf16[128,2,1280]{2,1,0:T(2,128)(2,1)S(1)}, u32[]{:S(2)}, u32[]{:S(2)}) async-start(bf16[128,2,1280]{2,1,0:T(2,128)(2,1)} %broadcast_select_fusion), calls=%async_computation | async-start | bytes 1310720 | tf_op jit(solution)/shard_map/all_to_all | solution.py:49
  163.0 25.5 %all-to-all-start.1 = ((bf16[4,8,9,2,1728]{4,1,3,2,0:T(8,128)(2,1)}), bf16[4,8,9,2,1728]{4,1,3,2,0:T(8,128)(2,1)S(1)}, u32[]{:S(2)}, u32[]{:S(2)}) async-start(bf16[4,8,9,2,1728]{4,1,3,2,0:T(8,128)(2,1)} %copy.92), calls=%async_computation.1 | async-start | bytes 4128768 | tf_op jit(solution)/shard_map/all_to_all | solution.py:137
  166.6 3.5 %copy-start.17 = (s32[1,2]{1,0:T(1,128)S(1)}, s32[1,2]{1,0:T(1,128)}, u32[]{:S(2)}) copy-start(s32[1,2]{1,0:T(1,128)} %param.23) | copy-start | bytes 28
  190.0 9.3 %copy-start.5 = (bf16[2,128,1280]{2,1,0:T(8,128)(2,1)S(1)}, bf16[2,128,1280]{2,1,0:T(8,128)(2,1)}, u32[]{:S(2)}) copy-start(bf16[2,128,1280]{2,1,0:T(8,128)(2,1)} %reshape.491) | copy-start | bytes 1966084
  191.0 15.8 %all-to-all-start.2 = ((bf16[8,9,16,108]{3,0,1,2:T(8,128)(2,1)}), bf16[8,9,16,108]{3,0,1,2:T(8,128)(2,1)S(1)}, u32[]{:S(2)}, u32[]{:S(2)}) async-start(bf16[8,9,16,108]{3,0,1,2:T(8,128)(2,1)} %copy.96), calls=%async_computation.2 | async-start | bytes 589824 | tf_op jit(solution)/shard_map/all_to_all | solution.py:142
  199.5 1.1 copy-start.4
  200.6 0.9 copy-start.7
  201.5 6.3 %copy-start.6 = (bf16[2,128,1280]{2,1,0:T(8,128)(2,1)}, bf16[2,128,1280]{2,1,0:T(8,128)(2,1)S(1)}, u32[]{:S(2)}) copy-start(bf16[2,128,1280]{2,1,0:T(8,128)(2,1)S(1)} %scatter_fusion.1) | copy-start | bytes 1966084
Sparse Core Ops, SparseCore 0:
  10.1 67.7 all-gather.1
